TPU v7x, 32 devices: a whole 2x2x4 slice. The times are simulated.
32 devices in a mesh: series: 4 (over y, x), tm: 8 (over z, core).
Axes of the slice: x: 2, y: 2, z: 4, core: 2. Of those that a mesh axis runs over, the one named last changes fastest.
Arguments:
- panel: bfloat16 [8192, 2048], P('series', 'tm'), may hold values from -6 to 6
- observed: int32 [8192, 256], P('series', 'tm'), may hold values from 0 to 255
- series_factors: float32 [8192, 128], P(('series', 'tm')), may hold values from -2 to 2
- time_factors: float32 [128, 2048], P(None, 'tm'), may hold values from -6 to 6
- ar_weights: float32 [25, 128], replicated, may hold values from -0.06 to 0.06
- lags: int32 [25], replicated, may hold values from 1 to 168, as said below
Outputs:
- factors_next: float32 [8192, 128], P(('series', 'tm'))
- times_next: float32 [128, 2048], P(None, 'tm')
- misfit_final: bfloat16 [8192, 2048], P('series', 'tm')
Inputs may be any that keep to these rules, and one draw needn't show every extreme that they name: lags rise strictly; the first is 1 and the last is 168.
All inputs are finite; a program needn't handle non-finite values.
Results may differ from a plain program's by a relative error of at most 0.0047.
Values may be sent and summed in bfloat16 or wider, within the bound.
No kernel may reach another device: no remote copies, remote signals or barrier semaphores. Data moves between devices by JAX's collectives and lax.ppermute only.
A program may use at most 64 MiB of HBM per device.

v0:
```python
import jax
import jax.numpy as jnp
from jax import lax
from jax.experimental import pallas as pl
from jax.experimental.pallas import tpu as pltpu
from jax.sharding import PartitionSpec as P

MAXLAG = 168
ITERS = 2


def shifted(block, axis, distance):
    devices = range(lax.axis_size(axis))
    route = [(i - distance, i) for i in devices if i - distance in devices]
    return lax.ppermute(block, axis, route)


def exchange(block, axis, bit):
    devices = lax.axis_size(axis)
    return lax.ppermute(block, axis, [(i, i ^ bit) for i in range(devices)])


def butterfly_sum(block, axis):
    devices = lax.axis_size(axis)
    bit = 1
    while bit < devices:
        block = block + exchange(block, axis, bit)
        bit *= 2
    return block


def halving_sum(block, axis):
    devices = lax.axis_size(axis)
    position = lax.axis_index(axis)
    levels = devices.bit_length() - 1
    rows = block.shape[0] // devices
    block = block.reshape((2,) * levels + (rows,) + block.shape[1:])
    for level in range(levels):
        bit = 1 << level
        upper = (position & bit) != 0
        at = levels - 1 - level
        low = lax.index_in_dim(block, 0, at, keepdims=False)
        high = lax.index_in_dim(block, 1, at, keepdims=False)
        keep = jnp.where(upper, high, low)
        send = jnp.where(upper, low, high)
        block = keep + exchange(send, axis, bit)
    return block


def doubling_gather(block, axis):
    devices = lax.axis_size(axis)
    position = lax.axis_index(axis)
    levels = devices.bit_length() - 1
    for step in range(levels):
        bit = 1 << (levels - 1 - step)
        upper = (position & bit) != 0
        other = exchange(block, axis, bit)
        low = jnp.where(upper, other, block)
        high = jnp.where(upper, block, other)
        block = jnp.stack([low, high], axis=step)
    return block.reshape((-1,) + block.shape[levels + 1 :])


def unpack(packed_words):
    shift_amounts = jnp.arange(8, dtype=jnp.int32)
    bit_values = jnp.right_shift(packed_words[:, :, None], shift_amounts) & 1
    return bit_values.reshape(packed_words.shape[0], packed_words.shape[1] * 8).astype(jnp.float32)


def lag_kernel(starts_ref, weights_ref, extended_ref, out_ref):
    width = out_ref.shape[0]
    running = jnp.zeros(out_ref.shape, jnp.float32)
    for k in range(weights_ref.shape[0]):
        row_block = extended_ref[pl.ds(starts_ref[k], width), :]
        running = running + weights_ref[pl.ds(k, 1), :] * row_block
    out_ref[...] = running


def lagged_sum(extended, weights, starts, width):
    rank = extended.shape[1]
    return pl.pallas_call(
        lag_kernel,
        out_shape=jax.ShapeDtypeStruct((width, rank), jnp.float32),
        in_specs=[
            pl.BlockSpec(memory_space=pltpu.SMEM),
            pl.BlockSpec(memory_space=pltpu.VMEM),
            pl.BlockSpec(memory_space=pltpu.VMEM),
        ],
        out_specs=pl.BlockSpec(memory_space=pltpu.VMEM),
        cost_estimate=pl.CostEstimate(
            flops=2 * weights.shape[0] * width * rank,
            transcendentals=0,
            bytes_accessed=4 * (extended.size + weights.size + width * rank),
        ),
    )(starts.astype(jnp.int32), weights, extended)


def fetch_rows(factors):
    return doubling_gather(factors.astype(jnp.bfloat16), "tm")


def local(panel, observed, series_factors, time_factors, ar_weights, lags):
    hours = panel.shape[1]
    total_hours = hours * lax.axis_size("tm")
    total_series = panel.shape[0] * lax.axis_size("series")
    mask_values = unpack(observed)
    position = lax.axis_index("tm")
    hour_index = position * hours + jnp.arange(hours, dtype=jnp.int32)
    active_rows = (hour_index >= MAXLAG)[:, None]

    def compute_misfit(rows_low, times_low):
        predicted = jnp.dot(rows_low, times_low, preferred_element_type=jnp.float32)
        return (mask_values * (predicted - panel.astype(jnp.float32))).astype(jnp.bfloat16)

    times = time_factors
    factors = series_factors
    for iteration in range(ITERS):
        rows_low = fetch_rows(factors)
        times_low = times.astype(jnp.bfloat16)
        misfit = compute_misfit(rows_low, times_low)
        grad_rows = halving_sum(
            lax.dot_general(
                misfit, times_low, (((1,), (1,)), ((), ())), preferred_element_type=jnp.float32
            ),
            "tm",
        )
        partial_value = lax.dot_general(
            rows_low, misfit, (((0,), (0,)), ((), ())), preferred_element_type=jnp.float32
        )
        grad_times = butterfly_sum(partial_value, "series")
        times_t = times.T
        tail_rows = shifted(times_t[hours - MAXLAG :], "tm", 1)
        errors = times_t - lagged_sum(
            jnp.concatenate([tail_rows, times_t], 0), ar_weights, MAXLAG - lags, hours
        )
        errors = jnp.where(active_rows, errors, 0.0)
        head_rows = shifted(errors[:MAXLAG], "tm", -1)
        ar_grad = (errors - lagged_sum(
            jnp.concatenate([errors, head_rows], 0), ar_weights, lags, hours
        )).T
        times_new = times - 24.0 / total_series * grad_times - 0.25 * ar_grad
        factors = factors - 2.0 / total_hours * grad_rows
        times = times_new
    final_rows = fetch_rows(factors)
    misfit_final = compute_misfit(final_rows, times.astype(jnp.bfloat16))
    return (factors, times, misfit_final)


def solution(mesh):
    in_specs = (
        P("series", "tm"),
        P("series", "tm"),
        P(("series", "tm"), None),
        P(None, "tm"),
        P(),
        P(),
    )
    out_specs = (P(("series", "tm"), None), P(None, "tm"), P("series", "tm"))
    return jax.shard_map(local, mesh=mesh, in_specs=in_specs, out_specs=out_specs, check_vma=False)
```

profile of v0, /device:TPU:0, one launch (start us, length us, event | category | flops | bytes accessed | tf_op | source)
XLA Modules:
  0.0 110.0 jit_solution(13356720080985014840)
XLA Ops:
  1.6 4.0 %collective-permute-start = (bf16[256,128]{1,0:T(8,128)(2,1)S(1)}, bf16[256,128]{1,0:T(8,128)(2,1)S(1)}, u32[]{:S(2)}, u32[]{:S(2)}) collective-permute-start(bf16[256,128]{1,0:T(8,128)(2,1)S(1)} %convert_element_type.36), channel_id=1, source_target_pairs={{0,4},{1,5},{2,6},{3,7},{4,0},{5,1},{6,2},{7,3},{8,12},{9,13},{10,... | collective-permute-start | bytes 196616 | tf_op jit(solution)/shard_map/ppermute | solution.py:20
  5.6 3.6 %collective-permute-done = bf16[256,128]{1,0:T(8,128)(2,1)S(1)} collective-permute-done((bf16[256,128]{1,0:T(8,128)(2,1)S(1)}, bf16[256,128]{1,0:T(8,128)(2,1)S(1)}, u32[]{:S(2)}, u32[]{:S(2)}) %collective-permute-start) | collective-permute-done | bytes 65568 | tf_op jit(solution)/shard_map/ppermute | solution.py:20
  11.0 4.3 %collective-permute-done.1 = bf16[2,256,128]{2,1,0:T(8,128)(2,1)S(1)} collective-permute-done((bf16[2,256,128]{2,1,0:T(8,128)(2,1)S(1)}, bf16[2,256,128]{2,1,0:T(8,128)(2,1)S(1)}, u32[]{:S(2)}, u32[]{:S(2)}) %collective-permute-start.1) | collective-permute-done | bytes 131104 | tf_op jit(solution)/shard_map/ppermute | solution.py:20
  15.4 1.6 %broadcast_bitcast_fusion = s32[2048,256]{0,1:T(8,128)} fusion(s32[2048,32]{0,1:T(8,128)S(1)} %copy-done), kind=kLoop, calls=%fused_computation.10 | loop fusion | bytes 2359296 | tf_op jit(solution)/shard_map/shift_right_arithmetic | solution.py:66
  17.0 1.9 %copy.21 = s32[2048,256]{1,0:T(8,128)S(1)} copy(s32[2048,256]{0,1:T(8,128)} %broadcast_bitcast_fusion) | data formatting | bytes 4194304 | tf_op jit(solution)/shard_map/shift_right_arithmetic | solution.py:66
  22.1 1.5 %collective-permute-done.3 = f32[2,2,256,128]{3,2,0,1:T(8,128)S(1)} collective-permute-done((f32[2,2,256,128]{3,2,0,1:T(8,128)S(1)}, f32[2,2,256,128]{3,2,0,1:T(8,128)S(1)}, u32[]{:S(2)}, u32[]{:S(2)}) %collective-permute-start.3) | collective-permute-done | bytes 524320 | tf_op jit(solution)/shard_map/ppermute | solution.py:20
  27.5 2.6 %collective-permute-start.11 = (f32[168,128]{1,0:T(8,128)}, f32[168,128]{1,0:T(8,128)}, u32[]{:S(2)}, u32[]{:S(2)}) collective-permute-start(f32[168,128]{1,0:T(8,128)} %slice.70), channel_id=1, source_target_pairs={{0,1},{1,2},{2,3},{3,4},{4,5},{5,6},{6,7},{8,9},{9,10},{10,11},{11... | collective-permute-start | bytes 258056 | tf_op jit(solution)/shard_map/ppermute | solution.py:15
  30.7 3.5 %collective-permute-done.4 = f32[2,256,128]{2,1,0:T(8,128)} collective-permute-done((f32[2,256,128]{2,1,0:T(8,128)}, f32[2,256,128]{2,1,0:T(8,128)}, u32[]{:S(2)}, u32[]{:S(2)}) %collective-permute-start.4) | collective-permute-done | bytes 262176 | tf_op jit(solution)/shard_map/ppermute | solution.py:20
  36.7 2.3 %collective-permute-start.5 = (f32[256,128]{1,0:T(8,128)}, f32[256,128]{1,0:T(8,128)}, u32[]{:S(2)}, u32[]{:S(2)}) collective-permute-start(f32[256,128]{1,0:T(8,128)} %select_bitcast_fusion.15), channel_id=1, source_target_pairs={{0,4},{1,5},{2,6},{3,7},{4,0},{5,1},{6,2},{7,3},{8,12},{9,13},{10,... | collective-permute-start | bytes 393224 | tf_op jit(solution)/shard_map/ppermute | solution.py:20
  39.0 1.6 %pad_maximum_fusion.6.extended_ref = f32[424,128]{1,0:T(8,128)} fusion(f32[256,128]{1,0:T(8,128)S(1)} %bitcast.107, f32[168,128]{1,0:T(8,128)} %collective-permute-done.11), kind=kLoop, calls=%fused_computation.31 | loop fusion | flops 54272 | bytes 434176 | tf_op jit(solution)/shard_map/concatenate | solution.py:134
  40.6 1.9 %shard_map.85 = f32[256,128]{1,0:T(8,128)} custom-call(s32[25]{0:T(128)} %broadcast_subtract_fusion.starts_ref, f32[25,128]{1,0:T(8,128)} %weights_ref.7, f32[424,128]{1,0:T(8,128)} %pad_maximum_fusion.6.extended_ref), custom_call_target="tpu_custom_call" | custom-call | flops 1638400 | bytes 360960 | tf_op jit(solution)/shard_map/pallas_call | solution.py:81
  42.6 3.1 %collective-permute-done.5 = f32[256,128]{1,0:T(8,128)} collective-permute-done((f32[256,128]{1,0:T(8,128)}, f32[256,128]{1,0:T(8,128)}, u32[]{:S(2)}, u32[]{:S(2)}) %collective-permute-start.5) | collective-permute-done | bytes 131104 | tf_op jit(solution)/shard_map/ppermute | solution.py:20
  45.7 1.8 %fusion.19 = (bf16[256,128]{1,0:T(8,128)(2,1)S(1)}, f32[256,128]{1,0:T(8,128)}) fusion(f32[256,128]{1,0:T(8,128)} %param.8, f32[256,128]{1,0:T(8,128)} %collective-permute-done.5, f32[2,256,128]{2,1,0:T(8,128)} %copy-done.8, pred[]{:T(512)S(6)} %ne.6), kind=kLoop, calls=%fused_computation.72 | loop fusion | flops 163840 | bytes 720897 | tf_op jit(solution)/shard_map/convert_element_type | solution.py:99
  47.5 1.6 %fusion.23 = f32[128,256]{0,1:T(8,128)S(1)} fusion(bf16[2048,128]{1,0:T(8,128)(2,1)} %bitcast.101, bf16[2048,256]{1,0:T(8,128)(2,1)S(1)} %fusion.3), kind=kOutput, calls=%fused_computation.75 | convolution fusion | flops 134217728 | bytes 1703936 | tf_op jit(solution)/shard_map/dot_general | solution.py:127
  49.0 1.8 %collective-permute-start.9 = (f32[128,256]{0,1:T(8,128)S(1)}, f32[128,256]{0,1:T(8,128)S(1)}, u32[]{:S(2)}, u32[]{:S(2)}) collective-permute-start(f32[128,256]{0,1:T(8,128)S(1)} %fusion.23), channel_id=1, source_target_pairs={{0,8},{8,0},{16,24},{24,16},{1,9},{9,1},{17,25},{25,17},{2,10},{10... | collective-permute-start | bytes 393224 | tf_op jit(solution)/shard_map/ppermute | solution.py:20
  50.8 2.9 %collective-permute-done.6 = bf16[256,128]{1,0:T(8,128)(2,1)S(1)} collective-permute-done((bf16[256,128]{1,0:T(8,128)(2,1)S(1)}, bf16[256,128]{1,0:T(8,128)(2,1)S(1)}, u32[]{:S(2)}, u32[]{:S(2)}) %collective-permute-start.6) | collective-permute-done | bytes 65568 | tf_op jit(solution)/shard_map/ppermute | solution.py:20
  55.9 1.6 %collective-permute-start.10 = (f32[128,256]{0,1:T(8,128)S(1)}, f32[128,256]{0,1:T(8,128)}, u32[]{:S(2)}, u32[]{:S(2)}) collective-permute-start(f32[128,256]{0,1:T(8,128)S(1)} %add.43), channel_id=1, source_target_pairs={{0,16},{8,24},{16,0},{24,8},{1,17},{9,25},{17,1},{25,9},{2,18},{10... | collective-permute-start | bytes 393224 | tf_op jit(solution)/shard_map/ppermute | solution.py:20
  59.6 2.0 %shard_map.86 = f32[256,128]{1,0:T(8,128)} custom-call(s32[25]{0:T(128)} %starts_ref.3, f32[25,128]{1,0:T(8,128)} %weights_ref.7, f32[424,128]{1,0:T(8,128)} %pad_maximum_fusion.7.extended_ref), custom_call_target="tpu_custom_call" | custom-call | flops 1638400 | bytes 360960 | tf_op jit(solution)/shard_map/pallas_call | solution.py:81
  66.8 1.5 %collective-permute-done.13 = f32[2,2,256,128]{3,2,0,1:T(8,128)S(1)} collective-permute-done((f32[2,2,256,128]{3,2,0,1:T(8,128)S(1)}, f32[2,2,256,128]{3,2,0,1:T(8,128)S(1)}, u32[]{:S(2)}, u32[]{:S(2)}) %collective-permute-start.13) | collective-permute-done | bytes 524320 | tf_op jit(solution)/shard_map/ppermute | solution.py:20
  69.6 1.8 %collective-permute-start.18 = (f32[168,128]{1,0:T(8,128)S(1)}, f32[168,128]{1,0:T(8,128)S(1)}, u32[]{:S(2)}, u32[]{:S(2)}) collective-permute-start(f32[168,128]{1,0:T(8,128)S(1)} %slice.78), channel_id=1, source_target_pairs={{0,1},{1,2},{2,3},{3,4},{4,5},{5,6},{6,7},{8,9},{9,10},{10,11},{11... | collective-permute-start | bytes 258056 | tf_op jit(solution)/shard_map/ppermute | solution.py:15
  71.4 5.7 %collective-permute-done.14 = f32[2,256,128]{2,1,0:T(8,128)S(1)} collective-permute-done((f32[2,256,128]{2,1,0:T(8,128)S(1)}, f32[2,256,128]{2,1,0:T(8,128)S(1)}, u32[]{:S(2)}, u32[]{:S(2)}) %collective-permute-start.14) | collective-permute-done | bytes 262176 | tf_op jit(solution)/shard_map/ppermute | solution.py:20
  78.5 1.5 %collective-permute-start.15 = (f32[256,128]{1,0:T(8,128)}, f32[256,128]{1,0:T(8,128)}, u32[]{:S(2)}, u32[]{:S(2)}) collective-permute-start(f32[256,128]{1,0:T(8,128)} %select_bitcast_fusion.12), channel_id=1, source_target_pairs={{0,4},{1,5},{2,6},{3,7},{4,0},{5,1},{6,2},{7,3},{8,12},{9,13},{10,... | collective-permute-start | bytes 393224 | tf_op jit(solution)/shard_map/ppermute | solution.py:20
  80.8 1.9 %shard_map.87 = f32[256,128]{1,0:T(8,128)} custom-call(s32[25]{0:T(128)} %broadcast_subtract_fusion.starts_ref, f32[25,128]{1,0:T(8,128)} %weights_ref.7, f32[424,128]{1,0:T(8,128)} %pad_maximum_fusion.8.extended_ref), custom_call_target="tpu_custom_call" | custom-call | flops 1638400 | bytes 360960 | tf_op jit(solution)/shard_map/pallas_call | solution.py:81
  82.7 4.8 %collective-permute-done.15 = f32[256,128]{1,0:T(8,128)} collective-permute-done((f32[256,128]{1,0:T(8,128)}, f32[256,128]{1,0:T(8,128)}, u32[]{:S(2)}, u32[]{:S(2)}) %collective-permute-start.15) | collective-permute-done | bytes 131104 | tf_op jit(solution)/shard_map/ppermute | solution.py:20
  87.5 1.8 %fusion.17 = (bf16[256,128]{1,0:T(8,128)(2,1)S(1)}, f32[256,128]{1,0:T(8,128)}) fusion(f32[256,128]{1,0:T(8,128)} %get-tuple-element.12, f32[256,128]{1,0:T(8,128)} %collective-permute-done.15, f32[2,256,128]{2,1,0:T(8,128)} %copy-done.7, pred[]{:T(512)S(6)} %ne.6), kind=kLoop, calls=%fused_computation.71 | loop fusion | flops 163840 | bytes 720897 | tf_op jit(solution)/shard_map/convert_element_type | solution.py:99
  89.3 1.6 %fusion.24 = f32[128,256]{0,1:T(8,128)S(1)} fusion(bf16[2048,128]{1,0:T(8,128)(2,1)} %bitcast.103, bf16[2048,256]{1,0:T(8,128)(2,1)S(1)} %fusion.4), kind=kOutput, calls=%fused_computation.76 | convolution fusion | flops 134217728 | bytes 1703936 | tf_op jit(solution)/shard_map/dot_general | solution.py:127
  90.9 1.5 %collective-permute-start.16 = (f32[128,256]{0,1:T(8,128)S(1)}, f32[128,256]{0,1:T(8,128)S(1)}, u32[]{:S(2)}, u32[]{:S(2)}) collective-permute-start(f32[128,256]{0,1:T(8,128)S(1)} %fusion.24), channel_id=1, source_target_pairs={{0,8},{8,0},{16,24},{24,16},{1,9},{9,1},{17,25},{25,17},{2,10},{10... | collective-permute-start | bytes 393224 | tf_op jit(solution)/shard_map/ppermute | solution.py:20
  92.4 2.1 %collective-permute-done.20 = bf16[256,128]{1,0:T(8,128)(2,1)S(1)} collective-permute-done((bf16[256,128]{1,0:T(8,128)(2,1)S(1)}, bf16[256,128]{1,0:T(8,128)(2,1)S(1)}, u32[]{:S(2)}, u32[]{:S(2)}) %collective-permute-start.20) | collective-permute-done | bytes 65568 | tf_op jit(solution)/shard_map/ppermute | solution.py:20
  101.7 2.0 %shard_map.88 = f32[256,128]{1,0:T(8,128)} custom-call(s32[25]{0:T(128)} %starts_ref.3, f32[25,128]{1,0:T(8,128)} %weights_ref.7, f32[424,128]{1,0:T(8,128)} %pad_maximum_fusion.9.extended_ref), custom_call_target="tpu_custom_call" | custom-call | flops 1638400 | bytes 360960 | tf_op jit(solution)/shard_map/pallas_call | solution.py:81
  103.7 1.9 %bitcast_subtract_fusion = f32[128,256]{0,1:T(8,128)} fusion(f32[256,128]{1,0:T(8,128)} %copy-done.9, f32[256,128]{1,0:T(8,128)} %shard_map.88, f32[128,256]{0,1:T(8,128)S(1)} %bitcast_subtract_fusion.1, f32[128,256]{0,1:T(8,128)} %add.50, f32[128,256]{0,1:T(8,128)} %collective-permute-done.17), kind=kLoop, calls=%fused_computation.38 | loop fusion | flops 196608 | bytes 786432 | tf_op jit(solution)/shard_map/sub | solution.py:141
  105.5 1.7 %copy.38 = f32[128,256]{1,0:T(8,128)} copy(f32[128,256]{0,1:T(8,128)} %bitcast_subtract_fusion) | data formatting | bytes 262144
  108.5 1.6 %fusion.5 = bf16[2048,256]{1,0:T(8,128)(2,1)} fusion(bf16[2048,256]{1,0:T(8,128)(2,1)S(1)} %copy-done.3, bf16[2048,128]{1,0:T(8,128)(2,1)S(1)} %bitcast.108, s32[2048,256]{1,0:T(8,128)S(1)} %copy.21, s32[256]{0:T(256)S(1)} %shift_right_arithmetic.23, f32[128,256]{0,1:T(8,128)S(1)} %copy-done.13), kind=kOutput, calls=%fused_computation.8 | convolution fusion | flops 137920512 | bytes 4850688 | tf_op jit(solution)/shard_map/dot_general | solution.py:112
  (116 shorter events, 33.8 us)
Async XLA Ops:
  0.6 14.8 %copy-start = (s32[2048,32]{0,1:T(8,128)S(1)}, s32[2048,32]{0,1:T(8,128)}, u32[]{:S(2)}) copy-start(s32[2048,32]{0,1:T(8,128)} %param.7) | copy-start | bytes 786436
  1.6 7.7 %collective-permute-start = (bf16[256,128]{1,0:T(8,128)(2,1)S(1)}, bf16[256,128]{1,0:T(8,128)(2,1)S(1)}, u32[]{:S(2)}, u32[]{:S(2)}) collective-permute-start(bf16[256,128]{1,0:T(8,128)(2,1)S(1)} %convert_element_type.36), channel_id=1, source_target_pairs={{0,4},{1,5},{2,6},{3,7},{4,0},{5,1},{6,2},{7,3},{8,12},{9,13},{10,... | collective-permute-start | bytes 196616 | tf_op jit(solution)/shard_map/ppermute | solution.py:20
  10.2 5.0 %collective-permute-start.1 = (bf16[2,256,128]{2,1,0:T(8,128)(2,1)S(1)}, bf16[2,256,128]{2,1,0:T(8,128)(2,1)S(1)}, u32[]{:S(2)}, u32[]{:S(2)}) collective-permute-start(bf16[2,256,128]{2,1,0:T(8,128)(2,1)S(1)} %pad_maximum_fusion.10), channel_id=1, source_target_pairs={{0,2},{1,3},{2,0},{3,1},{4,6},{5,7},{6,4},{7,5},{8,10},{9,11},{10,... | collective-permute-start | bytes 393224 | tf_op jit(solution)/shard_map/ppermute | solution.py:20
  15.3 3.6 %collective-permute-start.2 = (bf16[2,2,256,128]{3,2,1,0:T(8,128)(2,1)S(1)}, bf16[2,2,256,128]{3,2,1,0:T(8,128)(2,1)S(1)}, u32[]{:S(2)}, u32[]{:S(2)}) collective-permute-start(bf16[2,2,256,128]{3,2,1,0:T(8,128)(2,1)S(1)} %pad_maximum_fusion.3), channel_id=1, source_target_pairs={{0,1},{1,0},{2,3},{3,2},{4,5},{5,4},{6,7},{7,6},{8,9},{9,8},{10,11... | collective-permute-start | bytes 786440 | tf_op jit(solution)/shard_map/ppermute | solution.py:20
  19.1 1.9 %copy-start.5 = (bf16[2,2,2,256,128]{4,3,2,1,0:T(8,128)(2,1)}, bf16[2,2,2,256,128]{4,3,2,1,0:T(8,128)(2,1)S(1)}, u32[]{:S(2)}) copy-start(bf16[2,2,2,256,128]{4,3,2,1,0:T(8,128)(2,1)S(1)} %pad_maximum_fusion) | copy-start | bytes 1572868
  21.5 8.6 %copy-start.16 = (s32[25]{0:T(128)S(1)}, s32[25]{0:T(128)}, u32[]{:S(2)}) copy-start(s32[25]{0:T(128)} %starts_ref.3) | copy-start | bytes 304
  21.6 2.1 %collective-permute-start.3 = (f32[2,2,256,128]{3,2,0,1:T(8,128)S(1)}, f32[2,2,256,128]{3,2,0,1:T(8,128)S(1)}, u32[]{:S(2)}, u32[]{:S(2)}) collective-permute-start(f32[2,2,256,128]{3,2,0,1:T(8,128)S(1)} %select_bitcast_fusion.1), channel_id=1, source_target_pairs={{0,1},{1,0},{2,3},{3,2},{4,5},{5,4},{6,7},{7,6},{8,9},{9,8},{10,11... | collective-permute-start | bytes 1572872 | tf_op jit(solution)/shard_map/ppermute | solution.py:20
  25.3 8.9 %collective-permute-start.4 = (f32[2,256,128]{2,1,0:T(8,128)}, f32[2,256,128]{2,1,0:T(8,128)}, u32[]{:S(2)}, u32[]{:S(2)}) collective-permute-start(f32[2,256,128]{2,1,0:T(8,128)} %select_bitcast_fusion.7), channel_id=1, source_target_pairs={{0,2},{1,3},{2,0},{3,1},{4,6},{5,7},{6,4},{7,5},{8,10},{9,11},{10,... | collective-permute-start | bytes 786440 | tf_op jit(solution)/shard_map/ppermute | solution.py:20
  27.5 11.5 %collective-permute-start.11 = (f32[168,128]{1,0:T(8,128)}, f32[168,128]{1,0:T(8,128)}, u32[]{:S(2)}, u32[]{:S(2)}) collective-permute-start(f32[168,128]{1,0:T(8,128)} %slice.70), channel_id=1, source_target_pairs={{0,1},{1,2},{2,3},{3,4},{4,5},{5,6},{6,7},{8,9},{9,10},{10,11},{11... | collective-permute-start | bytes 258056 | tf_op jit(solution)/shard_map/ppermute | solution.py:15
  36.7 9.0 %collective-permute-start.5 = (f32[256,128]{1,0:T(8,128)}, f32[256,128]{1,0:T(8,128)}, u32[]{:S(2)}, u32[]{:S(2)}) collective-permute-start(f32[256,128]{1,0:T(8,128)} %select_bitcast_fusion.15), channel_id=1, source_target_pairs={{0,4},{1,5},{2,6},{3,7},{4,0},{5,1},{6,2},{7,3},{8,12},{9,13},{10,... | collective-permute-start | bytes 393224 | tf_op jit(solution)/shard_map/ppermute | solution.py:20
  42.6 11.9 %copy-start.15 = (f32[256,128]{1,0:T(8,128)S(1)}, f32[256,128]{1,0:T(8,128)}, u32[]{:S(2)}) copy-start(f32[256,128]{1,0:T(8,128)} %shard_map.85) | copy-start | bytes 393220
  47.5 6.2 %collective-permute-start.6 = (bf16[256,128]{1,0:T(8,128)(2,1)S(1)}, bf16[256,128]{1,0:T(8,128)(2,1)S(1)}, u32[]{:S(2)}, u32[]{:S(2)}) collective-permute-start(bf16[256,128]{1,0:T(8,128)(2,1)S(1)} %get-tuple-element.11), channel_id=1, source_target_pairs={{0,4},{1,5},{2,6},{3,7},{4,0},{5,1},{6,2},{7,3},{8,12},{9,13},{10,... | collective-permute-start | bytes 196616 | tf_op jit(solution)/shard_map/ppermute | solution.py:20
  49.0 6.9 %collective-permute-start.9 = (f32[128,256]{0,1:T(8,128)S(1)}, f32[128,256]{0,1:T(8,128)S(1)}, u32[]{:S(2)}, u32[]{:S(2)}) collective-permute-start(f32[128,256]{0,1:T(8,128)S(1)} %fusion.23), channel_id=1, source_target_pairs={{0,8},{8,0},{16,24},{24,16},{1,9},{9,1},{17,25},{25,17},{2,10},{10... | collective-permute-start | bytes 393224 | tf_op jit(solution)/shard_map/ppermute | solution.py:20
  53.7 5.0 %collective-permute-start.7 = (bf16[2,256,128]{2,1,0:T(8,128)(2,1)S(1)}, bf16[2,256,128]{2,1,0:T(8,128)(2,1)S(1)}, u32[]{:S(2)}, u32[]{:S(2)}) collective-permute-start(bf16[2,256,128]{2,1,0:T(8,128)(2,1)S(1)} %pad_maximum_fusion.11), channel_id=1, source_target_pairs={{0,2},{1,3},{2,0},{3,1},{4,6},{5,7},{6,4},{7,5},{8,10},{9,11},{10,... | collective-permute-start | bytes 393224 | tf_op jit(solution)/shard_map/ppermute | solution.py:20
  54.6 4.3 %collective-permute-start.12 = (f32[168,128]{1,0:T(8,128)S(1)}, f32[168,128]{1,0:T(8,128)S(1)}, u32[]{:S(2)}, u32[]{:S(2)}) collective-permute-start(f32[168,128]{1,0:T(8,128)S(1)} %slice.71), channel_id=1, source_target_pairs={{1,0},{2,1},{3,2},{4,3},{5,4},{6,5},{7,6},{9,8},{10,9},{11,10},{12... | collective-permute-start | bytes 258056 | tf_op jit(solution)/shard_map/ppermute | solution.py:15
  55.9 6.4 %collective-permute-start.10 = (f32[128,256]{0,1:T(8,128)S(1)}, f32[128,256]{0,1:T(8,128)}, u32[]{:S(2)}, u32[]{:S(2)}) collective-permute-start(f32[128,256]{0,1:T(8,128)S(1)} %add.43), channel_id=1, source_target_pairs={{0,16},{8,24},{16,0},{24,8},{1,17},{9,25},{17,1},{25,9},{2,18},{10... | collective-permute-start | bytes 393224 | tf_op jit(solution)/shard_map/ppermute | solution.py:20
  58.8 4.5 %collective-permute-start.8 = (bf16[2,2,256,128]{3,2,0,1:T(8,128)(2,1)S(1)}, bf16[2,2,256,128]{3,2,0,1:T(8,128)(2,1)}, u32[]{:S(2)}, u32[]{:S(2)}) collective-permute-start(bf16[2,2,256,128]{3,2,0,1:T(8,128)(2,1)S(1)} %pad_maximum_fusion.4), channel_id=1, source_target_pairs={{0,1},{1,0},{2,3},{3,2},{4,5},{5,4},{6,7},{7,6},{8,9},{9,8},{10,11... | collective-permute-start | bytes 786440 | tf_op jit(solution)/shard_map/ppermute | solution.py:20
  61.6 2.9 %copy-start.2 = (bf16[2048,256]{1,0:T(8,128)(2,1)S(1)}, bf16[2048,256]{1,0:T(8,128)(2,1)}, u32[]{:S(2)}) copy-start(bf16[2048,256]{1,0:T(8,128)(2,1)} %param.6) | copy-start | bytes 3145732
  65.8 2.6 %collective-permute-start.13 = (f32[2,2,256,128]{3,2,0,1:T(8,128)S(1)}, f32[2,2,256,128]{3,2,0,1:T(8,128)S(1)}, u32[]{:S(2)}, u32[]{:S(2)}) collective-permute-start(f32[2,2,256,128]{3,2,0,1:T(8,128)S(1)} %select_bitcast_fusion), channel_id=1, source_target_pairs={{0,1},{1,0},{2,3},{3,2},{4,5},{5,4},{6,7},{7,6},{8,9},{9,8},{10,11... | collective-permute-start | bytes 1572872 | tf_op jit(solution)/shard_map/ppermute | solution.py:20
  68.5 8.7 %collective-permute-start.14 = (f32[2,256,128]{2,1,0:T(8,128)S(1)}, f32[2,256,128]{2,1,0:T(8,128)S(1)}, u32[]{:S(2)}, u32[]{:S(2)}) collective-permute-start(f32[2,256,128]{2,1,0:T(8,128)S(1)} %select_bitcast_fusion.4), channel_id=1, source_target_pairs={{0,2},{1,3},{2,0},{3,1},{4,6},{5,7},{6,4},{7,5},{8,10},{9,11},{10,... | collective-permute-start | bytes 786440 | tf_op jit(solution)/shard_map/ppermute | solution.py:20
  69.6 10.5 %collective-permute-start.18 = (f32[168,128]{1,0:T(8,128)S(1)}, f32[168,128]{1,0:T(8,128)S(1)}, u32[]{:S(2)}, u32[]{:S(2)}) collective-permute-start(f32[168,128]{1,0:T(8,128)S(1)} %slice.78), channel_id=1, source_target_pairs={{0,1},{1,2},{2,3},{3,4},{4,5},{5,6},{6,7},{8,9},{9,10},{10,11},{11... | collective-permute-start | bytes 258056 | tf_op jit(solution)/shard_map/ppermute | solution.py:15
  78.5 9.0 %collective-permute-start.15 = (f32[256,128]{1,0:T(8,128)}, f32[256,128]{1,0:T(8,128)}, u32[]{:S(2)}, u32[]{:S(2)}) collective-permute-start(f32[256,128]{1,0:T(8,128)} %select_bitcast_fusion.12), channel_id=1, source_target_pairs={{0,4},{1,5},{2,6},{3,7},{4,0},{5,1},{6,2},{7,3},{8,12},{9,13},{10,... | collective-permute-start | bytes 393224 | tf_op jit(solution)/shard_map/ppermute | solution.py:20
  82.7 11.9 %copy-start.14 = (f32[256,128]{1,0:T(8,128)S(1)}, f32[256,128]{1,0:T(8,128)}, u32[]{:S(2)}) copy-start(f32[256,128]{1,0:T(8,128)} %shard_map.87) | copy-start | bytes 393220
  89.3 5.2 %collective-permute-start.20 = (bf16[256,128]{1,0:T(8,128)(2,1)S(1)}, bf16[256,128]{1,0:T(8,128)(2,1)S(1)}, u32[]{:S(2)}, u32[]{:S(2)}) collective-permute-start(bf16[256,128]{1,0:T(8,128)(2,1)S(1)} %get-tuple-element.9), channel_id=1, source_target_pairs={{0,4},{1,5},{2,6},{3,7},{4,0},{5,1},{6,2},{7,3},{8,12},{9,13},{10,... | collective-permute-start | bytes 196616 | tf_op jit(solution)/shard_map/ppermute | solution.py:20
  90.9 5.3 %collective-permute-start.16 = (f32[128,256]{0,1:T(8,128)S(1)}, f32[128,256]{0,1:T(8,128)S(1)}, u32[]{:S(2)}, u32[]{:S(2)}) collective-permute-start(f32[128,256]{0,1:T(8,128)S(1)} %fusion.24), channel_id=1, source_target_pairs={{0,8},{8,0},{16,24},{24,16},{1,9},{9,1},{17,25},{25,17},{2,10},{10... | collective-permute-start | bytes 393224 | tf_op jit(solution)/shard_map/ppermute | solution.py:20
  94.5 5.0 %collective-permute-start.21 = (bf16[2,256,128]{2,1,0:T(8,128)(2,1)S(1)}, bf16[2,256,128]{2,1,0:T(8,128)(2,1)S(1)}, u32[]{:S(2)}, u32[]{:S(2)}) collective-permute-start(bf16[2,256,128]{2,1,0:T(8,128)(2,1)S(1)} %pad_maximum_fusion.12), channel_id=1, source_target_pairs={{0,2},{1,3},{2,0},{3,1},{4,6},{5,7},{6,4},{7,5},{8,10},{9,11},{10,... | collective-permute-start | bytes 393224 | tf_op jit(solution)/shard_map/ppermute | solution.py:20
  94.7 6.3 %copy-start.9 = (f32[256,128]{1,0:T(8,128)}, f32[256,128]{1,0:T(8,128)S(1)}, u32[]{:S(2)}) copy-start(f32[256,128]{1,0:T(8,128)S(1)} %subtract_select_fusion) | copy-start | bytes 393220
  94.7 6.2 %collective-permute-start.19 = (f32[168,128]{1,0:T(8,128)S(1)}, f32[168,128]{1,0:T(8,128)S(1)}, u32[]{:S(2)}, u32[]{:S(2)}) collective-permute-start(f32[168,128]{1,0:T(8,128)S(1)} %slice.79), channel_id=1, source_target_pairs={{1,0},{2,1},{3,2},{4,3},{5,4},{6,5},{7,6},{9,8},{10,9},{11,10},{12... | collective-permute-start | bytes 258056 | tf_op jit(solution)/shard_map/ppermute | solution.py:15
  96.9 6.8 %collective-permute-start.17 = (f32[128,256]{0,1:T(8,128)}, f32[128,256]{0,1:T(8,128)}, u32[]{:S(2)}, u32[]{:S(2)}) collective-permute-start(f32[128,256]{0,1:T(8,128)} %add.50), channel_id=1, source_target_pairs={{0,16},{8,24},{16,0},{24,8},{1,17},{9,25},{17,1},{25,9},{2,18},{10... | collective-permute-start | bytes 393224 | tf_op jit(solution)/shard_map/ppermute | solution.py:20
  101.0 6.3 %collective-permute-start.22 = (bf16[2,2,256,128]{3,2,0,1:T(8,128)(2,1)}, bf16[2,2,256,128]{3,2,0,1:T(8,128)(2,1)}, u32[]{:S(2)}, u32[]{:S(2)}) collective-permute-start(bf16[2,2,256,128]{3,2,0,1:T(8,128)(2,1)} %pad_maximum_fusion.5), channel_id=1, source_target_pairs={{0,1},{1,0},{2,3},{3,2},{4,5},{5,4},{6,7},{7,6},{8,9},{9,8},{10,11... | collective-permute-start | bytes 786440 | tf_op jit(solution)/shard_map/ppermute | solution.py:20
  103.6 4.8 %copy-start.3 = (bf16[2048,256]{1,0:T(8,128)(2,1)S(1)}, bf16[2048,256]{1,0:T(8,128)(2,1)}, u32[]{:S(2)}) copy-start(bf16[2048,256]{1,0:T(8,128)(2,1)} %param.6) | copy-start | bytes 3145732
  105.5 2.9 %copy-start.13 = (f32[128,256]{0,1:T(8,128)S(1)}, f32[128,256]{0,1:T(8,128)}, u32[]{:S(2)}) copy-start(f32[128,256]{0,1:T(8,128)} %bitcast_subtract_fusion) | copy-start | bytes 393220
  (8 other events, 7.9 us)
where the time goes:
time: 111 us; the launch traced here: 110 us
  waiting for transfers between devices  36.2 us (33%)
  starting transfers between devices  26.3 us (24%)
  other arithmetic  20.3 us (18%)
  local copies, waits for them, and re-layouts  11.5 us (10%)
  Pallas kernels  7.83 us (7%)
  matrix products  6.8 us (6%)
  between operations  1.16 us (1%)
    ppermute x19, waiting for transfers between devices, exchange(): return lax.ppermute(block, axis, [(i, i ^ bit) for i in range(devices)])  36.2 us
    ppermute x19, starting transfers between devices, exchange(): return lax.ppermute(block, axis, [(i, i ^ bit) for i in range(devices)])  19.3 us
    pallas_call x4, Pallas kernels, lagged_sum(): pl.pallas_call(lag_kernel, out_shape=jax.ShapeDtypeStruct((width, rank),...  7.83 us
    ppermute x4, starting transfers between devices, shifted(): return lax.ppermute(block, axis, route)  7.03 us
    unnamed x36, local copies, waits for them, and re-layouts  6.97 us
    convert_element_type x3, other arithmetic, fetch_rows(): return doubling_gather(factors.astype(jnp.bfloat16), 'tm')  4.51 us
    another operation x18, other arithmetic, doubling_gather(): block = jnp.stack([low, high], axis=step)  4.11 us
    shift_right_arithmetic x4, local copies, waits for them, and re-layouts, unpack(): bit_values = jnp.right_shift(packed_words[:, :, None], shift_amounts) & 1  3.61 us
  transfers between devices with their start and end apart: 23, of which 14 were waited for; matrix products, arithmetic and copies ran while one was open for 20% of the time, Pallas kernels for 7%

commit v1 on v0

--- a/solution.py
+++ b/solution.py
@@ -42,8 +42,8 @@
         low = lax.index_in_dim(block, 0, at, keepdims=False)
         high = lax.index_in_dim(block, 1, at, keepdims=False)
         keep = jnp.where(upper, high, low)
-        send = jnp.where(upper, low, high)
-        block = keep + exchange(send, axis, bit)
+        send = jnp.where(upper, low, high).astype(jnp.bfloat16)
+        block = keep + exchange(send, axis, bit).astype(jnp.float32)
     return block
 
 

time: 111 us -> 105 us (0.946)
  waiting for transfers between devices: 36.2 us -> 28.1 us
  other arithmetic: 20.3 us -> 22 us
    ppermute x19, waiting for transfers between devices: 36.2 us -> 28.1 us  [exchange(): return lax.ppermute(block, axis, [(i, i ^ bit) for i in range(devices)])]
    convert_element_type x0 -> x6, other arithmetic: none -> 2.79 us  [halving_sum(): send = jnp.where(upper, low, high).astype(jnp.bfloat16)]
    select_n x6 -> x0, other arithmetic: 2.23 us -> none  [halving_sum(): send = jnp.where(upper, low, high)]
    add x4, other arithmetic: 1.35 us -> 2.58 us  [halving_sum(): block = keep + exchange(send, axis, bit).astype(jnp.float32)]
    unnamed x36 -> x40, local copies, waits for them, and re-layouts: 6.97 us -> 7.73 us
  transfers between devices with their start and end apart: 23 -> 23, of which waited for: 14 -> 13; matrix products, arithmetic and copies ran while one was open for 20% -> 23% of each run, Pallas kernels for 7% -> 8%
where the time goes in v1:
time: 105 us; the launch traced here: 104 us
  waiting for transfers between devices  28.1 us (27%)
  starting transfers between devices  25.7 us (24%)
  other arithmetic  22 us (21%)
  local copies, waits for them, and re-layouts  12.2 us (12%)
  Pallas kernels  7.91 us (8%)
  matrix products  6.79 us (6%)
  between operations  1.18 us (1%)
    ppermute x19, waiting for transfers between devices, exchange(): return lax.ppermute(block, axis, [(i, i ^ bit) for i in range(devices)])  28.1 us
    ppermute x19, starting transfers between devices, exchange(): return lax.ppermute(block, axis, [(i, i ^ bit) for i in range(devices)])  18.8 us
    pallas_call x4, Pallas kernels, lagged_sum(): pl.pallas_call(lag_kernel, out_shape=jax.ShapeDtypeStruct((width, rank),...  7.91 us
    unnamed x40, local copies, waits for them, and re-layouts  7.73 us
    ppermute x4, starting transfers between devices, shifted(): return lax.ppermute(block, axis, route)  6.9 us
    convert_element_type x3, other arithmetic, fetch_rows(): return doubling_gather(factors.astype(jnp.bfloat16), 'tm')  4.47 us
    another operation x18, other arithmetic, doubling_gather(): block = jnp.stack([low, high], axis=step)  4.11 us
    shift_right_arithmetic x4, local copies, waits for them, and re-layouts, unpack(): bit_values = jnp.right_shift(packed_words[:, :, None], shift_amounts) & 1  3.62 us
  transfers between devices with their start and end apart: 23, of which 13 were waited for; matrix products, arithmetic and copies ran while one was open for 23% of the time, Pallas kernels for 8%

profile of v1, /device:TPU:0, one launch (start us, length us, event | category | flops | bytes accessed | tf_op | source)
XLA Modules:
  0.0 103.9 jit_solution(12055915113981485721)
XLA Ops:
  1.6 4.0 %collective-permute-start = (bf16[256,128]{1,0:T(8,128)(2,1)S(1)}, bf16[256,128]{1,0:T(8,128)(2,1)S(1)}, u32[]{:S(2)}, u32[]{:S(2)}) collective-permute-start(bf16[256,128]{1,0:T(8,128)(2,1)S(1)} %convert_element_type.90), channel_id=1, source_target_pairs={{0,4},{1,5},{2,6},{3,7},{4,0},{5,1},{6,2},{7,3},{8,12},{9,13},{10,... | collective-permute-start | bytes 196616 | tf_op jit(solution)/shard_map/ppermute | solution.py:20
  5.6 3.6 %collective-permute-done = bf16[256,128]{1,0:T(8,128)(2,1)S(1)} collective-permute-done((bf16[256,128]{1,0:T(8,128)(2,1)S(1)}, bf16[256,128]{1,0:T(8,128)(2,1)S(1)}, u32[]{:S(2)}, u32[]{:S(2)}) %collective-permute-start) | collective-permute-done | bytes 65568 | tf_op jit(solution)/shard_map/ppermute | solution.py:20
  11.0 4.3 %collective-permute-done.1 = bf16[2,256,128]{2,1,0:T(8,128)(2,1)S(1)} collective-permute-done((bf16[2,256,128]{2,1,0:T(8,128)(2,1)S(1)}, bf16[2,256,128]{2,1,0:T(8,128)(2,1)S(1)}, u32[]{:S(2)}, u32[]{:S(2)}) %collective-permute-start.1) | collective-permute-done | bytes 131104 | tf_op jit(solution)/shard_map/ppermute | solution.py:20
  15.4 1.6 %broadcast_bitcast_fusion = s32[2048,256]{0,1:T(8,128)} fusion(s32[2048,32]{0,1:T(8,128)S(1)} %copy-done), kind=kLoop, calls=%fused_computation.10 | loop fusion | bytes 2359296 | tf_op jit(solution)/shard_map/shift_right_arithmetic | solution.py:66
  17.0 1.9 %copy.21 = s32[2048,256]{1,0:T(8,128)S(1)} copy(s32[2048,256]{0,1:T(8,128)} %broadcast_bitcast_fusion) | data formatting | bytes 4194304 | tf_op jit(solution)/shard_map/shift_right_arithmetic | solution.py:66
  25.2 2.6 %collective-permute-start.11 = (f32[168,128]{1,0:T(8,128)}, f32[168,128]{1,0:T(8,128)}, u32[]{:S(2)}, u32[]{:S(2)}) collective-permute-start(f32[168,128]{1,0:T(8,128)} %slice.70), channel_id=1, source_target_pairs={{0,1},{1,2},{2,3},{3,4},{4,5},{5,6},{6,7},{8,9},{9,10},{10,11},{11... | collective-permute-start | bytes 258056 | tf_op jit(solution)/shard_map/ppermute | solution.py:15
  27.7 1.3 %bitcast_add_fusion.1 = f32[2,2,256,128]{3,2,0,1:T(8,128)S(1)} fusion(bf16[2,2,256,128]{3,2,0,1:T(8,128)(2,1)} %collective-permute-done.3, f32[2,2,1,256,128]{4,3,2,1,0:T(8,128)} %copy-done.4, f32[2,2,1,256,128]{4,3,2,1,0:T(8,128)} %copy-done.5, pred[]{:T(512)S(6)} %ne.8), kind=kLoop, calls=%fused_computation.15 | loop fusion | flops 393216 | bytes 1835009 | tf_op jit(solution)/shard_map/add | solution.py:46
  31.2 5.7 %collective-permute-done.4 = bf16[2,256,128]{2,1,0:T(8,128)(2,1)} collective-permute-done((bf16[2,256,128]{2,1,0:T(8,128)(2,1)}, bf16[2,256,128]{2,1,0:T(8,128)(2,1)}, u32[]{:S(2)}, u32[]{:S(2)}) %collective-permute-start.4) | collective-permute-done | bytes 131104 | tf_op jit(solution)/shard_map/ppermute | solution.py:20
  40.6 1.6 %pad_maximum_fusion.6.extended_ref = f32[424,128]{1,0:T(8,128)} fusion(f32[256,128]{1,0:T(8,128)S(1)} %bitcast.107, f32[168,128]{1,0:T(8,128)} %collective-permute-done.11), kind=kLoop, calls=%fused_computation.33 | loop fusion | flops 54272 | bytes 434176 | tf_op jit(solution)/shard_map/concatenate | solution.py:134
  42.2 2.0 %shard_map.85 = f32[256,128]{1,0:T(8,128)} custom-call(s32[25]{0:T(128)} %broadcast_subtract_fusion.starts_ref, f32[25,128]{1,0:T(8,128)} %weights_ref.7, f32[424,128]{1,0:T(8,128)} %pad_maximum_fusion.6.extended_ref), custom_call_target="tpu_custom_call" | custom-call | flops 1638400 | bytes 360960 | tf_op jit(solution)/shard_map/pallas_call | solution.py:81
  44.2 1.4 %collective-permute-done.5 = bf16[256,128]{1,0:T(8,128)(2,1)} collective-permute-done((bf16[256,128]{1,0:T(8,128)(2,1)}, bf16[256,128]{1,0:T(8,128)(2,1)}, u32[]{:S(2)}, u32[]{:S(2)}) %collective-permute-start.5) | collective-permute-done | bytes 65568 | tf_op jit(solution)/shard_map/ppermute | solution.py:20
  45.6 1.8 %fusion.25 = (bf16[256,128]{1,0:T(8,128)(2,1)S(1)}, f32[256,128]{1,0:T(8,128)}) fusion(f32[256,128]{1,0:T(8,128)} %param.8, bf16[256,128]{1,0:T(8,128)(2,1)} %collective-permute-done.5, f32[2,256,128]{2,1,0:T(8,128)} %copy-done.11, pred[]{:T(512)S(6)} %ne.6), kind=kLoop, calls=%fused_computation.78 | loop fusion | flops 196608 | bytes 655361 | tf_op jit(solution)/shard_map/convert_element_type | solution.py:99
  48.3 1.6 %fusion.29 = f32[128,256]{0,1:T(8,128)S(1)} fusion(bf16[2048,128]{1,0:T(8,128)(2,1)} %bitcast.101, bf16[2048,256]{1,0:T(8,128)(2,1)S(1)} %fusion.3), kind=kOutput, calls=%fused_computation.81 | convolution fusion | flops 134217728 | bytes 1703936 | tf_op jit(solution)/shard_map/dot_general | solution.py:127
  49.9 1.6 %collective-permute-start.9 = (f32[128,256]{0,1:T(8,128)S(1)}, f32[128,256]{0,1:T(8,128)S(1)}, u32[]{:S(2)}, u32[]{:S(2)}) collective-permute-start(f32[128,256]{0,1:T(8,128)S(1)} %fusion.29), channel_id=1, source_target_pairs={{0,8},{8,0},{16,24},{24,16},{1,9},{9,1},{17,25},{25,17},{2,10},{10... | collective-permute-start | bytes 393224 | tf_op jit(solution)/shard_map/ppermute | solution.py:20
  51.4 1.8 %collective-permute-done.6 = bf16[256,128]{1,0:T(8,128)(2,1)S(1)} collective-permute-done((bf16[256,128]{1,0:T(8,128)(2,1)S(1)}, bf16[256,128]{1,0:T(8,128)(2,1)S(1)}, u32[]{:S(2)}, u32[]{:S(2)}) %collective-permute-start.6) | collective-permute-done | bytes 65568 | tf_op jit(solution)/shard_map/ppermute | solution.py:20
  55.2 1.6 %collective-permute-start.10 = (f32[128,256]{0,1:T(8,128)S(1)}, f32[128,256]{0,1:T(8,128)}, u32[]{:S(2)}, u32[]{:S(2)}) collective-permute-start(f32[128,256]{0,1:T(8,128)S(1)} %add.43), channel_id=1, source_target_pairs={{0,16},{8,24},{16,0},{24,8},{1,17},{9,25},{17,1},{25,9},{2,18},{10... | collective-permute-start | bytes 393224 | tf_op jit(solution)/shard_map/ppermute | solution.py:20
  56.8 1.5 %collective-permute-done.7 = bf16[2,256,128]{2,1,0:T(8,128)(2,1)S(1)} collective-permute-done((bf16[2,256,128]{2,1,0:T(8,128)(2,1)S(1)}, bf16[2,256,128]{2,1,0:T(8,128)(2,1)S(1)}, u32[]{:S(2)}, u32[]{:S(2)}) %collective-permute-start.7) | collective-permute-done | bytes 131104 | tf_op jit(solution)/shard_map/ppermute | solution.py:20
  59.2 2.0 %shard_map.86 = f32[256,128]{1,0:T(8,128)} custom-call(s32[25]{0:T(128)} %starts_ref.3, f32[25,128]{1,0:T(8,128)} %weights_ref.7, f32[424,128]{1,0:T(8,128)} %pad_maximum_fusion.7.extended_ref), custom_call_target="tpu_custom_call" | custom-call | flops 1638400 | bytes 360960 | tf_op jit(solution)/shard_map/pallas_call | solution.py:81
  68.8 1.8 %collective-permute-start.18 = (f32[168,128]{1,0:T(8,128)S(1)}, f32[168,128]{1,0:T(8,128)S(1)}, u32[]{:S(2)}, u32[]{:S(2)}) collective-permute-start(f32[168,128]{1,0:T(8,128)S(1)} %slice.78), channel_id=1, source_target_pairs={{0,1},{1,2},{2,3},{3,4},{4,5},{5,6},{6,7},{8,9},{9,10},{10,11},{11... | collective-permute-start | bytes 258056 | tf_op jit(solution)/shard_map/ppermute | solution.py:15
  70.5 2.9 %collective-permute-done.14 = bf16[2,256,128]{2,1,0:T(8,128)(2,1)S(1)} collective-permute-done((bf16[2,256,128]{2,1,0:T(8,128)(2,1)S(1)}, bf16[2,256,128]{2,1,0:T(8,128)(2,1)S(1)}, u32[]{:S(2)}, u32[]{:S(2)}) %collective-permute-start.14) | collective-permute-done | bytes 131104 | tf_op jit(solution)/shard_map/ppermute | solution.py:20
  74.9 1.4 %collective-permute-start.15 = (bf16[256,128]{1,0:T(8,128)(2,1)}, bf16[256,128]{1,0:T(8,128)(2,1)}, u32[]{:S(2)}, u32[]{:S(2)}) collective-permute-start(bf16[256,128]{1,0:T(8,128)(2,1)} %fusion.15), channel_id=1, source_target_pairs={{0,4},{1,5},{2,6},{3,7},{4,0},{5,1},{6,2},{7,3},{8,12},{9,13},{10,... | collective-permute-start | bytes 196616 | tf_op jit(solution)/shard_map/ppermute | solution.py:20
  76.9 2.0 %shard_map.87 = f32[256,128]{1,0:T(8,128)} custom-call(s32[25]{0:T(128)} %broadcast_subtract_fusion.starts_ref, f32[25,128]{1,0:T(8,128)} %weights_ref.7, f32[424,128]{1,0:T(8,128)} %pad_maximum_fusion.8.extended_ref), custom_call_target="tpu_custom_call" | custom-call | flops 1638400 | bytes 360960 | tf_op jit(solution)/shard_map/pallas_call | solution.py:81
  78.9 2.1 %collective-permute-done.15 = bf16[256,128]{1,0:T(8,128)(2,1)} collective-permute-done((bf16[256,128]{1,0:T(8,128)(2,1)}, bf16[256,128]{1,0:T(8,128)(2,1)}, u32[]{:S(2)}, u32[]{:S(2)}) %collective-permute-start.15) | collective-permute-done | bytes 65568 | tf_op jit(solution)/shard_map/ppermute | solution.py:20
  81.0 1.8 %fusion.23 = (bf16[256,128]{1,0:T(8,128)(2,1)S(1)}, f32[256,128]{1,0:T(8,128)}) fusion(f32[256,128]{1,0:T(8,128)} %get-tuple-element.12, bf16[256,128]{1,0:T(8,128)(2,1)} %collective-permute-done.15, f32[2,256,128]{2,1,0:T(8,128)} %copy-done.10, pred[]{:T(512)S(6)} %ne.6), kind=kLoop, calls=%fused_computation.77 | loop fusion | flops 196608 | bytes 655361 | tf_op jit(solution)/shard_map/convert_element_type | solution.py:99
  83.5 1.6 %fusion.30 = f32[128,256]{0,1:T(8,128)S(1)} fusion(bf16[2048,128]{1,0:T(8,128)(2,1)} %bitcast.103, bf16[2048,256]{1,0:T(8,128)(2,1)S(1)} %fusion.4), kind=kOutput, calls=%fused_computation.82 | convolution fusion | flops 134217728 | bytes 1703936 | tf_op jit(solution)/shard_map/dot_general | solution.py:127
  85.1 1.6 %collective-permute-start.16 = (f32[128,256]{0,1:T(8,128)S(1)}, f32[128,256]{0,1:T(8,128)S(1)}, u32[]{:S(2)}, u32[]{:S(2)}) collective-permute-start(f32[128,256]{0,1:T(8,128)S(1)} %fusion.30), channel_id=1, source_target_pairs={{0,8},{8,0},{16,24},{24,16},{1,9},{9,1},{17,25},{25,17},{2,10},{10... | collective-permute-start | bytes 393224 | tf_op jit(solution)/shard_map/ppermute | solution.py:20
  86.6 1.7 %collective-permute-done.20 = bf16[256,128]{1,0:T(8,128)(2,1)S(1)} collective-permute-done((bf16[256,128]{1,0:T(8,128)(2,1)S(1)}, bf16[256,128]{1,0:T(8,128)(2,1)S(1)}, u32[]{:S(2)}, u32[]{:S(2)}) %collective-permute-start.20) | collective-permute-done | bytes 65568 | tf_op jit(solution)/shard_map/ppermute | solution.py:20
  90.8 1.5 %collective-permute-start.17 = (f32[128,256]{0,1:T(8,128)}, f32[128,256]{0,1:T(8,128)}, u32[]{:S(2)}, u32[]{:S(2)}) collective-permute-start(f32[128,256]{0,1:T(8,128)} %add.50), channel_id=1, source_target_pairs={{0,16},{8,24},{16,0},{24,8},{1,17},{9,25},{17,1},{25,9},{2,18},{10... | collective-permute-start | bytes 393224 | tf_op jit(solution)/shard_map/ppermute | solution.py:20
  95.6 2.0 %shard_map.88 = f32[256,128]{1,0:T(8,128)} custom-call(s32[25]{0:T(128)} %starts_ref.3, f32[25,128]{1,0:T(8,128)} %weights_ref.7, f32[424,128]{1,0:T(8,128)} %pad_maximum_fusion.9.extended_ref), custom_call_target="tpu_custom_call" | custom-call | flops 1638400 | bytes 360960 | tf_op jit(solution)/shard_map/pallas_call | solution.py:81
  97.5 1.9 %bitcast_subtract_fusion = f32[128,256]{0,1:T(8,128)} fusion(f32[256,128]{1,0:T(8,128)} %copy-done.9, f32[256,128]{1,0:T(8,128)} %shard_map.88, f32[128,256]{0,1:T(8,128)S(1)} %bitcast_subtract_fusion.1, f32[128,256]{0,1:T(8,128)} %add.50, f32[128,256]{0,1:T(8,128)} %collective-permute-done.17), kind=kLoop, calls=%fused_computation.42 | loop fusion | flops 196608 | bytes 786432 | tf_op jit(solution)/shard_map/sub | solution.py:141
  99.4 1.7 %copy.38 = f32[128,256]{1,0:T(8,128)} copy(f32[128,256]{0,1:T(8,128)} %bitcast_subtract_fusion) | data formatting | bytes 262144
  102.4 1.6 %fusion.5 = bf16[2048,256]{1,0:T(8,128)(2,1)} fusion(bf16[2048,256]{1,0:T(8,128)(2,1)S(1)} %copy-done.3, bf16[2048,128]{1,0:T(8,128)(2,1)S(1)} %bitcast.108, s32[2048,256]{1,0:T(8,128)S(1)} %copy.21, s32[256]{0:T(256)S(1)} %shift_right_arithmetic.23, f32[128,256]{0,1:T(8,128)S(1)} %copy-done.15), kind=kOutput, calls=%fused_computation.8 | convolution fusion | flops 137920512 | bytes 4850688 | tf_op jit(solution)/shard_map/dot_general | solution.py:112
  (120 shorter events, 35.4 us)
Async XLA Ops:
  0.6 14.8 %copy-start = (s32[2048,32]{0,1:T(8,128)S(1)}, s32[2048,32]{0,1:T(8,128)}, u32[]{:S(2)}) copy-start(s32[2048,32]{0,1:T(8,128)} %param.7) | copy-start | bytes 786436
  1.6 7.7 %collective-permute-start = (bf16[256,128]{1,0:T(8,128)(2,1)S(1)}, bf16[256,128]{1,0:T(8,128)(2,1)S(1)}, u32[]{:S(2)}, u32[]{:S(2)}) collective-permute-start(bf16[256,128]{1,0:T(8,128)(2,1)S(1)} %convert_element_type.90), channel_id=1, source_target_pairs={{0,4},{1,5},{2,6},{3,7},{4,0},{5,1},{6,2},{7,3},{8,12},{9,13},{10,... | collective-permute-start | bytes 196616 | tf_op jit(solution)/shard_map/ppermute | solution.py:20
  10.2 5.0 %collective-permute-start.1 = (bf16[2,256,128]{2,1,0:T(8,128)(2,1)S(1)}, bf16[2,256,128]{2,1,0:T(8,128)(2,1)S(1)}, u32[]{:S(2)}, u32[]{:S(2)}) collective-permute-start(bf16[2,256,128]{2,1,0:T(8,128)(2,1)S(1)} %pad_maximum_fusion.10), channel_id=1, source_target_pairs={{0,2},{1,3},{2,0},{3,1},{4,6},{5,7},{6,4},{7,5},{8,10},{9,11},{10,... | collective-permute-start | bytes 393224 | tf_op jit(solution)/shard_map/ppermute | solution.py:20
  15.3 3.6 %collective-permute-start.2 = (bf16[2,2,256,128]{3,2,1,0:T(8,128)(2,1)S(1)}, bf16[2,2,256,128]{3,2,1,0:T(8,128)(2,1)S(1)}, u32[]{:S(2)}, u32[]{:S(2)}) collective-permute-start(bf16[2,2,256,128]{3,2,1,0:T(8,128)(2,1)S(1)} %pad_maximum_fusion.3), channel_id=1, source_target_pairs={{0,1},{1,0},{2,3},{3,2},{4,5},{5,4},{6,7},{7,6},{8,9},{9,8},{10,11... | collective-permute-start | bytes 786440 | tf_op jit(solution)/shard_map/ppermute | solution.py:20
  19.1 1.9 %copy-start.6 = (bf16[2,2,2,256,128]{4,3,2,1,0:T(8,128)(2,1)}, bf16[2,2,2,256,128]{4,3,2,1,0:T(8,128)(2,1)S(1)}, u32[]{:S(2)}) copy-start(bf16[2,2,2,256,128]{4,3,2,1,0:T(8,128)(2,1)S(1)} %pad_maximum_fusion) | copy-start | bytes 1572868
  21.5 9.0 %copy-start.18 = (s32[25]{0:T(128)S(1)}, s32[25]{0:T(128)}, u32[]{:S(2)}) copy-start(s32[25]{0:T(128)} %starts_ref.3) | copy-start | bytes 304
  23.1 4.7 %collective-permute-start.3 = (bf16[2,2,256,128]{3,2,0,1:T(8,128)(2,1)}, bf16[2,2,256,128]{3,2,0,1:T(8,128)(2,1)}, u32[]{:S(2)}, u32[]{:S(2)}) collective-permute-start(bf16[2,2,256,128]{3,2,0,1:T(8,128)(2,1)} %fusion.6), channel_id=1, source_target_pairs={{0,1},{1,0},{2,3},{3,2},{4,5},{5,4},{6,7},{7,6},{8,9},{9,8},{10,11... | collective-permute-start | bytes 786440 | tf_op jit(solution)/shard_map/ppermute | solution.py:20
  25.2 15.4 %collective-permute-start.11 = (f32[168,128]{1,0:T(8,128)}, f32[168,128]{1,0:T(8,128)}, u32[]{:S(2)}, u32[]{:S(2)}) collective-permute-start(f32[168,128]{1,0:T(8,128)} %slice.70), channel_id=1, source_target_pairs={{0,1},{1,2},{2,3},{3,4},{4,5},{5,6},{6,7},{8,9},{9,10},{10,11},{11... | collective-permute-start | bytes 258056 | tf_op jit(solution)/shard_map/ppermute | solution.py:15
  30.6 6.3 %collective-permute-start.4 = (bf16[2,256,128]{2,1,0:T(8,128)(2,1)}, bf16[2,256,128]{2,1,0:T(8,128)(2,1)}, u32[]{:S(2)}, u32[]{:S(2)}) collective-permute-start(bf16[2,256,128]{2,1,0:T(8,128)(2,1)} %fusion.8), channel_id=1, source_target_pairs={{0,2},{1,3},{2,0},{3,1},{4,6},{5,7},{6,4},{7,5},{8,10},{9,11},{10,... | collective-permute-start | bytes 393224 | tf_op jit(solution)/shard_map/ppermute | solution.py:20
  39.4 6.2 %collective-permute-start.5 = (bf16[256,128]{1,0:T(8,128)(2,1)}, bf16[256,128]{1,0:T(8,128)(2,1)}, u32[]{:S(2)}, u32[]{:S(2)}) collective-permute-start(bf16[256,128]{1,0:T(8,128)(2,1)} %fusion.14), channel_id=1, source_target_pairs={{0,4},{1,5},{2,6},{3,7},{4,0},{5,1},{6,2},{7,3},{8,12},{9,13},{10,... | collective-permute-start | bytes 196616 | tf_op jit(solution)/shard_map/ppermute | solution.py:20
  44.2 9.5 %copy-start.17 = (f32[256,128]{1,0:T(8,128)S(1)}, f32[256,128]{1,0:T(8,128)}, u32[]{:S(2)}) copy-start(f32[256,128]{1,0:T(8,128)} %shard_map.85) | copy-start | bytes 393220
  47.4 5.9 %collective-permute-start.6 = (bf16[256,128]{1,0:T(8,128)(2,1)S(1)}, bf16[256,128]{1,0:T(8,128)(2,1)S(1)}, u32[]{:S(2)}, u32[]{:S(2)}) collective-permute-start(bf16[256,128]{1,0:T(8,128)(2,1)S(1)} %get-tuple-element.11), channel_id=1, source_target_pairs={{0,4},{1,5},{2,6},{3,7},{4,0},{5,1},{6,2},{7,3},{8,12},{9,13},{10,... | collective-permute-start | bytes 196616 | tf_op jit(solution)/shard_map/ppermute | solution.py:20
  49.9 5.3 %collective-permute-start.9 = (f32[128,256]{0,1:T(8,128)S(1)}, f32[128,256]{0,1:T(8,128)S(1)}, u32[]{:S(2)}, u32[]{:S(2)}) collective-permute-start(f32[128,256]{0,1:T(8,128)S(1)} %fusion.29), channel_id=1, source_target_pairs={{0,8},{8,0},{16,24},{24,16},{1,9},{9,1},{17,25},{25,17},{2,10},{10... | collective-permute-start | bytes 393224 | tf_op jit(solution)/shard_map/ppermute | solution.py:20
  53.3 5.0 %collective-permute-start.7 = (bf16[2,256,128]{2,1,0:T(8,128)(2,1)S(1)}, bf16[2,256,128]{2,1,0:T(8,128)(2,1)S(1)}, u32[]{:S(2)}, u32[]{:S(2)}) collective-permute-start(bf16[2,256,128]{2,1,0:T(8,128)(2,1)S(1)} %pad_maximum_fusion.11), channel_id=1, source_target_pairs={{0,2},{1,3},{2,0},{3,1},{4,6},{5,7},{6,4},{7,5},{8,10},{9,11},{10,... | collective-permute-start | bytes 393224 | tf_op jit(solution)/shard_map/ppermute | solution.py:20
  53.9 4.6 %collective-permute-start.12 = (f32[168,128]{1,0:T(8,128)S(1)}, f32[168,128]{1,0:T(8,128)S(1)}, u32[]{:S(2)}, u32[]{:S(2)}) collective-permute-start(f32[168,128]{1,0:T(8,128)S(1)} %slice.71), channel_id=1, source_target_pairs={{1,0},{2,1},{3,2},{4,3},{5,4},{6,5},{7,6},{9,8},{10,9},{11,10},{12... | collective-permute-start | bytes 258056 | tf_op jit(solution)/shard_map/ppermute | solution.py:15
  55.2 6.4 %collective-permute-start.10 = (f32[128,256]{0,1:T(8,128)S(1)}, f32[128,256]{0,1:T(8,128)}, u32[]{:S(2)}, u32[]{:S(2)}) collective-permute-start(f32[128,256]{0,1:T(8,128)S(1)} %add.43), channel_id=1, source_target_pairs={{0,16},{8,24},{16,0},{24,8},{1,17},{9,25},{17,1},{25,9},{2,18},{10... | collective-permute-start | bytes 393224 | tf_op jit(solution)/shard_map/ppermute | solution.py:20
  58.4 4.2 %collective-permute-start.8 = (bf16[2,2,256,128]{3,2,0,1:T(8,128)(2,1)S(1)}, bf16[2,2,256,128]{3,2,0,1:T(8,128)(2,1)}, u32[]{:S(2)}, u32[]{:S(2)}) collective-permute-start(bf16[2,2,256,128]{3,2,0,1:T(8,128)(2,1)S(1)} %pad_maximum_fusion.4), channel_id=1, source_target_pairs={{0,1},{1,0},{2,3},{3,2},{4,5},{5,4},{6,7},{7,6},{8,9},{9,8},{10,11... | collective-permute-start | bytes 786440 | tf_op jit(solution)/shard_map/ppermute | solution.py:20
  61.1 2.6 %copy-start.2 = (bf16[2048,256]{1,0:T(8,128)(2,1)S(1)}, bf16[2048,256]{1,0:T(8,128)(2,1)}, u32[]{:S(2)}) copy-start(bf16[2048,256]{1,0:T(8,128)(2,1)} %param.6) | copy-start | bytes 3145732
  65.0 2.5 %collective-permute-start.13 = (bf16[2,2,256,128]{3,2,0,1:T(8,128)(2,1)S(1)}, bf16[2,2,256,128]{3,2,0,1:T(8,128)(2,1)S(1)}, u32[]{:S(2)}, u32[]{:S(2)}) collective-permute-start(bf16[2,2,256,128]{3,2,0,1:T(8,128)(2,1)S(1)} %fusion.7), channel_id=1, source_target_pairs={{0,1},{1,0},{2,3},{3,2},{4,5},{5,4},{6,7},{7,6},{8,9},{9,8},{10,11... | collective-permute-start | bytes 786440 | tf_op jit(solution)/shard_map/ppermute | solution.py:20
  67.6 5.8 %collective-permute-start.14 = (bf16[2,256,128]{2,1,0:T(8,128)(2,1)S(1)}, bf16[2,256,128]{2,1,0:T(8,128)(2,1)S(1)}, u32[]{:S(2)}, u32[]{:S(2)}) collective-permute-start(bf16[2,256,128]{2,1,0:T(8,128)(2,1)S(1)} %fusion.9), channel_id=1, source_target_pairs={{0,2},{1,3},{2,0},{3,1},{4,6},{5,7},{6,4},{7,5},{8,10},{9,11},{10,... | collective-permute-start | bytes 393224 | tf_op jit(solution)/shard_map/ppermute | solution.py:20
  68.8 7.5 %collective-permute-start.18 = (f32[168,128]{1,0:T(8,128)S(1)}, f32[168,128]{1,0:T(8,128)S(1)}, u32[]{:S(2)}, u32[]{:S(2)}) collective-permute-start(f32[168,128]{1,0:T(8,128)S(1)} %slice.78), channel_id=1, source_target_pairs={{0,1},{1,2},{2,3},{3,4},{4,5},{5,6},{6,7},{8,9},{9,10},{10,11},{11... | collective-permute-start | bytes 258056 | tf_op jit(solution)/shard_map/ppermute | solution.py:15
  74.9 6.2 %collective-permute-start.15 = (bf16[256,128]{1,0:T(8,128)(2,1)}, bf16[256,128]{1,0:T(8,128)(2,1)}, u32[]{:S(2)}, u32[]{:S(2)}) collective-permute-start(bf16[256,128]{1,0:T(8,128)(2,1)} %fusion.15), channel_id=1, source_target_pairs={{0,4},{1,5},{2,6},{3,7},{4,0},{5,1},{6,2},{7,3},{8,12},{9,13},{10,... | collective-permute-start | bytes 196616 | tf_op jit(solution)/shard_map/ppermute | solution.py:20
  78.9 9.6 %copy-start.16 = (f32[256,128]{1,0:T(8,128)S(1)}, f32[256,128]{1,0:T(8,128)}, u32[]{:S(2)}) copy-start(f32[256,128]{1,0:T(8,128)} %shard_map.87) | copy-start | bytes 393220
  82.8 5.6 %collective-permute-start.20 = (bf16[256,128]{1,0:T(8,128)(2,1)S(1)}, bf16[256,128]{1,0:T(8,128)(2,1)S(1)}, u32[]{:S(2)}, u32[]{:S(2)}) collective-permute-start(bf16[256,128]{1,0:T(8,128)(2,1)S(1)} %get-tuple-element.9), channel_id=1, source_target_pairs={{0,4},{1,5},{2,6},{3,7},{4,0},{5,1},{6,2},{7,3},{8,12},{9,13},{10,... | collective-permute-start | bytes 196616 | tf_op jit(solution)/shard_map/ppermute | solution.py:20
  85.1 5.0 %collective-permute-start.16 = (f32[128,256]{0,1:T(8,128)S(1)}, f32[128,256]{0,1:T(8,128)S(1)}, u32[]{:S(2)}, u32[]{:S(2)}) collective-permute-start(f32[128,256]{0,1:T(8,128)S(1)} %fusion.30), channel_id=1, source_target_pairs={{0,8},{8,0},{16,24},{24,16},{1,9},{9,1},{17,25},{25,17},{2,10},{10... | collective-permute-start | bytes 393224 | tf_op jit(solution)/shard_map/ppermute | solution.py:20
  88.4 5.0 %collective-permute-start.21 = (bf16[2,256,128]{2,1,0:T(8,128)(2,1)S(1)}, bf16[2,256,128]{2,1,0:T(8,128)(2,1)S(1)}, u32[]{:S(2)}, u32[]{:S(2)}) collective-permute-start(bf16[2,256,128]{2,1,0:T(8,128)(2,1)S(1)} %pad_maximum_fusion.12), channel_id=1, source_target_pairs={{0,2},{1,3},{2,0},{3,1},{4,6},{5,7},{6,4},{7,5},{8,10},{9,11},{10,... | collective-permute-start | bytes 393224 | tf_op jit(solution)/shard_map/ppermute | solution.py:20
  88.6 6.3 %copy-start.9 = (f32[256,128]{1,0:T(8,128)}, f32[256,128]{1,0:T(8,128)S(1)}, u32[]{:S(2)}) copy-start(f32[256,128]{1,0:T(8,128)S(1)} %subtract_select_fusion) | copy-start | bytes 393220
  88.6 6.2 %collective-permute-start.19 = (f32[168,128]{1,0:T(8,128)S(1)}, f32[168,128]{1,0:T(8,128)S(1)}, u32[]{:S(2)}, u32[]{:S(2)}) collective-permute-start(f32[168,128]{1,0:T(8,128)S(1)} %slice.79), channel_id=1, source_target_pairs={{1,0},{2,1},{3,2},{4,3},{5,4},{6,5},{7,6},{9,8},{10,9},{11,10},{12... | collective-permute-start | bytes 258056 | tf_op jit(solution)/shard_map/ppermute | solution.py:15
  90.8 6.8 %collective-permute-start.17 = (f32[128,256]{0,1:T(8,128)}, f32[128,256]{0,1:T(8,128)}, u32[]{:S(2)}, u32[]{:S(2)}) collective-permute-start(f32[128,256]{0,1:T(8,128)} %add.50), channel_id=1, source_target_pairs={{0,16},{8,24},{16,0},{24,8},{1,17},{9,25},{17,1},{25,9},{2,18},{10... | collective-permute-start | bytes 393224 | tf_op jit(solution)/shard_map/ppermute | solution.py:20
  94.8 6.3 %collective-permute-start.22 = (bf16[2,2,256,128]{3,2,0,1:T(8,128)(2,1)}, bf16[2,2,256,128]{3,2,0,1:T(8,128)(2,1)}, u32[]{:S(2)}, u32[]{:S(2)}) collective-permute-start(bf16[2,2,256,128]{3,2,0,1:T(8,128)(2,1)} %pad_maximum_fusion.5), channel_id=1, source_target_pairs={{0,1},{1,0},{2,3},{3,2},{4,5},{5,4},{6,7},{7,6},{8,9},{9,8},{10,11... | collective-permute-start | bytes 786440 | tf_op jit(solution)/shard_map/ppermute | solution.py:20
  97.5 4.8 %copy-start.3 = (bf16[2048,256]{1,0:T(8,128)(2,1)S(1)}, bf16[2048,256]{1,0:T(8,128)(2,1)}, u32[]{:S(2)}) copy-start(bf16[2048,256]{1,0:T(8,128)(2,1)} %param.6) | copy-start | bytes 3145732
  99.4 2.9 %copy-start.15 = (f32[128,256]{0,1:T(8,128)S(1)}, f32[128,256]{0,1:T(8,128)}, u32[]{:S(2)}) copy-start(f32[128,256]{0,1:T(8,128)} %bitcast_subtract_fusion) | copy-start | bytes 393220
  (10 other events, 10.2 us)

commit v2 on v1

--- a/solution.py
+++ b/solution.py
@@ -62,9 +62,13 @@
 
 
 def unpack(packed_words):
-    shift_amounts = jnp.arange(8, dtype=jnp.int32)
-    bit_values = jnp.right_shift(packed_words[:, :, None], shift_amounts) & 1
-    return bit_values.reshape(packed_words.shape[0], packed_words.shape[1] * 8).astype(jnp.float32)
+    words = packed_words.shape[1]
+    hour = jnp.arange(words * 8, dtype=jnp.int32)
+    spread = (hour[None, :] // 8 == jnp.arange(words, dtype=jnp.int32)[:, None]).astype(jnp.bfloat16)
+    repeated = jnp.dot(
+        packed_words.astype(jnp.bfloat16), spread, preferred_element_type=jnp.float32
+    ).astype(jnp.int32)
+    return (jnp.right_shift(repeated, hour % 8) & 1).astype(jnp.float32)
 
 
 def lag_kernel(starts_ref, weights_ref, extended_ref, out_ref):

time: 105 us -> 99.8 us (0.950)
  waiting for transfers between devices: 28.1 us -> 23.8 us
  starting transfers between devices: 25.7 us -> 27.9 us
  local copies, waits for them, and re-layouts: 12.2 us -> 10.5 us
  other arithmetic: 22 us -> 20.4 us
    ppermute x19, waiting for transfers between devices: 28.1 us -> 23.8 us  [exchange(): return lax.ppermute(block, axis, [(i, i ^ bit) for i in range(devices)])]
    shift_right_arithmetic x4 -> x0, local copies, waits for them, and re-layouts: 3.62 us -> none  [unpack(): bit_values = jnp.right_shift(packed_words[:, :, None], shift_amounts) & 1]
    unnamed x40 -> x44, local copies, waits for them, and re-layouts: 7.73 us -> 9.62 us
    ppermute x19, starting transfers between devices: 18.8 us -> 20.4 us  [exchange(): return lax.ppermute(block, axis, [(i, i ^ bit) for i in range(devices)])]
  transfers between devices with their start and end apart: 23 -> 23, of which waited for: 13 -> 12; matrix products, arithmetic and copies ran while one was open for 23% -> 19% of each run, Pallas kernels for 8% -> 8%
where the time goes in v2:
time: 99.8 us; the launch traced here: 99.2 us
  starting transfers between devices  27.9 us (28%)
  waiting for transfers between devices  23.8 us (24%)
  other arithmetic  20.4 us (20%)
  local copies, waits for them, and re-layouts  10.5 us (11%)
  Pallas kernels  7.88 us (8%)
  matrix products  7.46 us (7%)
  between operations  1.09 us (1%)
    ppermute x19, waiting for transfers between devices, exchange(): return lax.ppermute(block, axis, [(i, i ^ bit) for i in range(devices)])  23.8 us
    ppermute x19, starting transfers between devices, exchange(): return lax.ppermute(block, axis, [(i, i ^ bit) for i in range(devices)])  20.4 us
    unnamed x44, local copies, waits for them, and re-layouts  9.62 us
    pallas_call x4, Pallas kernels, lagged_sum(): pl.pallas_call(lag_kernel, out_shape=jax.ShapeDtypeStruct((width, rank),...  7.88 us
    ppermute x4, starting transfers between devices, shifted(): return lax.ppermute(block, axis, route)  7.51 us
    another operation x18, other arithmetic, doubling_gather(): block = jnp.stack([low, high], axis=step)  4.91 us
    convert_element_type x3, other arithmetic, fetch_rows(): return doubling_gather(factors.astype(jnp.bfloat16), 'tm')  4.2 us
    dot_general x2, matrix products, local(): lax.dot_general(rows_low, misfit, (((0,), (0,)), ((), ())), preferred_ele...  3.56 us
  transfers between devices with their start and end apart: 23, of which 12 were waited for; matrix products, arithmetic and copies ran while one was open for 19% of the time, Pallas kernels for 8%

profile of v2, /device:TPU:0, one launch (start us, length us, event | category | flops | bytes accessed | tf_op | source)
XLA Modules:
  0.0 99.2 jit_solution(734266321401007211)
XLA Ops:
  1.6 4.0 %collective-permute-start = (bf16[256,128]{1,0:T(8,128)(2,1)S(1)}, bf16[256,128]{1,0:T(8,128)(2,1)S(1)}, u32[]{:S(2)}, u32[]{:S(2)}) collective-permute-start(bf16[256,128]{1,0:T(8,128)(2,1)S(1)} %convert_element_type.104), channel_id=1, source_target_pairs={{0,4},{1,5},{2,6},{3,7},{4,0},{5,1},{6,2},{7,3},{8,12},{9,13},{10,... | collective-permute-start | bytes 196616 | tf_op jit(solution)/shard_map/ppermute | solution.py:20
  5.6 3.6 %collective-permute-done = bf16[256,128]{1,0:T(8,128)(2,1)S(1)} collective-permute-done((bf16[256,128]{1,0:T(8,128)(2,1)S(1)}, bf16[256,128]{1,0:T(8,128)(2,1)S(1)}, u32[]{:S(2)}, u32[]{:S(2)}) %collective-permute-start) | collective-permute-done | bytes 65568 | tf_op jit(solution)/shard_map/ppermute | solution.py:20
  10.9 1.5 %copy.29 = bf16[2048,256]{0,1:T(8,128)(2,1)S(1)} copy(bf16[2048,256]{1,0:T(8,128)(2,1)} %param.6) | data formatting | bytes 2097152 | tf_op args[0]
  12.4 2.9 %collective-permute-done.1 = bf16[2,256,128]{2,1,0:T(8,128)(2,1)S(1)} collective-permute-done((bf16[2,256,128]{2,1,0:T(8,128)(2,1)S(1)}, bf16[2,256,128]{2,1,0:T(8,128)(2,1)S(1)}, u32[]{:S(2)}, u32[]{:S(2)}) %collective-permute-start.1) | collective-permute-done | bytes 131104 | tf_op jit(solution)/shard_map/ppermute | solution.py:20
  21.2 3.0 %collective-permute-start.11 = (f32[168,128]{1,0:T(8,128)}, f32[168,128]{1,0:T(8,128)}, u32[]{:S(2)}, u32[]{:S(2)}) collective-permute-start(f32[168,128]{1,0:T(8,128)} %slice.70), channel_id=1, source_target_pairs={{0,1},{1,2},{2,3},{3,4},{4,5},{5,6},{6,7},{8,9},{9,10},{10,11},{11... | collective-permute-start | bytes 258056 | tf_op jit(solution)/shard_map/ppermute | solution.py:15
  24.3 1.3 %bitcast_add_fusion.1 = f32[2,2,256,128]{3,2,0,1:T(8,128)S(1)} fusion(bf16[2,2,256,128]{3,2,0,1:T(8,128)(2,1)} %collective-permute-done.3, f32[2,2,1,256,128]{4,3,2,1,0:T(8,128)} %copy-done.4, f32[2,2,1,256,128]{4,3,2,1,0:T(8,128)} %copy-done.5, pred[]{:T(512)S(6)} %ne.65), kind=kLoop, calls=%fused_computation.18 | loop fusion | flops 393216 | bytes 1835009 | tf_op jit(solution)/shard_map/add | solution.py:46
  27.7 5.3 %collective-permute-done.4 = bf16[2,256,128]{2,1,0:T(8,128)(2,1)S(1)} collective-permute-done((bf16[2,256,128]{2,1,0:T(8,128)(2,1)}, bf16[2,256,128]{2,1,0:T(8,128)(2,1)S(1)}, u32[]{:S(2)}, u32[]{:S(2)}) %collective-permute-start.4) | collective-permute-done | bytes 131104 | tf_op jit(solution)/shard_map/ppermute | solution.py:20
  34.8 2.0 %collective-permute-start.5 = (bf16[256,128]{1,0:T(8,128)(2,1)S(1)}, bf16[256,128]{1,0:T(8,128)(2,1)S(1)}, u32[]{:S(2)}, u32[]{:S(2)}) collective-permute-start(bf16[256,128]{1,0:T(8,128)(2,1)S(1)} %fusion.19), channel_id=1, source_target_pairs={{0,4},{1,5},{2,6},{3,7},{4,0},{5,1},{6,2},{7,3},{8,12},{9,13},{10,... | collective-permute-start | bytes 196616 | tf_op jit(solution)/shard_map/ppermute | solution.py:20
  36.8 1.6 %pad_maximum_fusion.6.extended_ref = f32[424,128]{1,0:T(8,128)} fusion(f32[256,128]{1,0:T(8,128)S(1)} %bitcast.107, f32[168,128]{1,0:T(8,128)} %collective-permute-done.11), kind=kLoop, calls=%fused_computation.36 | loop fusion | flops 54272 | bytes 434176 | tf_op jit(solution)/shard_map/concatenate | solution.py:138
  38.4 2.0 %shard_map.85 = f32[256,128]{1,0:T(8,128)} custom-call(s32[25]{0:T(128)} %broadcast_subtract_fusion.starts_ref, f32[25,128]{1,0:T(8,128)} %weights_ref.7, f32[424,128]{1,0:T(8,128)} %pad_maximum_fusion.6.extended_ref), custom_call_target="tpu_custom_call" | custom-call | flops 1638400 | bytes 360960 | tf_op jit(solution)/shard_map/pallas_call | solution.py:85
  40.7 1.7 %fusion.33 = (bf16[256,128]{1,0:T(8,128)(2,1)S(1)}, f32[256,128]{1,0:T(8,128)}) fusion(f32[256,128]{1,0:T(8,128)S(1)} %copy-done.9, bf16[256,128]{1,0:T(8,128)(2,1)S(1)} %collective-permute-done.5, f32[2,256,128]{2,1,0:T(8,128)} %copy-done.7, pred[]{:T(512)S(6)} %ne.63), kind=kLoop, calls=%fused_computation.91 | loop fusion | flops 196608 | bytes 655361 | tf_op jit(solution)/shard_map/convert_element_type | solution.py:103
  42.4 1.3 %collective-permute-start.6 = (bf16[256,128]{1,0:T(8,128)(2,1)S(1)}, bf16[256,128]{1,0:T(8,128)(2,1)S(1)}, u32[]{:S(2)}, u32[]{:S(2)}) collective-permute-start(bf16[256,128]{1,0:T(8,128)(2,1)S(1)} %get-tuple-element.11), channel_id=1, source_target_pairs={{0,4},{1,5},{2,6},{3,7},{4,0},{5,1},{6,2},{7,3},{8,12},{9,13},{10,... | collective-permute-start | bytes 196616 | tf_op jit(solution)/shard_map/ppermute | solution.py:20
  43.7 1.8 %fusion.37 = f32[128,256]{0,1:T(8,128)S(1)} fusion(bf16[2048,256]{0,1:T(8,128)(2,1)} %copy-done, bf16[2048,128]{1,0:T(8,128)(2,1)} %bitcast.101), kind=kOutput, calls=%fused_computation.94 | convolution fusion | flops 134217728 | bytes 1703936 | tf_op jit(solution)/shard_map/dot_general | solution.py:131
  45.5 1.6 %collective-permute-start.9 = (f32[128,256]{0,1:T(8,128)S(1)}, f32[128,256]{0,1:T(8,128)S(1)}, u32[]{:S(2)}, u32[]{:S(2)}) collective-permute-start(f32[128,256]{0,1:T(8,128)S(1)} %fusion.37), channel_id=1, source_target_pairs={{0,8},{8,0},{16,24},{24,16},{1,9},{9,1},{17,25},{25,17},{2,10},{10... | collective-permute-start | bytes 393224 | tf_op jit(solution)/shard_map/ppermute | solution.py:20
  49.4 1.3 %collective-permute-start.12 = (f32[168,128]{1,0:T(8,128)S(1)}, f32[168,128]{1,0:T(8,128)S(1)}, u32[]{:S(2)}, u32[]{:S(2)}) collective-permute-start(f32[168,128]{1,0:T(8,128)S(1)} %slice.71), channel_id=1, source_target_pairs={{1,0},{2,1},{3,2},{4,3},{5,4},{6,5},{7,6},{9,8},{10,9},{11,10},{12... | collective-permute-start | bytes 258056 | tf_op jit(solution)/shard_map/ppermute | solution.py:15
  50.7 1.6 %collective-permute-start.10 = (f32[128,256]{0,1:T(8,128)S(1)}, f32[128,256]{0,1:T(8,128)}, u32[]{:S(2)}, u32[]{:S(2)}) collective-permute-start(f32[128,256]{0,1:T(8,128)S(1)} %add.60), channel_id=1, source_target_pairs={{0,16},{8,24},{16,0},{24,8},{1,17},{9,25},{17,1},{25,9},{2,18},{10... | collective-permute-start | bytes 393224 | tf_op jit(solution)/shard_map/ppermute | solution.py:20
  55.4 2.0 %shard_map.86 = f32[256,128]{1,0:T(8,128)} custom-call(s32[25]{0:T(128)} %starts_ref.3, f32[25,128]{1,0:T(8,128)} %weights_ref.7, f32[424,128]{1,0:T(8,128)} %pad_maximum_fusion.7.extended_ref), custom_call_target="tpu_custom_call" | custom-call | flops 1638400 | bytes 360960 | tf_op jit(solution)/shard_map/pallas_call | solution.py:85
  64.4 1.9 %collective-permute-start.18 = (f32[168,128]{1,0:T(8,128)S(1)}, f32[168,128]{1,0:T(8,128)S(1)}, u32[]{:S(2)}, u32[]{:S(2)}) collective-permute-start(f32[168,128]{1,0:T(8,128)S(1)} %slice.78), channel_id=1, source_target_pairs={{0,1},{1,2},{2,3},{3,4},{4,5},{5,6},{6,7},{8,9},{9,10},{10,11},{11... | collective-permute-start | bytes 258056 | tf_op jit(solution)/shard_map/ppermute | solution.py:15
  66.3 2.9 %collective-permute-done.14 = bf16[2,256,128]{2,1,0:T(8,128)(2,1)S(1)} collective-permute-done((bf16[2,256,128]{2,1,0:T(8,128)(2,1)S(1)}, bf16[2,256,128]{2,1,0:T(8,128)(2,1)S(1)}, u32[]{:S(2)}, u32[]{:S(2)}) %collective-permute-start.14) | collective-permute-done | bytes 131104 | tf_op jit(solution)/shard_map/ppermute | solution.py:20
  69.9 1.6 %collective-permute-start.15 = (bf16[256,128]{1,0:T(8,128)(2,1)}, bf16[256,128]{1,0:T(8,128)(2,1)}, u32[]{:S(2)}, u32[]{:S(2)}) collective-permute-start(bf16[256,128]{1,0:T(8,128)(2,1)} %fusion.20), channel_id=1, source_target_pairs={{0,4},{1,5},{2,6},{3,7},{4,0},{5,1},{6,2},{7,3},{8,12},{9,13},{10,... | collective-permute-start | bytes 196616 | tf_op jit(solution)/shard_map/ppermute | solution.py:20
  72.1 2.0 %shard_map.87 = f32[256,128]{1,0:T(8,128)} custom-call(s32[25]{0:T(128)} %broadcast_subtract_fusion.starts_ref, f32[25,128]{1,0:T(8,128)} %weights_ref.7, f32[424,128]{1,0:T(8,128)} %pad_maximum_fusion.8.extended_ref), custom_call_target="tpu_custom_call" | custom-call | flops 1638400 | bytes 360960 | tf_op jit(solution)/shard_map/pallas_call | solution.py:85
  74.1 1.9 %collective-permute-done.15 = bf16[256,128]{1,0:T(8,128)(2,1)} collective-permute-done((bf16[256,128]{1,0:T(8,128)(2,1)}, bf16[256,128]{1,0:T(8,128)(2,1)}, u32[]{:S(2)}, u32[]{:S(2)}) %collective-permute-start.15) | collective-permute-done | bytes 65568 | tf_op jit(solution)/shard_map/ppermute | solution.py:20
  76.1 1.6 %fusion.31 = (bf16[256,128]{1,0:T(8,128)(2,1)S(1)}, f32[256,128]{1,0:T(8,128)}) fusion(f32[256,128]{1,0:T(8,128)} %get-tuple-element.12, bf16[256,128]{1,0:T(8,128)(2,1)} %collective-permute-done.15, f32[2,256,128]{2,1,0:T(8,128)S(1)} %bitcast_add_fusion.2, pred[]{:T(512)S(6)} %ne.63), kind=kLoop, calls=%fused_computation.90 | loop fusion | flops 196608 | bytes 655361 | tf_op jit(solution)/shard_map/convert_element_type | solution.py:103
  78.6 1.8 %fusion.38 = f32[128,256]{0,1:T(8,128)S(1)} fusion(bf16[2048,256]{0,1:T(8,128)(2,1)} %copy-done.1, bf16[2048,128]{1,0:T(8,128)(2,1)} %bitcast.103), kind=kOutput, calls=%fused_computation.95 | convolution fusion | flops 134217728 | bytes 1703936 | tf_op jit(solution)/shard_map/dot_general | solution.py:131
  80.4 1.6 %collective-permute-start.16 = (f32[128,256]{0,1:T(8,128)S(1)}, f32[128,256]{0,1:T(8,128)S(1)}, u32[]{:S(2)}, u32[]{:S(2)}) collective-permute-start(f32[128,256]{0,1:T(8,128)S(1)} %fusion.38), channel_id=1, source_target_pairs={{0,8},{8,0},{16,24},{24,16},{1,9},{9,1},{17,25},{25,17},{2,10},{10... | collective-permute-start | bytes 393224 | tf_op jit(solution)/shard_map/ppermute | solution.py:20
  82.0 1.2 %collective-permute-done.20 = bf16[256,128]{1,0:T(8,128)(2,1)S(1)} collective-permute-done((bf16[256,128]{1,0:T(8,128)(2,1)S(1)}, bf16[256,128]{1,0:T(8,128)(2,1)S(1)}, u32[]{:S(2)}, u32[]{:S(2)}) %collective-permute-start.20) | collective-permute-done | bytes 65568 | tf_op jit(solution)/shard_map/ppermute | solution.py:20
  84.1 1.3 %collective-permute-start.19 = (f32[168,128]{1,0:T(8,128)S(1)}, f32[168,128]{1,0:T(8,128)S(1)}, u32[]{:S(2)}, u32[]{:S(2)}) collective-permute-start(f32[168,128]{1,0:T(8,128)S(1)} %slice.79), channel_id=1, source_target_pairs={{1,0},{2,1},{3,2},{4,3},{5,4},{6,5},{7,6},{9,8},{10,9},{11,10},{12... | collective-permute-start | bytes 258056 | tf_op jit(solution)/shard_map/ppermute | solution.py:15
  85.5 1.6 %collective-permute-start.17 = (f32[128,256]{0,1:T(8,128)S(1)}, f32[128,256]{0,1:T(8,128)}, u32[]{:S(2)}, u32[]{:S(2)}) collective-permute-start(f32[128,256]{0,1:T(8,128)S(1)} %add.67), channel_id=1, source_target_pairs={{0,16},{8,24},{16,0},{24,8},{1,17},{9,25},{17,1},{25,9},{2,18},{10... | collective-permute-start | bytes 393224 | tf_op jit(solution)/shard_map/ppermute | solution.py:20
  87.1 1.3 %collective-permute-done.21 = bf16[2,256,128]{2,1,0:T(8,128)(2,1)S(1)} collective-permute-done((bf16[2,256,128]{2,1,0:T(8,128)(2,1)S(1)}, bf16[2,256,128]{2,1,0:T(8,128)(2,1)S(1)}, u32[]{:S(2)}, u32[]{:S(2)}) %collective-permute-start.21) | collective-permute-done | bytes 131104 | tf_op jit(solution)/shard_map/ppermute | solution.py:20
  90.4 2.0 %shard_map.88 = f32[256,128]{1,0:T(8,128)} custom-call(s32[25]{0:T(128)} %starts_ref.3, f32[25,128]{1,0:T(8,128)} %weights_ref.7, f32[424,128]{1,0:T(8,128)} %pad_maximum_fusion.9.extended_ref), custom_call_target="tpu_custom_call" | custom-call | flops 1638400 | bytes 360960 | tf_op jit(solution)/shard_map/pallas_call | solution.py:85
  95.4 1.5 %fusion.9 = bf16[2048,256]{0,1:T(8,128)(2,1)} fusion(f32[2048,256]{0,1:T(8,128)S(1)} %fusion.3, bf16[2048,256]{0,1:T(8,128)(2,1)S(1)} %copy.29, bf16[2048,128]{1,0:T(8,128)(2,1)S(1)} %bitcast.108, f32[128,256]{0,1:T(8,128)S(1)} %bitcast_subtract_fusion), kind=kOutput, calls=%fused_computation.13 | convolution fusion | flops 136347648 | bytes 4849664 | tf_op jit(solution)/shard_map/dot_general | solution.py:116
  96.9 2.3 %copy.46 = bf16[2048,256]{1,0:T(8,128)(2,1)} copy(bf16[2048,256]{0,1:T(8,128)(2,1)} %fusion.9) | data formatting | bytes 2097152
  (122 shorter events, 33.3 us)
Async XLA Ops:
  0.6 14.8 %copy-start.18 = (s32[2048,32]{0,1:T(8,128)S(1)}, s32[2048,32]{0,1:T(8,128)}, u32[]{:S(2)}) copy-start(s32[2048,32]{0,1:T(8,128)} %param.7) | copy-start | bytes 786436
  1.6 7.7 %collective-permute-start = (bf16[256,128]{1,0:T(8,128)(2,1)S(1)}, bf16[256,128]{1,0:T(8,128)(2,1)S(1)}, u32[]{:S(2)}, u32[]{:S(2)}) collective-permute-start(bf16[256,128]{1,0:T(8,128)(2,1)S(1)} %convert_element_type.104), channel_id=1, source_target_pairs={{0,4},{1,5},{2,6},{3,7},{4,0},{5,1},{6,2},{7,3},{8,12},{9,13},{10,... | collective-permute-start | bytes 196616 | tf_op jit(solution)/shard_map/ppermute | solution.py:20
  10.2 5.0 %collective-permute-start.1 = (bf16[2,256,128]{2,1,0:T(8,128)(2,1)S(1)}, bf16[2,256,128]{2,1,0:T(8,128)(2,1)S(1)}, u32[]{:S(2)}, u32[]{:S(2)}) collective-permute-start(bf16[2,256,128]{2,1,0:T(8,128)(2,1)S(1)} %pad_maximum_fusion.10), channel_id=1, source_target_pairs={{0,2},{1,3},{2,0},{3,1},{4,6},{5,7},{6,4},{7,5},{8,10},{9,11},{10,... | collective-permute-start | bytes 393224 | tf_op jit(solution)/shard_map/ppermute | solution.py:20
  15.3 1.6 %collective-permute-start.2 = (bf16[2,2,256,128]{3,2,1,0:T(8,128)(2,1)S(1)}, bf16[2,2,256,128]{3,2,1,0:T(8,128)(2,1)S(1)}, u32[]{:S(2)}, u32[]{:S(2)}) collective-permute-start(bf16[2,2,256,128]{3,2,1,0:T(8,128)(2,1)S(1)} %pad_maximum_fusion.3), channel_id=1, source_target_pairs={{0,1},{1,0},{2,3},{3,2},{4,5},{5,4},{6,7},{7,6},{8,9},{9,8},{10,11... | collective-permute-start | bytes 786440 | tf_op jit(solution)/shard_map/ppermute | solution.py:20
  15.4 1.6 %copy-start.8 = (f32[128,256]{1,0:T(8,128)S(1)}, f32[128,256]{1,0:T(8,128)}, u32[]{:S(2)}) copy-start(f32[128,256]{1,0:T(8,128)} %param.9) | copy-start | bytes 393220
  18.8 1.5 %copy-start.5 = (f32[2,2,1,256,128]{4,3,2,1,0:T(8,128)}, f32[2,2,1,256,128]{4,3,2,1,0:T(8,128)S(1)}, u32[]{:S(2)}) copy-start(f32[2,2,1,256,128]{4,3,2,1,0:T(8,128)S(1)} %get-tuple-element.16) | copy-start | bytes 1572868
  18.8 8.3 %copy-start.19 = (s32[25]{0:T(128)S(1)}, s32[25]{0:T(128)}, u32[]{:S(2)}) copy-start(s32[25]{0:T(128)} %starts_ref.3) | copy-start | bytes 304
  20.3 3.9 %collective-permute-start.3 = (bf16[2,2,256,128]{3,2,0,1:T(8,128)(2,1)}, bf16[2,2,256,128]{3,2,0,1:T(8,128)(2,1)}, u32[]{:S(2)}, u32[]{:S(2)}) collective-permute-start(bf16[2,2,256,128]{3,2,0,1:T(8,128)(2,1)} %fusion.10), channel_id=1, source_target_pairs={{0,1},{1,0},{2,3},{3,2},{4,5},{5,4},{6,7},{7,6},{8,9},{9,8},{10,11... | collective-permute-start | bytes 786440 | tf_op jit(solution)/shard_map/ppermute | solution.py:20
  21.2 19.5 %copy-start.9 = (f32[256,128]{1,0:T(8,128)S(1)}, f32[256,128]{1,0:T(8,128)}, u32[]{:S(2)}) copy-start(f32[256,128]{1,0:T(8,128)} %param.8) | copy-start | bytes 393220
  21.2 15.6 %collective-permute-start.11 = (f32[168,128]{1,0:T(8,128)}, f32[168,128]{1,0:T(8,128)}, u32[]{:S(2)}, u32[]{:S(2)}) collective-permute-start(f32[168,128]{1,0:T(8,128)} %slice.70), channel_id=1, source_target_pairs={{0,1},{1,2},{2,3},{3,4},{4,5},{5,6},{6,7},{8,9},{9,10},{10,11},{11... | collective-permute-start | bytes 258056 | tf_op jit(solution)/shard_map/ppermute | solution.py:15
  27.1 5.9 %collective-permute-start.4 = (bf16[2,256,128]{2,1,0:T(8,128)(2,1)}, bf16[2,256,128]{2,1,0:T(8,128)(2,1)S(1)}, u32[]{:S(2)}, u32[]{:S(2)}) collective-permute-start(bf16[2,256,128]{2,1,0:T(8,128)(2,1)} %fusion.12), channel_id=1, source_target_pairs={{0,2},{1,3},{2,0},{3,1},{4,6},{5,7},{6,4},{7,5},{8,10},{9,11},{10,... | collective-permute-start | bytes 393224 | tf_op jit(solution)/shard_map/ppermute | solution.py:20
  34.8 6.0 %collective-permute-start.5 = (bf16[256,128]{1,0:T(8,128)(2,1)S(1)}, bf16[256,128]{1,0:T(8,128)(2,1)S(1)}, u32[]{:S(2)}, u32[]{:S(2)}) collective-permute-start(bf16[256,128]{1,0:T(8,128)(2,1)S(1)} %fusion.19), channel_id=1, source_target_pairs={{0,4},{1,5},{2,6},{3,7},{4,0},{5,1},{6,2},{7,3},{8,12},{9,13},{10,... | collective-permute-start | bytes 196616 | tf_op jit(solution)/shard_map/ppermute | solution.py:20
  40.3 8.9 %copy-start.16 = (f32[256,128]{1,0:T(8,128)S(1)}, f32[256,128]{1,0:T(8,128)}, u32[]{:S(2)}) copy-start(f32[256,128]{1,0:T(8,128)} %shard_map.85) | copy-start | bytes 393220
  42.4 5.9 %collective-permute-start.6 = (bf16[256,128]{1,0:T(8,128)(2,1)S(1)}, bf16[256,128]{1,0:T(8,128)(2,1)S(1)}, u32[]{:S(2)}, u32[]{:S(2)}) collective-permute-start(bf16[256,128]{1,0:T(8,128)(2,1)S(1)} %get-tuple-element.11), channel_id=1, source_target_pairs={{0,4},{1,5},{2,6},{3,7},{4,0},{5,1},{6,2},{7,3},{8,12},{9,13},{10,... | collective-permute-start | bytes 196616 | tf_op jit(solution)/shard_map/ppermute | solution.py:20
  45.5 5.2 %collective-permute-start.9 = (f32[128,256]{0,1:T(8,128)S(1)}, f32[128,256]{0,1:T(8,128)S(1)}, u32[]{:S(2)}, u32[]{:S(2)}) collective-permute-start(f32[128,256]{0,1:T(8,128)S(1)} %fusion.37), channel_id=1, source_target_pairs={{0,8},{8,0},{16,24},{24,16},{1,9},{9,1},{17,25},{25,17},{2,10},{10... | collective-permute-start | bytes 393224 | tf_op jit(solution)/shard_map/ppermute | solution.py:20
  48.3 5.0 %collective-permute-start.7 = (bf16[2,256,128]{2,1,0:T(8,128)(2,1)S(1)}, bf16[2,256,128]{2,1,0:T(8,128)(2,1)S(1)}, u32[]{:S(2)}, u32[]{:S(2)}) collective-permute-start(bf16[2,256,128]{2,1,0:T(8,128)(2,1)S(1)} %pad_maximum_fusion.11), channel_id=1, source_target_pairs={{0,2},{1,3},{2,0},{3,1},{4,6},{5,7},{6,4},{7,5},{8,10},{9,11},{10,... | collective-permute-start | bytes 393224 | tf_op jit(solution)/shard_map/ppermute | solution.py:20
  49.4 5.4 %collective-permute-start.12 = (f32[168,128]{1,0:T(8,128)S(1)}, f32[168,128]{1,0:T(8,128)S(1)}, u32[]{:S(2)}, u32[]{:S(2)}) collective-permute-start(f32[168,128]{1,0:T(8,128)S(1)} %slice.71), channel_id=1, source_target_pairs={{1,0},{2,1},{3,2},{4,3},{5,4},{6,5},{7,6},{9,8},{10,9},{11,10},{12... | collective-permute-start | bytes 258056 | tf_op jit(solution)/shard_map/ppermute | solution.py:15
  50.7 6.7 %copy-start.17 = (f32[128,256]{0,1:T(8,128)}, f32[128,256]{0,1:T(8,128)S(1)}, u32[]{:S(2)}) copy-start(f32[128,256]{0,1:T(8,128)S(1)} %add.60) | copy-start | bytes 393220
  50.7 6.7 %collective-permute-start.10 = (f32[128,256]{0,1:T(8,128)S(1)}, f32[128,256]{0,1:T(8,128)}, u32[]{:S(2)}, u32[]{:S(2)}) collective-permute-start(f32[128,256]{0,1:T(8,128)S(1)} %add.60), channel_id=1, source_target_pairs={{0,16},{8,24},{16,0},{24,8},{1,17},{9,25},{17,1},{25,9},{2,18},{10... | collective-permute-start | bytes 393224 | tf_op jit(solution)/shard_map/ppermute | solution.py:20
  54.7 3.7 %collective-permute-start.8 = (bf16[2,2,256,128]{3,2,0,1:T(8,128)(2,1)}, bf16[2,2,256,128]{3,2,0,1:T(8,128)(2,1)}, u32[]{:S(2)}, u32[]{:S(2)}) collective-permute-start(bf16[2,2,256,128]{3,2,0,1:T(8,128)(2,1)} %pad_maximum_fusion.4), channel_id=1, source_target_pairs={{0,1},{1,0},{2,3},{3,2},{4,5},{5,4},{6,7},{7,6},{8,9},{9,8},{10,11... | collective-permute-start | bytes 786440 | tf_op jit(solution)/shard_map/ppermute | solution.py:20
  61.5 1.7 %collective-permute-start.13 = (bf16[2,2,256,128]{3,2,0,1:T(8,128)(2,1)S(1)}, bf16[2,2,256,128]{3,2,0,1:T(8,128)(2,1)S(1)}, u32[]{:S(2)}, u32[]{:S(2)}) collective-permute-start(bf16[2,2,256,128]{3,2,0,1:T(8,128)(2,1)S(1)} %fusion.11), channel_id=1, source_target_pairs={{0,1},{1,0},{2,3},{3,2},{4,5},{5,4},{6,7},{7,6},{8,9},{9,8},{10,11... | collective-permute-start | bytes 786440 | tf_op jit(solution)/shard_map/ppermute | solution.py:20
  63.3 5.8 %collective-permute-start.14 = (bf16[2,256,128]{2,1,0:T(8,128)(2,1)S(1)}, bf16[2,256,128]{2,1,0:T(8,128)(2,1)S(1)}, u32[]{:S(2)}, u32[]{:S(2)}) collective-permute-start(bf16[2,256,128]{2,1,0:T(8,128)(2,1)S(1)} %fusion.13), channel_id=1, source_target_pairs={{0,2},{1,3},{2,0},{3,1},{4,6},{5,7},{6,4},{7,5},{8,10},{9,11},{10,... | collective-permute-start | bytes 393224 | tf_op jit(solution)/shard_map/ppermute | solution.py:20
  64.4 7.0 %collective-permute-start.18 = (f32[168,128]{1,0:T(8,128)S(1)}, f32[168,128]{1,0:T(8,128)S(1)}, u32[]{:S(2)}, u32[]{:S(2)}) collective-permute-start(f32[168,128]{1,0:T(8,128)S(1)} %slice.78), channel_id=1, source_target_pairs={{0,1},{1,2},{2,3},{3,4},{4,5},{5,6},{6,7},{8,9},{9,10},{10,11},{11... | collective-permute-start | bytes 258056 | tf_op jit(solution)/shard_map/ppermute | solution.py:15
  69.9 6.2 %collective-permute-start.15 = (bf16[256,128]{1,0:T(8,128)(2,1)}, bf16[256,128]{1,0:T(8,128)(2,1)}, u32[]{:S(2)}, u32[]{:S(2)}) collective-permute-start(bf16[256,128]{1,0:T(8,128)(2,1)} %fusion.20), channel_id=1, source_target_pairs={{0,4},{1,5},{2,6},{3,7},{4,0},{5,1},{6,2},{7,3},{8,12},{9,13},{10,... | collective-permute-start | bytes 196616 | tf_op jit(solution)/shard_map/ppermute | solution.py:20
  74.1 9.9 %copy-start.14 = (f32[256,128]{1,0:T(8,128)S(1)}, f32[256,128]{1,0:T(8,128)}, u32[]{:S(2)}) copy-start(f32[256,128]{1,0:T(8,128)} %shard_map.87) | copy-start | bytes 393220
  77.7 5.6 %collective-permute-start.20 = (bf16[256,128]{1,0:T(8,128)(2,1)S(1)}, bf16[256,128]{1,0:T(8,128)(2,1)S(1)}, u32[]{:S(2)}, u32[]{:S(2)}) collective-permute-start(bf16[256,128]{1,0:T(8,128)(2,1)S(1)} %get-tuple-element.9), channel_id=1, source_target_pairs={{0,4},{1,5},{2,6},{3,7},{4,0},{5,1},{6,2},{7,3},{8,12},{9,13},{10,... | collective-permute-start | bytes 196616 | tf_op jit(solution)/shard_map/ppermute | solution.py:20
  80.4 5.0 %collective-permute-start.16 = (f32[128,256]{0,1:T(8,128)S(1)}, f32[128,256]{0,1:T(8,128)S(1)}, u32[]{:S(2)}, u32[]{:S(2)}) collective-permute-start(f32[128,256]{0,1:T(8,128)S(1)} %fusion.38), channel_id=1, source_target_pairs={{0,8},{8,0},{16,24},{24,16},{1,9},{9,1},{17,25},{25,17},{2,10},{10... | collective-permute-start | bytes 393224 | tf_op jit(solution)/shard_map/ppermute | solution.py:20
  83.3 5.0 %collective-permute-start.21 = (bf16[2,256,128]{2,1,0:T(8,128)(2,1)S(1)}, bf16[2,256,128]{2,1,0:T(8,128)(2,1)S(1)}, u32[]{:S(2)}, u32[]{:S(2)}) collective-permute-start(bf16[2,256,128]{2,1,0:T(8,128)(2,1)S(1)} %pad_maximum_fusion.12), channel_id=1, source_target_pairs={{0,2},{1,3},{2,0},{3,1},{4,6},{5,7},{6,4},{7,5},{8,10},{9,11},{10,... | collective-permute-start | bytes 393224 | tf_op jit(solution)/shard_map/ppermute | solution.py:20
  84.1 5.6 %collective-permute-start.19 = (f32[168,128]{1,0:T(8,128)S(1)}, f32[168,128]{1,0:T(8,128)S(1)}, u32[]{:S(2)}, u32[]{:S(2)}) collective-permute-start(f32[168,128]{1,0:T(8,128)S(1)} %slice.79), channel_id=1, source_target_pairs={{1,0},{2,1},{3,2},{4,3},{5,4},{6,5},{7,6},{9,8},{10,9},{11,10},{12... | collective-permute-start | bytes 258056 | tf_op jit(solution)/shard_map/ppermute | solution.py:15
  85.5 6.9 %copy-start.15 = (f32[128,256]{0,1:T(8,128)}, f32[128,256]{0,1:T(8,128)S(1)}, u32[]{:S(2)}) copy-start(f32[128,256]{0,1:T(8,128)S(1)} %add.67) | copy-start | bytes 393220
  85.5 6.9 %collective-permute-start.17 = (f32[128,256]{0,1:T(8,128)S(1)}, f32[128,256]{0,1:T(8,128)}, u32[]{:S(2)}, u32[]{:S(2)}) collective-permute-start(f32[128,256]{0,1:T(8,128)S(1)} %add.67), channel_id=1, source_target_pairs={{0,16},{8,24},{16,0},{24,8},{1,17},{9,25},{17,1},{25,9},{2,18},{10... | collective-permute-start | bytes 393224 | tf_op jit(solution)/shard_map/ppermute | solution.py:20
  89.7 4.5 %collective-permute-start.22 = (bf16[2,2,256,128]{3,2,0,1:T(8,128)(2,1)}, bf16[2,2,256,128]{3,2,0,1:T(8,128)(2,1)}, u32[]{:S(2)}, u32[]{:S(2)}) collective-permute-start(bf16[2,2,256,128]{3,2,0,1:T(8,128)(2,1)} %pad_maximum_fusion.5), channel_id=1, source_target_pairs={{0,1},{1,0},{2,3},{3,2},{4,5},{5,4},{6,7},{7,6},{8,9},{9,8},{10,11... | collective-permute-start | bytes 786440 | tf_op jit(solution)/shard_map/ppermute | solution.py:20
  (11 other events, 9.9 us)

commit v3 on v2

--- a/solution.py
+++ b/solution.py
@@ -71,17 +71,19 @@
     return (jnp.right_shift(repeated, hour % 8) & 1).astype(jnp.float32)
 
 
-def lag_kernel(starts_ref, weights_ref, extended_ref, out_ref):
-    width = out_ref.shape[0]
+def lag_kernel(starts_ref, weights_ref, first_ref, second_ref, out_ref, window_ref):
+    width, lead = out_ref.shape[0], first_ref.shape[0]
+    window_ref[pl.ds(0, lead), :] = first_ref[...]
+    window_ref[pl.ds(lead, second_ref.shape[0]), :] = second_ref[...]
     running = jnp.zeros(out_ref.shape, jnp.float32)
     for k in range(weights_ref.shape[0]):
-        row_block = extended_ref[pl.ds(starts_ref[k], width), :]
+        row_block = window_ref[pl.ds(starts_ref[k], width), :]
         running = running + weights_ref[pl.ds(k, 1), :] * row_block
     out_ref[...] = running
 
 
-def lagged_sum(extended, weights, starts, width):
-    rank = extended.shape[1]
+def lagged_sum(first, second, weights, starts, width):
+    rows, rank = first.shape[0] + second.shape[0], first.shape[1]
     return pl.pallas_call(
         lag_kernel,
         out_shape=jax.ShapeDtypeStruct((width, rank), jnp.float32),
@@ -89,14 +91,16 @@
             pl.BlockSpec(memory_space=pltpu.SMEM),
             pl.BlockSpec(memory_space=pltpu.VMEM),
             pl.BlockSpec(memory_space=pltpu.VMEM),
+            pl.BlockSpec(memory_space=pltpu.VMEM),
         ],
         out_specs=pl.BlockSpec(memory_space=pltpu.VMEM),
+        scratch_shapes=[pltpu.VMEM((rows, rank), jnp.float32)],
         cost_estimate=pl.CostEstimate(
             flops=2 * weights.shape[0] * width * rank,
             transcendentals=0,
-            bytes_accessed=4 * (extended.size + weights.size + width * rank),
+            bytes_accessed=4 * (rows * rank + weights.size + width * rank),
         ),
-    )(starts.astype(jnp.int32), weights, extended)
+    )(starts.astype(jnp.int32), weights, first, second)
 
 
 def fetch_rows(factors):
@@ -134,14 +138,10 @@
         grad_times = butterfly_sum(partial_value, "series")
         times_t = times.T
         tail_rows = shifted(times_t[hours - MAXLAG :], "tm", 1)
-        errors = times_t - lagged_sum(
-            jnp.concatenate([tail_rows, times_t], 0), ar_weights, MAXLAG - lags, hours
-        )
+        errors = times_t - lagged_sum(tail_rows, times_t, ar_weights, MAXLAG - lags, hours)
         errors = jnp.where(active_rows, errors, 0.0)
         head_rows = shifted(errors[:MAXLAG], "tm", -1)
-        ar_grad = (errors - lagged_sum(
-            jnp.concatenate([errors, head_rows], 0), ar_weights, lags, hours
-        )).T
+        ar_grad = (errors - lagged_sum(errors, head_rows, ar_weights, lags, hours)).T
         times_new = times - 24.0 / total_series * grad_times - 0.25 * ar_grad
         factors = factors - 2.0 / total_hours * grad_rows
         times = times_new

time: 99.8 us -> 97.5 us (0.977)
  other arithmetic: 20.4 us -> 16.9 us
  starting transfers between devices: 27.9 us -> 30 us
  local copies, waits for them, and re-layouts: 10.5 us -> 9.08 us
    concatenate x4 -> x0, other arithmetic: 3.68 us -> none  [the longest x2 2.29 us: local(): jnp.concatenate([tail_rows, times_t], 0)]
    ppermute x19, starting transfers between devices: 20.4 us -> 22.3 us  [exchange(): return lax.ppermute(block, axis, [(i, i ^ bit) for i in range(devices)])]
    unnamed x44 -> x40, local copies, waits for them, and re-layouts: 9.62 us -> 8.17 us
    add x2, other arithmetic: 0.03 us -> 1.33 us  [butterfly_sum(): block = block + exchange(block, axis, bit)]
    add x4, other arithmetic: 2.52 us -> 1.49 us  [halving_sum(): block = keep + exchange(send, axis, bit).astype(jnp.float32)]
  transfers between devices with their start and end apart: 23 -> 23, of which waited for: 12 -> 12; matrix products, arithmetic and copies ran while one was open for 19% -> 17% of each run, Pallas kernels for 8% -> 8%
where the time goes in v3:
time: 97.5 us; the launch traced here: 96.9 us
  starting transfers between devices  30 us (31%)
  waiting for transfers between devices  23.6 us (24%)
  other arithmetic  16.9 us (17%)
  local copies, waits for them, and re-layouts  9.08 us (9%)
  matrix products  8.42 us (9%)
  Pallas kernels  7.81 us (8%)
  between operations  1.08 us (1%)
    ppermute x19, waiting for transfers between devices, exchange(): return lax.ppermute(block, axis, [(i, i ^ bit) for i in range(devices)])  23.6 us
    ppermute x19, starting transfers between devices, exchange(): return lax.ppermute(block, axis, [(i, i ^ bit) for i in range(devices)])  22.3 us
    unnamed x40, local copies, waits for them, and re-layouts  8.17 us
    pallas_call x4, Pallas kernels, lagged_sum(): pl.pallas_call(lag_kernel, out_shape=jax.ShapeDtypeStruct((width, rank),...  7.81 us
    ppermute x4, starting transfers between devices, shifted(): return lax.ppermute(block, axis, route)  7.69 us
    another operation x18, other arithmetic, doubling_gather(): block = jnp.stack([low, high], axis=step)  4.83 us
    convert_element_type x3, other arithmetic, fetch_rows(): return doubling_gather(factors.astype(jnp.bfloat16), 'tm')  4.1 us
    dot_general x2, matrix products, local(): lax.dot_general(rows_low, misfit, (((0,), (0,)), ((), ())), preferred_ele...  3.57 us
  transfers between devices with their start and end apart: 23, of which 12 were waited for; matrix products, arithmetic and copies ran while one was open for 17% of the time, Pallas kernels for 8%

profile of v3, /device:TPU:0, one launch (start us, length us, event | category | flops | bytes accessed | tf_op | source)
XLA Modules:
  0.0 96.9 jit_solution(16138335623933392464)
XLA Ops:
  1.5 4.0 %collective-permute-start = (bf16[256,128]{1,0:T(8,128)(2,1)S(1)}, bf16[256,128]{1,0:T(8,128)(2,1)S(1)}, u32[]{:S(2)}, u32[]{:S(2)}) collective-permute-start(bf16[256,128]{1,0:T(8,128)(2,1)S(1)} %convert_element_type.104), channel_id=1, source_target_pairs={{0,4},{1,5},{2,6},{3,7},{4,0},{5,1},{6,2},{7,3},{8,12},{9,13},{10,... | collective-permute-start | bytes 196616 | tf_op jit(solution)/shard_map/ppermute | solution.py:20
  5.6 3.6 %collective-permute-done = bf16[256,128]{1,0:T(8,128)(2,1)S(1)} collective-permute-done((bf16[256,128]{1,0:T(8,128)(2,1)S(1)}, bf16[256,128]{1,0:T(8,128)(2,1)S(1)}, u32[]{:S(2)}, u32[]{:S(2)}) %collective-permute-start) | collective-permute-done | bytes 65568 | tf_op jit(solution)/shard_map/ppermute | solution.py:20
  10.8 1.5 %copy.29 = bf16[2048,256]{0,1:T(8,128)(2,1)S(1)} copy(bf16[2048,256]{1,0:T(8,128)(2,1)} %param.6) | data formatting | bytes 2097152 | tf_op args[0]
  12.3 2.9 %collective-permute-done.1 = bf16[2,256,128]{2,1,0:T(8,128)(2,1)S(1)} collective-permute-done((bf16[2,256,128]{2,1,0:T(8,128)(2,1)S(1)}, bf16[2,256,128]{2,1,0:T(8,128)(2,1)S(1)}, u32[]{:S(2)}, u32[]{:S(2)}) %collective-permute-start.1) | collective-permute-done | bytes 131104 | tf_op jit(solution)/shard_map/ppermute | solution.py:20
  15.4 1.5 %fusion.3 = f32[2048,256]{0,1:T(8,128)S(1)} fusion(s32[256]{0:T(256)S(1)} %get-tuple-element.35, s32[2048,32]{0,1:T(8,128)} %param.7, s32[256]{0:T(256)S(1)} %get-tuple-element.36), kind=kOutput, calls=%fused_computation.7 | convolution fusion | flops 35725312 | bytes 2361344 | tf_op jit(solution)/shard_map/dot_general | solution.py:68
  21.6 2.6 %collective-permute-start.11 = (f32[168,128]{1,0:T(8,128)}, f32[168,128]{1,0:T(8,128)}, u32[]{:S(2)}, u32[]{:S(2)}) collective-permute-start(f32[168,128]{1,0:T(8,128)} %slice.70), channel_id=1, source_target_pairs={{0,1},{1,2},{2,3},{3,4},{4,5},{5,6},{6,7},{8,9},{9,10},{10,11},{11... | collective-permute-start | bytes 258056 | tf_op jit(solution)/shard_map/ppermute | solution.py:15
  24.2 1.3 %bitcast_add_fusion.1 = f32[2,2,256,128]{3,2,0,1:T(8,128)S(1)} fusion(bf16[2,2,256,128]{3,2,0,1:T(8,128)(2,1)} %collective-permute-done.3, f32[2,2,1,256,128]{4,3,2,1,0:T(8,128)} %copy-done.6, f32[2,2,1,256,128]{4,3,2,1,0:T(8,128)} %copy-done.7, pred[]{:T(512)S(6)} %ne.65), kind=kLoop, calls=%fused_computation.18 | loop fusion | flops 393216 | bytes 1835009 | tf_op jit(solution)/shard_map/add | solution.py:46
  26.2 5.4 %collective-permute-done.4 = bf16[2,256,128]{2,1,0:T(8,128)(2,1)S(1)} collective-permute-done((bf16[2,256,128]{2,1,0:T(8,128)(2,1)S(1)}, bf16[2,256,128]{2,1,0:T(8,128)(2,1)S(1)}, u32[]{:S(2)}, u32[]{:S(2)}) %collective-permute-start.4) | collective-permute-done | bytes 131104 | tf_op jit(solution)/shard_map/ppermute | solution.py:20
  33.5 2.0 %shard_map.85 = f32[256,128]{1,0:T(8,128)} custom-call(s32[25]{0:T(128)} %broadcast_subtract_fusion.starts_ref, f32[25,128]{1,0:T(8,128)} %weights_ref.7, f32[168,128]{1,0:T(8,128)} %collective-permute-done.11.first_ref, f32[256,128]{1,0:T(8,128)} %bitcast.107), custom_call_target="tpu_custom_call" | custom-call | flops 1638400 | bytes 360960 | tf_op jit(solution)/shard_map/pallas_call | solution.py:87
  35.5 3.0 %collective-permute-done.5 = bf16[256,128]{1,0:T(8,128)(2,1)} collective-permute-done((bf16[256,128]{1,0:T(8,128)(2,1)}, bf16[256,128]{1,0:T(8,128)(2,1)}, u32[]{:S(2)}, u32[]{:S(2)}) %collective-permute-start.5) | collective-permute-done | bytes 65568 | tf_op jit(solution)/shard_map/ppermute | solution.py:20
  38.5 1.6 %fusion.33 = (bf16[256,128]{1,0:T(8,128)(2,1)S(1)}, f32[256,128]{1,0:T(8,128)}) fusion(f32[256,128]{1,0:T(8,128)} %param.8, bf16[256,128]{1,0:T(8,128)(2,1)} %collective-permute-done.5, f32[2,256,128]{2,1,0:T(8,128)S(1)} %bitcast_add_fusion.3, pred[]{:T(512)S(6)} %ne.63), kind=kLoop, calls=%fused_computation.87 | loop fusion | flops 196608 | bytes 655361 | tf_op jit(solution)/shard_map/convert_element_type | solution.py:107
  41.1 1.8 %fusion.37 = f32[128,256]{0,1:T(8,128)S(1)} fusion(bf16[2048,256]{0,1:T(8,128)(2,1)} %copy-done, bf16[2048,128]{1,0:T(8,128)(2,1)} %bitcast.101), kind=kOutput, calls=%fused_computation.90 | convolution fusion | flops 134217728 | bytes 1703936 | tf_op jit(solution)/shard_map/dot_general | solution.py:135
  42.9 1.6 %collective-permute-start.9 = (f32[128,256]{0,1:T(8,128)S(1)}, f32[128,256]{0,1:T(8,128)S(1)}, u32[]{:S(2)}, u32[]{:S(2)}) collective-permute-start(f32[128,256]{0,1:T(8,128)S(1)} %fusion.37), channel_id=1, source_target_pairs={{0,8},{8,0},{16,24},{24,16},{1,9},{9,1},{17,25},{25,17},{2,10},{10... | collective-permute-start | bytes 393224 | tf_op jit(solution)/shard_map/ppermute | solution.py:20
  46.9 1.3 %collective-permute-start.12 = (f32[168,128]{1,0:T(8,128)S(1)}, f32[168,128]{1,0:T(8,128)}, u32[]{:S(2)}, u32[]{:S(2)}) collective-permute-start(f32[168,128]{1,0:T(8,128)S(1)} %slice.71), channel_id=1, source_target_pairs={{1,0},{2,1},{3,2},{4,3},{5,4},{6,5},{7,6},{9,8},{10,9},{11,10},{12... | collective-permute-start | bytes 258056 | tf_op jit(solution)/shard_map/ppermute | solution.py:15
  48.9 1.5 %collective-permute-start.10 = (f32[128,256]{0,1:T(8,128)}, f32[128,256]{0,1:T(8,128)}, u32[]{:S(2)}, u32[]{:S(2)}) collective-permute-start(f32[128,256]{0,1:T(8,128)} %add.60), channel_id=1, source_target_pairs={{0,16},{8,24},{16,0},{24,8},{1,17},{9,25},{17,1},{25,9},{2,18},{10... | collective-permute-start | bytes 393224 | tf_op jit(solution)/shard_map/ppermute | solution.py:20
  52.6 2.0 %shard_map.86 = f32[256,128]{1,0:T(8,128)} custom-call(s32[25]{0:T(128)} %starts_ref.3, f32[25,128]{1,0:T(8,128)} %weights_ref.7, f32[256,128]{1,0:T(8,128)} %copy-done.11, f32[168,128]{1,0:T(8,128)} %collective-permute-done.12.second_ref), custom_call_target="tpu_custom_call" | custom-call | flops 1638400 | bytes 360960 | tf_op jit(solution)/shard_map/pallas_call | solution.py:87
  59.7 1.4 %collective-permute-done.13 = bf16[2,2,256,128]{3,2,0,1:T(8,128)(2,1)S(1)} collective-permute-done((bf16[2,2,256,128]{3,2,0,1:T(8,128)(2,1)S(1)}, bf16[2,2,256,128]{3,2,0,1:T(8,128)(2,1)S(1)}, u32[]{:S(2)}, u32[]{:S(2)}) %collective-permute-start.13) | collective-permute-done | bytes 262176 | tf_op jit(solution)/shard_map/ppermute | solution.py:20
  61.2 1.4 %collective-permute-start.14 = (bf16[2,256,128]{2,1,0:T(8,128)(2,1)S(1)}, bf16[2,256,128]{2,1,0:T(8,128)(2,1)S(1)}, u32[]{:S(2)}, u32[]{:S(2)}) collective-permute-start(bf16[2,256,128]{2,1,0:T(8,128)(2,1)S(1)} %fusion.13), channel_id=1, source_target_pairs={{0,2},{1,3},{2,0},{3,1},{4,6},{5,7},{6,4},{7,5},{8,10},{9,11},{10,... | collective-permute-start | bytes 393224 | tf_op jit(solution)/shard_map/ppermute | solution.py:20
  62.7 2.5 %collective-permute-start.18 = (f32[168,128]{1,0:T(8,128)S(1)}, f32[168,128]{1,0:T(8,128)}, u32[]{:S(2)}, u32[]{:S(2)}) collective-permute-start(f32[168,128]{1,0:T(8,128)S(1)} %slice.78), channel_id=1, source_target_pairs={{0,1},{1,2},{2,3},{3,4},{4,5},{5,6},{6,7},{8,9},{9,10},{10,11},{11... | collective-permute-start | bytes 258056 | tf_op jit(solution)/shard_map/ppermute | solution.py:15
  65.3 1.6 %collective-permute-done.14 = bf16[2,256,128]{2,1,0:T(8,128)(2,1)S(1)} collective-permute-done((bf16[2,256,128]{2,1,0:T(8,128)(2,1)S(1)}, bf16[2,256,128]{2,1,0:T(8,128)(2,1)S(1)}, u32[]{:S(2)}, u32[]{:S(2)}) %collective-permute-start.14) | collective-permute-done | bytes 131104 | tf_op jit(solution)/shard_map/ppermute | solution.py:20
  67.5 2.3 %collective-permute-start.15 = (bf16[256,128]{1,0:T(8,128)(2,1)}, bf16[256,128]{1,0:T(8,128)(2,1)}, u32[]{:S(2)}, u32[]{:S(2)}) collective-permute-start(bf16[256,128]{1,0:T(8,128)(2,1)} %fusion.20), channel_id=1, source_target_pairs={{0,4},{1,5},{2,6},{3,7},{4,0},{5,1},{6,2},{7,3},{8,12},{9,13},{10,... | collective-permute-start | bytes 196616 | tf_op jit(solution)/shard_map/ppermute | solution.py:20
  69.8 1.9 %shard_map.87 = f32[256,128]{1,0:T(8,128)} custom-call(s32[25]{0:T(128)} %broadcast_subtract_fusion.starts_ref, f32[25,128]{1,0:T(8,128)} %weights_ref.7, f32[168,128]{1,0:T(8,128)} %collective-permute-done.18.first_ref, f32[256,128]{1,0:T(8,128)} %bitcast.99), custom_call_target="tpu_custom_call" | custom-call | flops 1638400 | bytes 360960 | tf_op jit(solution)/shard_map/pallas_call | solution.py:87
  71.8 1.3 %collective-permute-done.15 = bf16[256,128]{1,0:T(8,128)(2,1)} collective-permute-done((bf16[256,128]{1,0:T(8,128)(2,1)}, bf16[256,128]{1,0:T(8,128)(2,1)}, u32[]{:S(2)}, u32[]{:S(2)}) %collective-permute-start.15) | collective-permute-done | bytes 65568 | tf_op jit(solution)/shard_map/ppermute | solution.py:20
  73.0 1.6 %fusion.31 = (bf16[256,128]{1,0:T(8,128)(2,1)S(1)}, f32[256,128]{1,0:T(8,128)}) fusion(f32[256,128]{1,0:T(8,128)} %get-tuple-element.12, bf16[256,128]{1,0:T(8,128)(2,1)} %collective-permute-done.15, f32[2,256,128]{2,1,0:T(8,128)S(1)} %bitcast_add_fusion.2, pred[]{:T(512)S(6)} %ne.63), kind=kLoop, calls=%fused_computation.86 | loop fusion | flops 196608 | bytes 655361 | tf_op jit(solution)/shard_map/convert_element_type | solution.py:107
  74.6 2.3 %collective-permute-start.20 = (bf16[256,128]{1,0:T(8,128)(2,1)S(1)}, bf16[256,128]{1,0:T(8,128)(2,1)S(1)}, u32[]{:S(2)}, u32[]{:S(2)}) collective-permute-start(bf16[256,128]{1,0:T(8,128)(2,1)S(1)} %get-tuple-element.9), channel_id=1, source_target_pairs={{0,4},{1,5},{2,6},{3,7},{4,0},{5,1},{6,2},{7,3},{8,12},{9,13},{10,... | collective-permute-start | bytes 196616 | tf_op jit(solution)/shard_map/ppermute | solution.py:20
  76.9 1.8 %fusion.38 = f32[128,256]{0,1:T(8,128)S(1)} fusion(bf16[2048,256]{0,1:T(8,128)(2,1)} %copy-done.1, bf16[2048,128]{1,0:T(8,128)(2,1)} %bitcast.103), kind=kOutput, calls=%fused_computation.91 | convolution fusion | flops 134217728 | bytes 1703936 | tf_op jit(solution)/shard_map/dot_general | solution.py:135
  78.7 1.6 %collective-permute-start.16 = (f32[128,256]{0,1:T(8,128)S(1)}, f32[128,256]{0,1:T(8,128)S(1)}, u32[]{:S(2)}, u32[]{:S(2)}) collective-permute-start(f32[128,256]{0,1:T(8,128)S(1)} %fusion.38), channel_id=1, source_target_pairs={{0,8},{8,0},{16,24},{24,16},{1,9},{9,1},{17,25},{25,17},{2,10},{10... | collective-permute-start | bytes 393224 | tf_op jit(solution)/shard_map/ppermute | solution.py:20
  81.4 1.3 %collective-permute-start.19 = (f32[168,128]{1,0:T(8,128)S(1)}, f32[168,128]{1,0:T(8,128)}, u32[]{:S(2)}, u32[]{:S(2)}) collective-permute-start(f32[168,128]{1,0:T(8,128)S(1)} %slice.79), channel_id=1, source_target_pairs={{1,0},{2,1},{3,2},{4,3},{5,4},{6,5},{7,6},{9,8},{10,9},{11,10},{12... | collective-permute-start | bytes 258056 | tf_op jit(solution)/shard_map/ppermute | solution.py:15
  84.4 1.5 %collective-permute-start.17 = (f32[128,256]{0,1:T(8,128)}, f32[128,256]{0,1:T(8,128)}, u32[]{:S(2)}, u32[]{:S(2)}) collective-permute-start(f32[128,256]{0,1:T(8,128)} %add.67), channel_id=1, source_target_pairs={{0,16},{8,24},{16,0},{24,8},{1,17},{9,25},{17,1},{25,9},{2,18},{10... | collective-permute-start | bytes 393224 | tf_op jit(solution)/shard_map/ppermute | solution.py:20
  87.3 2.0 %shard_map.88 = f32[256,128]{1,0:T(8,128)} custom-call(s32[25]{0:T(128)} %starts_ref.3, f32[25,128]{1,0:T(8,128)} %weights_ref.7, f32[256,128]{1,0:T(8,128)} %copy-done.10, f32[168,128]{1,0:T(8,128)} %collective-permute-done.19.second_ref), custom_call_target="tpu_custom_call" | custom-call | flops 1638400 | bytes 360960 | tf_op jit(solution)/shard_map/pallas_call | solution.py:87
  93.2 1.4 %fusion.9 = bf16[2048,256]{0,1:T(8,128)(2,1)} fusion(f32[2048,256]{0,1:T(8,128)S(1)} %fusion.3, bf16[2048,256]{0,1:T(8,128)(2,1)S(1)} %copy.29, bf16[2048,128]{1,0:T(8,128)(2,1)S(1)} %bitcast.108, f32[128,256]{0,1:T(8,128)S(1)} %bitcast_subtract_fusion), kind=kOutput, calls=%fused_computation.13 | convolution fusion | flops 136347648 | bytes 4849664 | tf_op jit(solution)/shard_map/dot_general | solution.py:120
  94.7 2.3 %copy.46 = bf16[2048,256]{1,0:T(8,128)(2,1)} copy(bf16[2048,256]{0,1:T(8,128)(2,1)} %fusion.9) | data formatting | bytes 2097152
  (114 shorter events, 30.1 us)
Async XLA Ops:
  1.5 7.7 %collective-permute-start = (bf16[256,128]{1,0:T(8,128)(2,1)S(1)}, bf16[256,128]{1,0:T(8,128)(2,1)S(1)}, u32[]{:S(2)}, u32[]{:S(2)}) collective-permute-start(bf16[256,128]{1,0:T(8,128)(2,1)S(1)} %convert_element_type.104), channel_id=1, source_target_pairs={{0,4},{1,5},{2,6},{3,7},{4,0},{5,1},{6,2},{7,3},{8,12},{9,13},{10,... | collective-permute-start | bytes 196616 | tf_op jit(solution)/shard_map/ppermute | solution.py:20
  10.2 5.0 %collective-permute-start.1 = (bf16[2,256,128]{2,1,0:T(8,128)(2,1)S(1)}, bf16[2,256,128]{2,1,0:T(8,128)(2,1)S(1)}, u32[]{:S(2)}, u32[]{:S(2)}) collective-permute-start(bf16[2,256,128]{2,1,0:T(8,128)(2,1)S(1)} %pad_maximum_fusion.6), channel_id=1, source_target_pairs={{0,2},{1,3},{2,0},{3,1},{4,6},{5,7},{6,4},{7,5},{8,10},{9,11},{10,... | collective-permute-start | bytes 393224 | tf_op jit(solution)/shard_map/ppermute | solution.py:20
  15.3 1.6 %collective-permute-start.2 = (bf16[2,2,256,128]{3,2,1,0:T(8,128)(2,1)S(1)}, bf16[2,2,256,128]{3,2,1,0:T(8,128)(2,1)S(1)}, u32[]{:S(2)}, u32[]{:S(2)}) collective-permute-start(bf16[2,2,256,128]{3,2,1,0:T(8,128)(2,1)S(1)} %pad_maximum_fusion.3), channel_id=1, source_target_pairs={{0,1},{1,0},{2,3},{3,2},{4,5},{5,4},{6,7},{7,6},{8,9},{9,8},{10,11... | collective-permute-start | bytes 786440 | tf_op jit(solution)/shard_map/ppermute | solution.py:20
  18.8 6.8 %copy-start.17 = (s32[25]{0:T(128)S(1)}, s32[25]{0:T(128)}, u32[]{:S(2)}) copy-start(s32[25]{0:T(128)} %starts_ref.3) | copy-start | bytes 304
  20.3 3.8 %collective-permute-start.3 = (bf16[2,2,256,128]{3,2,0,1:T(8,128)(2,1)}, bf16[2,2,256,128]{3,2,0,1:T(8,128)(2,1)}, u32[]{:S(2)}, u32[]{:S(2)}) collective-permute-start(bf16[2,2,256,128]{3,2,0,1:T(8,128)(2,1)} %fusion.10), channel_id=1, source_target_pairs={{0,1},{1,0},{2,3},{3,2},{4,5},{5,4},{6,7},{7,6},{8,9},{9,8},{10,11... | collective-permute-start | bytes 786440 | tf_op jit(solution)/shard_map/ppermute | solution.py:20
  20.9 12.6 %copy-start.8 = (f32[128,256]{0,1:T(8,128)}, f32[128,256]{0,1:T(8,128)S(1)}, u32[]{:S(2)}) copy-start(f32[128,256]{0,1:T(8,128)S(1)} %copy.36) | copy-start | bytes 393220
  21.6 11.9 %collective-permute-start.11 = (f32[168,128]{1,0:T(8,128)}, f32[168,128]{1,0:T(8,128)}, u32[]{:S(2)}, u32[]{:S(2)}) collective-permute-start(f32[168,128]{1,0:T(8,128)} %slice.70), channel_id=1, source_target_pairs={{0,1},{1,2},{2,3},{3,4},{4,5},{5,6},{6,7},{8,9},{9,10},{10,11},{11... | collective-permute-start | bytes 258056 | tf_op jit(solution)/shard_map/ppermute | solution.py:15
  25.5 6.1 %collective-permute-start.4 = (bf16[2,256,128]{2,1,0:T(8,128)(2,1)S(1)}, bf16[2,256,128]{2,1,0:T(8,128)(2,1)S(1)}, u32[]{:S(2)}, u32[]{:S(2)}) collective-permute-start(bf16[2,256,128]{2,1,0:T(8,128)(2,1)S(1)} %fusion.12), channel_id=1, source_target_pairs={{0,2},{1,3},{2,0},{3,1},{4,6},{5,7},{6,4},{7,5},{8,10},{9,11},{10,... | collective-permute-start | bytes 393224 | tf_op jit(solution)/shard_map/ppermute | solution.py:20
  32.3 6.2 %collective-permute-start.5 = (bf16[256,128]{1,0:T(8,128)(2,1)}, bf16[256,128]{1,0:T(8,128)(2,1)}, u32[]{:S(2)}, u32[]{:S(2)}) collective-permute-start(bf16[256,128]{1,0:T(8,128)(2,1)} %fusion.19), channel_id=1, source_target_pairs={{0,4},{1,5},{2,6},{3,7},{4,0},{5,1},{6,2},{7,3},{8,12},{9,13},{10,... | collective-permute-start | bytes 196616 | tf_op jit(solution)/shard_map/ppermute | solution.py:20
  35.5 11.2 %copy-start.9 = (f32[128,256]{0,1:T(8,128)S(1)}, f32[128,256]{0,1:T(8,128)}, u32[]{:S(2)}) copy-start(f32[128,256]{0,1:T(8,128)} %copy-done.8) | copy-start | bytes 393220
  35.5 11.2 %copy-start.16 = (f32[256,128]{1,0:T(8,128)S(1)}, f32[256,128]{1,0:T(8,128)}, u32[]{:S(2)}) copy-start(f32[256,128]{1,0:T(8,128)} %shard_map.85) | copy-start | bytes 393220
  40.1 5.5 %collective-permute-start.6 = (bf16[256,128]{1,0:T(8,128)(2,1)S(1)}, bf16[256,128]{1,0:T(8,128)(2,1)S(1)}, u32[]{:S(2)}, u32[]{:S(2)}) collective-permute-start(bf16[256,128]{1,0:T(8,128)(2,1)S(1)} %get-tuple-element.11), channel_id=1, source_target_pairs={{0,4},{1,5},{2,6},{3,7},{4,0},{5,1},{6,2},{7,3},{8,12},{9,13},{10,... | collective-permute-start | bytes 196616 | tf_op jit(solution)/shard_map/ppermute | solution.py:20
  42.9 5.3 %collective-permute-start.9 = (f32[128,256]{0,1:T(8,128)S(1)}, f32[128,256]{0,1:T(8,128)S(1)}, u32[]{:S(2)}, u32[]{:S(2)}) collective-permute-start(f32[128,256]{0,1:T(8,128)S(1)} %fusion.37), channel_id=1, source_target_pairs={{0,8},{8,0},{16,24},{24,16},{1,9},{9,1},{17,25},{25,17},{2,10},{10... | collective-permute-start | bytes 393224 | tf_op jit(solution)/shard_map/ppermute | solution.py:20
  45.7 5.0 %collective-permute-start.7 = (bf16[2,256,128]{2,1,0:T(8,128)(2,1)S(1)}, bf16[2,256,128]{2,1,0:T(8,128)(2,1)S(1)}, u32[]{:S(2)}, u32[]{:S(2)}) collective-permute-start(bf16[2,256,128]{2,1,0:T(8,128)(2,1)S(1)} %pad_maximum_fusion.7), channel_id=1, source_target_pairs={{0,2},{1,3},{2,0},{3,1},{4,6},{5,7},{6,4},{7,5},{8,10},{9,11},{10,... | collective-permute-start | bytes 393224 | tf_op jit(solution)/shard_map/ppermute | solution.py:20
  46.9 5.8 %copy-start.11 = (f32[256,128]{1,0:T(8,128)}, f32[256,128]{1,0:T(8,128)S(1)}, u32[]{:S(2)}) copy-start(f32[256,128]{1,0:T(8,128)S(1)} %subtract_select_fusion.1.first_ref) | copy-start | bytes 393220
  46.9 5.8 %collective-permute-start.12 = (f32[168,128]{1,0:T(8,128)S(1)}, f32[168,128]{1,0:T(8,128)}, u32[]{:S(2)}, u32[]{:S(2)}) collective-permute-start(f32[168,128]{1,0:T(8,128)S(1)} %slice.71), channel_id=1, source_target_pairs={{1,0},{2,1},{3,2},{4,3},{5,4},{6,5},{7,6},{9,8},{10,9},{11,10},{12... | collective-permute-start | bytes 258056 | tf_op jit(solution)/shard_map/ppermute | solution.py:15
  48.9 6.5 %collective-permute-start.10 = (f32[128,256]{0,1:T(8,128)}, f32[128,256]{0,1:T(8,128)}, u32[]{:S(2)}, u32[]{:S(2)}) collective-permute-start(f32[128,256]{0,1:T(8,128)} %add.60), channel_id=1, source_target_pairs={{0,16},{8,24},{16,0},{24,8},{1,17},{9,25},{17,1},{25,9},{2,18},{10... | collective-permute-start | bytes 393224 | tf_op jit(solution)/shard_map/ppermute | solution.py:20
  52.2 4.4 %collective-permute-start.8 = (bf16[2,2,256,128]{3,2,0,1:T(8,128)(2,1)}, bf16[2,2,256,128]{3,2,0,1:T(8,128)(2,1)}, u32[]{:S(2)}, u32[]{:S(2)}) collective-permute-start(bf16[2,2,256,128]{3,2,0,1:T(8,128)(2,1)} %pad_maximum_fusion.4), channel_id=1, source_target_pairs={{0,1},{1,0},{2,3},{3,2},{4,5},{5,4},{6,7},{7,6},{8,9},{9,8},{10,11... | collective-permute-start | bytes 786440 | tf_op jit(solution)/shard_map/ppermute | solution.py:20
  56.5 6.2 %copy-start.2 = (f32[128,256]{0,1:T(8,128)}, f32[128,256]{0,1:T(8,128)S(1)}, u32[]{:S(2)}) copy-start(f32[128,256]{0,1:T(8,128)S(1)} %bitcast_subtract_fusion.1) | copy-start | bytes 393220
  59.5 1.6 %collective-permute-start.13 = (bf16[2,2,256,128]{3,2,0,1:T(8,128)(2,1)S(1)}, bf16[2,2,256,128]{3,2,0,1:T(8,128)(2,1)S(1)}, u32[]{:S(2)}, u32[]{:S(2)}) collective-permute-start(bf16[2,2,256,128]{3,2,0,1:T(8,128)(2,1)S(1)} %fusion.11), channel_id=1, source_target_pairs={{0,1},{1,0},{2,3},{3,2},{4,5},{5,4},{6,7},{7,6},{8,9},{9,8},{10,11... | collective-permute-start | bytes 786440 | tf_op jit(solution)/shard_map/ppermute | solution.py:20
  61.2 5.6 %collective-permute-start.14 = (bf16[2,256,128]{2,1,0:T(8,128)(2,1)S(1)}, bf16[2,256,128]{2,1,0:T(8,128)(2,1)S(1)}, u32[]{:S(2)}, u32[]{:S(2)}) collective-permute-start(bf16[2,256,128]{2,1,0:T(8,128)(2,1)S(1)} %fusion.13), channel_id=1, source_target_pairs={{0,2},{1,3},{2,0},{3,1},{4,6},{5,7},{6,4},{7,5},{8,10},{9,11},{10,... | collective-permute-start | bytes 393224 | tf_op jit(solution)/shard_map/ppermute | solution.py:20
  62.7 18.6 %copy-start.3 = (f32[128,256]{0,1:T(8,128)S(1)}, f32[128,256]{0,1:T(8,128)}, u32[]{:S(2)}) copy-start(f32[128,256]{0,1:T(8,128)} %copy-done.2) | copy-start | bytes 393220
  62.7 7.1 %collective-permute-start.18 = (f32[168,128]{1,0:T(8,128)S(1)}, f32[168,128]{1,0:T(8,128)}, u32[]{:S(2)}, u32[]{:S(2)}) collective-permute-start(f32[168,128]{1,0:T(8,128)S(1)} %slice.78), channel_id=1, source_target_pairs={{0,1},{1,2},{2,3},{3,4},{4,5},{5,6},{6,7},{8,9},{9,10},{10,11},{11... | collective-permute-start | bytes 258056 | tf_op jit(solution)/shard_map/ppermute | solution.py:15
  67.5 5.5 %collective-permute-start.15 = (bf16[256,128]{1,0:T(8,128)(2,1)}, bf16[256,128]{1,0:T(8,128)(2,1)}, u32[]{:S(2)}, u32[]{:S(2)}) collective-permute-start(bf16[256,128]{1,0:T(8,128)(2,1)} %fusion.20), channel_id=1, source_target_pairs={{0,4},{1,5},{2,6},{3,7},{4,0},{5,1},{6,2},{7,3},{8,12},{9,13},{10,... | collective-permute-start | bytes 196616 | tf_op jit(solution)/shard_map/ppermute | solution.py:20
  71.8 9.5 %copy-start.15 = (f32[256,128]{1,0:T(8,128)S(1)}, f32[256,128]{1,0:T(8,128)}, u32[]{:S(2)}) copy-start(f32[256,128]{1,0:T(8,128)} %shard_map.87) | copy-start | bytes 393220
  74.6 5.6 %collective-permute-start.20 = (bf16[256,128]{1,0:T(8,128)(2,1)S(1)}, bf16[256,128]{1,0:T(8,128)(2,1)S(1)}, u32[]{:S(2)}, u32[]{:S(2)}) collective-permute-start(bf16[256,128]{1,0:T(8,128)(2,1)S(1)} %get-tuple-element.9), channel_id=1, source_target_pairs={{0,4},{1,5},{2,6},{3,7},{4,0},{5,1},{6,2},{7,3},{8,12},{9,13},{10,... | collective-permute-start | bytes 196616 | tf_op jit(solution)/shard_map/ppermute | solution.py:20
  78.7 5.0 %collective-permute-start.16 = (f32[128,256]{0,1:T(8,128)S(1)}, f32[128,256]{0,1:T(8,128)S(1)}, u32[]{:S(2)}, u32[]{:S(2)}) collective-permute-start(f32[128,256]{0,1:T(8,128)S(1)} %fusion.38), channel_id=1, source_target_pairs={{0,8},{8,0},{16,24},{24,16},{1,9},{9,1},{17,25},{25,17},{2,10},{10... | collective-permute-start | bytes 393224 | tf_op jit(solution)/shard_map/ppermute | solution.py:20
  80.3 5.6 %collective-permute-start.21 = (bf16[2,256,128]{2,1,0:T(8,128)(2,1)S(1)}, bf16[2,256,128]{2,1,0:T(8,128)(2,1)S(1)}, u32[]{:S(2)}, u32[]{:S(2)}) collective-permute-start(bf16[2,256,128]{2,1,0:T(8,128)(2,1)S(1)} %pad_maximum_fusion.8), channel_id=1, source_target_pairs={{0,2},{1,3},{2,0},{3,1},{4,6},{5,7},{6,4},{7,5},{8,10},{9,11},{10,... | collective-permute-start | bytes 393224 | tf_op jit(solution)/shard_map/ppermute | solution.py:20
  81.4 5.9 %copy-start.10 = (f32[256,128]{1,0:T(8,128)}, f32[256,128]{1,0:T(8,128)S(1)}, u32[]{:S(2)}) copy-start(f32[256,128]{1,0:T(8,128)S(1)} %subtract_select_fusion.first_ref) | copy-start | bytes 393220
  81.4 5.9 %collective-permute-start.19 = (f32[168,128]{1,0:T(8,128)S(1)}, f32[168,128]{1,0:T(8,128)}, u32[]{:S(2)}, u32[]{:S(2)}) collective-permute-start(f32[168,128]{1,0:T(8,128)S(1)} %slice.79), channel_id=1, source_target_pairs={{1,0},{2,1},{3,2},{4,3},{5,4},{6,5},{7,6},{9,8},{10,9},{11,10},{12... | collective-permute-start | bytes 258056 | tf_op jit(solution)/shard_map/ppermute | solution.py:15
  84.4 5.9 %collective-permute-start.17 = (f32[128,256]{0,1:T(8,128)}, f32[128,256]{0,1:T(8,128)}, u32[]{:S(2)}, u32[]{:S(2)}) collective-permute-start(f32[128,256]{0,1:T(8,128)} %add.67), channel_id=1, source_target_pairs={{0,16},{8,24},{16,0},{24,8},{1,17},{9,25},{17,1},{25,9},{2,18},{10... | collective-permute-start | bytes 393224 | tf_op jit(solution)/shard_map/ppermute | solution.py:20
  87.3 4.8 %collective-permute-start.22 = (bf16[2,2,256,128]{3,2,0,1:T(8,128)(2,1)}, bf16[2,2,256,128]{3,2,0,1:T(8,128)(2,1)}, u32[]{:S(2)}, u32[]{:S(2)}) collective-permute-start(bf16[2,2,256,128]{3,2,0,1:T(8,128)(2,1)} %pad_maximum_fusion.5), channel_id=1, source_target_pairs={{0,1},{1,0},{2,3},{3,2},{4,5},{5,4},{6,7},{7,6},{8,9},{9,8},{10,11... | collective-permute-start | bytes 786440 | tf_op jit(solution)/shard_map/ppermute | solution.py:20
  (9 other events, 8.9 us)

commit v4 on v3

--- a/solution.py
+++ b/solution.py
@@ -3,6 +3,7 @@
 from jax import lax
 from jax.experimental import pallas as pl
 from jax.experimental.pallas import tpu as pltpu
+from jax.experimental.layout import Layout, with_layout_constraint
 from jax.sharding import PartitionSpec as P
 
 MAXLAG = 168
@@ -71,22 +72,37 @@
     return (jnp.right_shift(repeated, hour % 8) & 1).astype(jnp.float32)
 
 
-def lag_kernel(starts_ref, weights_ref, first_ref, second_ref, out_ref, window_ref):
-    width, lead = out_ref.shape[0], first_ref.shape[0]
-    window_ref[pl.ds(0, lead), :] = first_ref[...]
-    window_ref[pl.ds(lead, second_ref.shape[0]), :] = second_ref[...]
-    running = jnp.zeros(out_ref.shape, jnp.float32)
+def lag_total(window_ref, weights_ref, starts_ref, width):
+    running = jnp.zeros((width, window_ref.shape[1]), jnp.float32)
     for k in range(weights_ref.shape[0]):
         row_block = window_ref[pl.ds(starts_ref[k], width), :]
         running = running + weights_ref[pl.ds(k, 1), :] * row_block
-    out_ref[...] = running
+    return running
 
 
-def lagged_sum(first, second, weights, starts, width):
-    rows, rank = first.shape[0] + second.shape[0], first.shape[1]
+def error_kernel(scalars_ref, weights_ref, before_ref, times_ref, out_ref, window_ref):
+    width = times_ref.shape[1]
+    current = times_ref[...].T
+    window_ref[pl.ds(0, width), :] = before_ref[...].T
+    window_ref[pl.ds(width, width), :] = current
+    errors = current - lag_total(window_ref, weights_ref, scalars_ref, width)
+    hour = lax.broadcasted_iota(jnp.int32, errors.shape, 0) + scalars_ref[weights_ref.shape[0]]
+    out_ref[...] = jnp.where(hour >= MAXLAG, errors, 0.0).T
+
+
+def ar_kernel(scalars_ref, weights_ref, errors_ref, after_ref, out_ref, window_ref):
+    width = errors_ref.shape[1]
+    current = errors_ref[...].T
+    window_ref[pl.ds(0, width), :] = current
+    window_ref[pl.ds(width, width), :] = after_ref[...].T
+    out_ref[...] = (current - lag_total(window_ref, weights_ref, scalars_ref, width)).T
+
+
+def lag_call(kernel, scalars, weights, first, second):
+    rank, width = first.shape
     return pl.pallas_call(
-        lag_kernel,
-        out_shape=jax.ShapeDtypeStruct((width, rank), jnp.float32),
+        kernel,
+        out_shape=jax.ShapeDtypeStruct((rank, width), jnp.float32),
         in_specs=[
             pl.BlockSpec(memory_space=pltpu.SMEM),
             pl.BlockSpec(memory_space=pltpu.VMEM),
@@ -94,13 +110,13 @@
             pl.BlockSpec(memory_space=pltpu.VMEM),
         ],
         out_specs=pl.BlockSpec(memory_space=pltpu.VMEM),
-        scratch_shapes=[pltpu.VMEM((rows, rank), jnp.float32)],
+        scratch_shapes=[pltpu.VMEM((2 * width, rank), jnp.float32)],
         cost_estimate=pl.CostEstimate(
             flops=2 * weights.shape[0] * width * rank,
             transcendentals=0,
-            bytes_accessed=4 * (rows * rank + weights.size + width * rank),
+            bytes_accessed=4 * (3 * width * rank + weights.size),
         ),
-    )(starts.astype(jnp.int32), weights, first, second)
+    )(scalars, weights, first, second)
 
 
 def fetch_rows(factors):
@@ -113,12 +129,15 @@
     total_series = panel.shape[0] * lax.axis_size("series")
     mask_values = unpack(observed)
     position = lax.axis_index("tm")
-    hour_index = position * hours + jnp.arange(hours, dtype=jnp.int32)
-    active_rows = (hour_index >= MAXLAG)[:, None]
+    before_scalars = jnp.concatenate(
+        [hours - lags.astype(jnp.int32), (position * hours)[None].astype(jnp.int32)]
+    )
+    after_scalars = lags.astype(jnp.int32)
 
     def compute_misfit(rows_low, times_low):
         predicted = jnp.dot(rows_low, times_low, preferred_element_type=jnp.float32)
-        return (mask_values * (predicted - panel.astype(jnp.float32))).astype(jnp.bfloat16)
+        misfit = (mask_values * (predicted - panel.astype(jnp.float32))).astype(jnp.bfloat16)
+        return with_layout_constraint(misfit, Layout((0, 1)))
 
     times = time_factors
     factors = series_factors
@@ -136,12 +155,10 @@
             rows_low, misfit, (((0,), (0,)), ((), ())), preferred_element_type=jnp.float32
         )
         grad_times = butterfly_sum(partial_value, "series")
-        times_t = times.T
-        tail_rows = shifted(times_t[hours - MAXLAG :], "tm", 1)
-        errors = times_t - lagged_sum(tail_rows, times_t, ar_weights, MAXLAG - lags, hours)
-        errors = jnp.where(active_rows, errors, 0.0)
-        head_rows = shifted(errors[:MAXLAG], "tm", -1)
-        ar_grad = (errors - lagged_sum(errors, head_rows, ar_weights, lags, hours)).T
+        before_block = shifted(times, "tm", 1)
+        errors = lag_call(error_kernel, before_scalars, ar_weights, before_block, times)
+        after_block = shifted(errors, "tm", -1)
+        ar_grad = lag_call(ar_kernel, after_scalars, ar_weights, errors, after_block)
         times_new = times - 24.0 / total_series * grad_times - 0.25 * ar_grad
         factors = factors - 2.0 / total_hours * grad_rows
         times = times_new

time: 97.5 us -> 94.7 us (0.971)
  local copies, waits for them, and re-layouts: 9.08 us -> 0.24 us
  waiting for transfers between devices: 23.6 us -> 27 us
  starting transfers between devices: 30 us -> 32.6 us
  other arithmetic: 16.9 us -> 15.4 us
  Pallas kernels: 7.81 us -> 8.91 us
    unnamed x40 -> x10, local copies, waits for them, and re-layouts: 8.17 us -> 0.03 us
    ppermute x19, starting transfers between devices: 22.3 us -> 26.2 us  [exchange(): return lax.ppermute(block, axis, [(i, i ^ bit) for i in range(devices)])]
    ppermute x19, waiting for transfers between devices: 23.6 us -> 26.9 us  [exchange(): return lax.ppermute(block, axis, [(i, i ^ bit) for i in range(devices)])]
    another operation x18, other arithmetic: 4.83 us -> 7.88 us  [doubling_gather(): block = jnp.stack([low, high], axis=step)]
    dot_general x2, matrix products: 3.57 us -> 0.68 us  [local(): lax.dot_general(rows_low, misfit, (((0,), (0,)), ((), ())), preferred_ele...]
    convert_element_type x6, other arithmetic: 2.13 us -> 0.19 us  [halving_sum(): send = jnp.where(upper, low, high).astype(jnp.bfloat16)]
    convert_element_type x3, other arithmetic: 4.1 us -> 2.31 us  [fetch_rows(): return doubling_gather(factors.astype(jnp.bfloat16), 'tm')]
    dot_general x3, matrix products: 2.36 us -> 4.1 us  [compute_misfit(): predicted = jnp.dot(rows_low, times_low, preferred_element_type=jnp.float32)]
  transfers between devices with their start and end apart: 23 -> 23, of which waited for: 12 -> 12; matrix products, arithmetic and copies ran while one was open for 17% -> 14% of each run, Pallas kernels for 8% -> 9%
where the time goes in v4:
time: 94.7 us; the launch traced here: 94.2 us
  starting transfers between devices  32.6 us (34%)
  waiting for transfers between devices  27 us (29%)
  other arithmetic  15.4 us (16%)
  matrix products  9.08 us (10%)
  Pallas kernels  8.91 us (9%)
  between operations  0.98 us (1%)
    ppermute x19, waiting for transfers between devices, exchange(): return lax.ppermute(block, axis, [(i, i ^ bit) for i in range(devices)])  26.9 us
    ppermute x19, starting transfers between devices, exchange(): return lax.ppermute(block, axis, [(i, i ^ bit) for i in range(devices)])  26.2 us
    pallas_call x4, Pallas kernels, lag_call(): pl.pallas_call(kernel, out_shape=jax.ShapeDtypeStruct((rank, width), jnp....  8.91 us
    another operation x18, other arithmetic, doubling_gather(): block = jnp.stack([low, high], axis=step)  7.88 us
    ppermute x4, starting transfers between devices, shifted(): return lax.ppermute(block, axis, route)  6.43 us
    dot_general x3, matrix products, compute_misfit(): predicted = jnp.dot(rows_low, times_low, preferred_element_type=jnp.float32)  4.1 us
    sub x2, other arithmetic, local(): times_new = times - 24.0 / total_series * grad_times - 0.25 * ar_grad  2.91 us
    dot_general x2, matrix products, local(): lax.dot_general(misfit, times_low, (((1,), (1,)), ((), ())), preferred_el...  2.66 us
  transfers between devices with their start and end apart: 23, of which 12 were waited for; matrix products, arithmetic and copies ran while one was open for 14% of the time, Pallas kernels for 9%

profile of v4, /device:TPU:0, one launch (start us, length us, event | category | flops | bytes accessed | tf_op | source)
XLA Modules:
  0.0 94.2 jit_solution(13982515485374446684)
XLA Ops:
  1.5 4.0 %collective-permute-start = (bf16[256,128]{1,0:T(8,128)(2,1)S(1)}, bf16[256,128]{1,0:T(8,128)(2,1)S(1)}, u32[]{:S(2)}, u32[]{:S(2)}) collective-permute-start(bf16[256,128]{1,0:T(8,128)(2,1)S(1)} %convert_element_type.104), channel_id=1, source_target_pairs={{0,4},{1,5},{2,6},{3,7},{4,0},{5,1},{6,2},{7,3},{8,12},{9,13},{10,... | collective-permute-start | bytes 196616 | tf_op jit(solution)/shard_map/ppermute | solution.py:21
  5.6 3.6 %collective-permute-done = bf16[256,128]{1,0:T(8,128)(2,1)S(1)} collective-permute-done((bf16[256,128]{1,0:T(8,128)(2,1)S(1)}, bf16[256,128]{1,0:T(8,128)(2,1)S(1)}, u32[]{:S(2)}, u32[]{:S(2)}) %collective-permute-start) | collective-permute-done | bytes 65568 | tf_op jit(solution)/shard_map/ppermute | solution.py:21
  10.8 4.4 %collective-permute-done.1 = bf16[2,256,128]{2,1,0:T(8,128)(2,1)S(1)} collective-permute-done((bf16[2,256,128]{2,1,0:T(8,128)(2,1)S(1)}, bf16[2,256,128]{2,1,0:T(8,128)(2,1)S(1)}, u32[]{:S(2)}, u32[]{:S(2)}) %collective-permute-start.1) | collective-permute-done | bytes 131104 | tf_op jit(solution)/shard_map/ppermute | solution.py:21
  15.4 1.6 %fusion.3 = f32[2048,256]{1,0:T(8,128)S(1)} fusion(s32[256]{0:T(256)S(1)} %get-tuple-element.29, s32[2048,32]{0,1:T(8,128)} %param.7, s32[256]{0:T(256)S(1)} %get-tuple-element.30), kind=kOutput, calls=%fused_computation.7 | convolution fusion | flops 35725312 | bytes 2361344 | tf_op jit(solution)/shard_map/dot_general | solution.py:69
  17.1 1.3 %fusion.7 = bf16[2048,256]{1,0:T(8,128)(2,1)S(1)} fusion(f32[2048,256]{1,0:T(8,128)S(1)} %fusion.3, bf16[2048,256]{1,0:T(8,128)(2,1)S(1)} %copy-done, bf16[2048,128]{1,0:T(8,128)(2,1)S(1)} %bitcast.93, f32[128,256]{1,0:T(8,128)} %times_ref.1), kind=kOutput, calls=%fused_computation.11 | convolution fusion | flops 136347648 | bytes 4849664 | tf_op jit(solution)/shard_map/dot_general | solution.py:138
  18.5 1.3 %fusion.25 = f32[2048,128]{1,0:T(8,128)S(1)} fusion(bf16[2048,256]{1,0:T(8,128)(2,1)S(1)} %fusion.7, f32[128,256]{1,0:T(8,128)} %times_ref.1), kind=kOutput, calls=%fused_computation.70 | convolution fusion | flops 134250496 | bytes 2228224 | tf_op jit(solution)/shard_map/dot_general | solution.py:149
  22.4 5.2 %collective-permute-done.4 = bf16[2,256,128]{2,1,0:T(8,128)(2,1)S(1)} collective-permute-done((bf16[2,256,128]{2,1,0:T(8,128)(2,1)S(1)}, bf16[2,256,128]{2,1,0:T(8,128)(2,1)S(1)}, u32[]{:S(2)}, u32[]{:S(2)}) %collective-permute-start.4) | collective-permute-done | bytes 131104 | tf_op jit(solution)/shard_map/ppermute | solution.py:21
  27.7 2.4 %collective-permute-start.5 = (bf16[256,128]{1,0:T(8,128)(2,1)S(1)}, bf16[256,128]{1,0:T(8,128)(2,1)S(1)}, u32[]{:S(2)}, u32[]{:S(2)}) collective-permute-start(bf16[256,128]{1,0:T(8,128)(2,1)S(1)} %fusion.19), channel_id=1, source_target_pairs={{0,4},{1,5},{2,6},{3,7},{4,0},{5,1},{6,2},{7,3},{8,12},{9,13},{10,... | collective-permute-start | bytes 196616 | tf_op jit(solution)/shard_map/ppermute | solution.py:21
  30.1 1.9 %collective-permute-start.11 = (f32[128,256]{1,0:T(8,128)}, f32[128,256]{1,0:T(8,128)}, u32[]{:S(2)}, u32[]{:S(2)}) collective-permute-start(f32[128,256]{1,0:T(8,128)} %times_ref.1), channel_id=1, source_target_pairs={{0,1},{1,2},{2,3},{3,4},{4,5},{5,6},{6,7},{8,9},{9,10},{10,11},{11... | collective-permute-start | bytes 393224 | tf_op jit(solution)/shard_map/ppermute | solution.py:16
  32.0 1.8 %collective-permute-done.5 = bf16[256,128]{1,0:T(8,128)(2,1)S(1)} collective-permute-done((bf16[256,128]{1,0:T(8,128)(2,1)S(1)}, bf16[256,128]{1,0:T(8,128)(2,1)S(1)}, u32[]{:S(2)}, u32[]{:S(2)}) %collective-permute-start.5) | collective-permute-done | bytes 65568 | tf_op jit(solution)/shard_map/ppermute | solution.py:21
  34.5 1.5 %collective-permute-start.6 = (bf16[256,128]{1,0:T(8,128)(2,1)S(1)}, bf16[256,128]{1,0:T(8,128)(2,1)S(1)}, u32[]{:S(2)}, u32[]{:S(2)}) collective-permute-start(bf16[256,128]{1,0:T(8,128)(2,1)S(1)} %get-tuple-element.5), channel_id=1, source_target_pairs={{0,4},{1,5},{2,6},{3,7},{4,0},{5,1},{6,2},{7,3},{8,12},{9,13},{10,... | collective-permute-start | bytes 196616 | tf_op jit(solution)/shard_map/ppermute | solution.py:21
  36.3 1.6 %collective-permute-start.9 = (f32[128,256]{1,0:T(8,128)S(1)}, f32[128,256]{1,0:T(8,128)S(1)}, u32[]{:S(2)}, u32[]{:S(2)}) collective-permute-start(f32[128,256]{1,0:T(8,128)S(1)} %fusion.37), channel_id=1, source_target_pairs={{0,8},{8,0},{16,24},{24,16},{1,9},{9,1},{17,25},{25,17},{2,10},{10... | collective-permute-start | bytes 393224 | tf_op jit(solution)/shard_map/ppermute | solution.py:21
  37.9 2.4 %collective-permute-done.6 = bf16[256,128]{1,0:T(8,128)(2,1)S(1)} collective-permute-done((bf16[256,128]{1,0:T(8,128)(2,1)S(1)}, bf16[256,128]{1,0:T(8,128)(2,1)S(1)}, u32[]{:S(2)}, u32[]{:S(2)}) %collective-permute-start.6) | collective-permute-done | bytes 65568 | tf_op jit(solution)/shard_map/ppermute | solution.py:21
  41.9 2.2 %shard_map.85.errors_ref = f32[128,256]{1,0:T(8,128)} custom-call(s32[26]{0:T(128)} %pad_add_fusion.scalars_ref, f32[25,128]{1,0:T(8,128)} %weights_ref.7, f32[128,256]{1,0:T(8,128)} %collective-permute-done.11.before_ref, f32[128,256]{1,0:T(8,128)} %times_ref.1), custom_call_target="tpu_custom_call" | custom-call | flops 1638400 | bytes 406016 | tf_op jit(solution)/shard_map/pallas_call | solution.py:103
  44.2 1.3 %collective-permute-start.12 = (f32[128,256]{1,0:T(8,128)}, f32[128,256]{1,0:T(8,128)}, u32[]{:S(2)}, u32[]{:S(2)}) collective-permute-start(f32[128,256]{1,0:T(8,128)} %shard_map.85.errors_ref), channel_id=1, source_target_pairs={{1,0},{2,1},{3,2},{4,3},{5,4},{6,5},{7,6},{9,8},{10,9},{11,10},{12... | collective-permute-start | bytes 393224 | tf_op jit(solution)/shard_map/ppermute | solution.py:16
  46.1 1.4 %collective-permute-start.10 = (f32[128,256]{1,0:T(8,128)}, f32[128,256]{1,0:T(8,128)}, u32[]{:S(2)}, u32[]{:S(2)}) collective-permute-start(f32[128,256]{1,0:T(8,128)} %add.50), channel_id=1, source_target_pairs={{0,16},{8,24},{16,0},{24,8},{1,17},{9,25},{17,1},{25,9},{2,18},{10... | collective-permute-start | bytes 393224 | tf_op jit(solution)/shard_map/ppermute | solution.py:21
  50.0 2.2 %shard_map.86 = f32[128,256]{1,0:T(8,128)} custom-call(s32[25]{0:T(128)} %scalars_ref.3, f32[25,128]{1,0:T(8,128)} %weights_ref.7, f32[128,256]{1,0:T(8,128)} %shard_map.85.errors_ref, f32[128,256]{1,0:T(8,128)} %collective-permute-done.12.after_ref), custom_call_target="tpu_custom_call" | custom-call | flops 1638400 | bytes 406016 | tf_op jit(solution)/shard_map/pallas_call | solution.py:103
  52.7 1.8 %multiply_subtract_fusion.1.times_ref = f32[128,256]{1,0:T(8,128)} fusion(f32[128,256]{1,0:T(8,128)} %shard_map.86, f32[128,256]{1,0:T(8,128)} %times_ref.1, f32[128,256]{1,0:T(8,128)} %add.50, f32[128,256]{1,0:T(8,128)} %collective-permute-done.10), kind=kLoop, calls=%fused_computation.51 | loop fusion | flops 163840 | bytes 655360 | tf_op jit(solution)/shard_map/sub | solution.py:162
  55.5 1.3 %fusion.8 = bf16[2048,256]{1,0:T(8,128)(2,1)S(1)} fusion(f32[2048,256]{1,0:T(8,128)S(1)} %fusion.3, bf16[2048,256]{1,0:T(8,128)(2,1)S(1)} %copy-done, bf16[2048,128]{1,0:T(8,128)(2,1)S(1)} %bitcast.91, f32[128,256]{1,0:T(8,128)} %multiply_subtract_fusion.1.times_ref), kind=kOutput, calls=%fused_computation.12 | convolution fusion | flops 136347648 | bytes 4849664 | tf_op jit(solution)/shard_map/dot_general | solution.py:138
  56.9 1.3 %fusion.22 = f32[2048,128]{1,0:T(8,128)S(1)} fusion(bf16[2048,256]{1,0:T(8,128)(2,1)S(1)} %fusion.8, f32[128,256]{1,0:T(8,128)} %multiply_subtract_fusion.1.times_ref), kind=kOutput, calls=%fused_computation.67 | convolution fusion | flops 134250496 | bytes 2228224 | tf_op jit(solution)/shard_map/dot_general | solution.py:149
  60.4 1.8 %collective-permute-start.14 = (bf16[2,256,128]{2,1,0:T(8,128)(2,1)S(1)}, bf16[2,256,128]{2,1,0:T(8,128)(2,1)S(1)}, u32[]{:S(2)}, u32[]{:S(2)}) collective-permute-start(bf16[2,256,128]{2,1,0:T(8,128)(2,1)S(1)} %fusion.13), channel_id=1, source_target_pairs={{0,2},{1,3},{2,0},{3,1},{4,6},{5,7},{6,4},{7,5},{8,10},{9,11},{10,... | collective-permute-start | bytes 393224 | tf_op jit(solution)/shard_map/ppermute | solution.py:21
  62.2 4.1 %collective-permute-done.14 = bf16[2,256,128]{2,1,0:T(8,128)(2,1)S(1)} collective-permute-done((bf16[2,256,128]{2,1,0:T(8,128)(2,1)S(1)}, bf16[2,256,128]{2,1,0:T(8,128)(2,1)S(1)}, u32[]{:S(2)}, u32[]{:S(2)}) %collective-permute-start.14) | collective-permute-done | bytes 131104 | tf_op jit(solution)/shard_map/ppermute | solution.py:21
  66.3 2.6 %collective-permute-start.15 = (bf16[256,128]{1,0:T(8,128)(2,1)S(1)}, bf16[256,128]{1,0:T(8,128)(2,1)S(1)}, u32[]{:S(2)}, u32[]{:S(2)}) collective-permute-start(bf16[256,128]{1,0:T(8,128)(2,1)S(1)} %fusion.20), channel_id=1, source_target_pairs={{0,4},{1,5},{2,6},{3,7},{4,0},{5,1},{6,2},{7,3},{8,12},{9,13},{10,... | collective-permute-start | bytes 196616 | tf_op jit(solution)/shard_map/ppermute | solution.py:21
  68.9 1.9 %collective-permute-start.18 = (f32[128,256]{1,0:T(8,128)}, f32[128,256]{1,0:T(8,128)}, u32[]{:S(2)}, u32[]{:S(2)}) collective-permute-start(f32[128,256]{1,0:T(8,128)} %multiply_subtract_fusion.1.times_ref), channel_id=1, source_target_pairs={{0,1},{1,2},{2,3},{3,4},{4,5},{5,6},{6,7},{8,9},{9,10},{10,11},{11... | collective-permute-start | bytes 393224 | tf_op jit(solution)/shard_map/ppermute | solution.py:16
  72.6 2.2 %collective-permute-start.20 = (bf16[256,128]{1,0:T(8,128)(2,1)S(1)}, bf16[256,128]{1,0:T(8,128)(2,1)S(1)}, u32[]{:S(2)}, u32[]{:S(2)}) collective-permute-start(bf16[256,128]{1,0:T(8,128)(2,1)S(1)} %get-tuple-element.3), channel_id=1, source_target_pairs={{0,4},{1,5},{2,6},{3,7},{4,0},{5,1},{6,2},{7,3},{8,12},{9,13},{10,... | collective-permute-start | bytes 196616 | tf_op jit(solution)/shard_map/ppermute | solution.py:21
  75.2 1.4 %collective-permute-start.16 = (f32[128,256]{1,0:T(8,128)S(1)}, f32[128,256]{1,0:T(8,128)S(1)}, u32[]{:S(2)}, u32[]{:S(2)}) collective-permute-start(f32[128,256]{1,0:T(8,128)S(1)} %fusion.38), channel_id=1, source_target_pairs={{0,8},{8,0},{16,24},{24,16},{1,9},{9,1},{17,25},{25,17},{2,10},{10... | collective-permute-start | bytes 393224 | tf_op jit(solution)/shard_map/ppermute | solution.py:21
  78.5 1.3 %collective-permute-start.21 = (bf16[2,256,128]{2,1,0:T(8,128)(2,1)}, bf16[2,256,128]{2,1,0:T(8,128)(2,1)}, u32[]{:S(2)}, u32[]{:S(2)}) collective-permute-start(bf16[2,256,128]{2,1,0:T(8,128)(2,1)} %pad_maximum_fusion.8), channel_id=1, source_target_pairs={{0,2},{1,3},{2,0},{3,1},{4,6},{5,7},{6,4},{7,5},{8,10},{9,11},{10,... | collective-permute-start | bytes 393224 | tf_op jit(solution)/shard_map/ppermute | solution.py:21
  79.8 2.2 %shard_map.87.errors_ref = f32[128,256]{1,0:T(8,128)} custom-call(s32[26]{0:T(128)} %pad_add_fusion.scalars_ref, f32[25,128]{1,0:T(8,128)} %weights_ref.7, f32[128,256]{1,0:T(8,128)} %collective-permute-done.18.before_ref, f32[128,256]{1,0:T(8,128)} %multiply_subtract_fusion.1.times_ref), custom_call_target="tpu_custom_call" | custom-call | flops 1638400 | bytes 406016 | tf_op jit(solution)/shard_map/pallas_call | solution.py:103
  82.0 1.3 %collective-permute-start.19 = (f32[128,256]{1,0:T(8,128)}, f32[128,256]{1,0:T(8,128)}, u32[]{:S(2)}, u32[]{:S(2)}) collective-permute-start(f32[128,256]{1,0:T(8,128)} %shard_map.87.errors_ref), channel_id=1, source_target_pairs={{1,0},{2,1},{3,2},{4,3},{5,4},{6,5},{7,6},{9,8},{10,9},{11,10},{12... | collective-permute-start | bytes 393224 | tf_op jit(solution)/shard_map/ppermute | solution.py:16
  84.0 1.4 %collective-permute-start.17 = (f32[128,256]{1,0:T(8,128)}, f32[128,256]{1,0:T(8,128)}, u32[]{:S(2)}, u32[]{:S(2)}) collective-permute-start(f32[128,256]{1,0:T(8,128)} %add.55), channel_id=1, source_target_pairs={{0,16},{8,24},{16,0},{24,8},{1,17},{9,25},{17,1},{25,9},{2,18},{10... | collective-permute-start | bytes 393224 | tf_op jit(solution)/shard_map/ppermute | solution.py:21
  87.9 2.2 %shard_map.88 = f32[128,256]{1,0:T(8,128)} custom-call(s32[25]{0:T(128)} %scalars_ref.3, f32[25,128]{1,0:T(8,128)} %weights_ref.7, f32[128,256]{1,0:T(8,128)} %shard_map.87.errors_ref, f32[128,256]{1,0:T(8,128)} %collective-permute-done.19.after_ref), custom_call_target="tpu_custom_call" | custom-call | flops 1638400 | bytes 406016 | tf_op jit(solution)/shard_map/pallas_call | solution.py:103
  92.8 1.4 %fusion.9 = bf16[2048,256]{1,0:T(8,128)(2,1)} fusion(f32[2048,256]{1,0:T(8,128)S(1)} %fusion.3, bf16[2048,256]{1,0:T(8,128)(2,1)S(1)} %copy-done, bf16[2048,128]{1,0:T(8,128)(2,1)S(1)} %bitcast.97, f32[128,256]{1,0:T(8,128)S(1)} %multiply_subtract_fusion), kind=kOutput, calls=%fused_computation.13 | convolution fusion | flops 136347648 | bytes 4849664 | tf_op jit(solution)/shard_map/dot_general | solution.py:138
  (78 shorter events, 24.7 us)
Async XLA Ops:
  1.5 7.7 %collective-permute-start = (bf16[256,128]{1,0:T(8,128)(2,1)S(1)}, bf16[256,128]{1,0:T(8,128)(2,1)S(1)}, u32[]{:S(2)}, u32[]{:S(2)}) collective-permute-start(bf16[256,128]{1,0:T(8,128)(2,1)S(1)} %convert_element_type.104), channel_id=1, source_target_pairs={{0,4},{1,5},{2,6},{3,7},{4,0},{5,1},{6,2},{7,3},{8,12},{9,13},{10,... | collective-permute-start | bytes 196616 | tf_op jit(solution)/shard_map/ppermute | solution.py:21
  10.2 5.0 %collective-permute-start.1 = (bf16[2,256,128]{2,1,0:T(8,128)(2,1)S(1)}, bf16[2,256,128]{2,1,0:T(8,128)(2,1)S(1)}, u32[]{:S(2)}, u32[]{:S(2)}) collective-permute-start(bf16[2,256,128]{2,1,0:T(8,128)(2,1)S(1)} %pad_maximum_fusion.6), channel_id=1, source_target_pairs={{0,2},{1,3},{2,0},{3,1},{4,6},{5,7},{6,4},{7,5},{8,10},{9,11},{10,... | collective-permute-start | bytes 393224 | tf_op jit(solution)/shard_map/ppermute | solution.py:21
  15.3 1.7 %collective-permute-start.2 = (bf16[2,2,256,128]{3,2,1,0:T(8,128)(2,1)S(1)}, bf16[2,2,256,128]{3,2,1,0:T(8,128)(2,1)S(1)}, u32[]{:S(2)}, u32[]{:S(2)}) collective-permute-start(bf16[2,2,256,128]{3,2,1,0:T(8,128)(2,1)S(1)} %pad_maximum_fusion.3), channel_id=1, source_target_pairs={{0,1},{1,0},{2,3},{3,2},{4,5},{5,4},{6,7},{7,6},{8,9},{9,8},{10,11... | collective-permute-start | bytes 786440 | tf_op jit(solution)/shard_map/ppermute | solution.py:21
  15.3 1.8 %copy-start = (bf16[2048,256]{1,0:T(8,128)(2,1)S(1)}, bf16[2048,256]{1,0:T(8,128)(2,1)}, u32[]{:S(2)}) copy-start(bf16[2048,256]{1,0:T(8,128)(2,1)} %param.6) | copy-start | bytes 3145732
  19.9 13.9 %copy-start.1 = (f32[256,128]{1,0:T(8,128)S(1)}, f32[256,128]{1,0:T(8,128)}, u32[]{:S(2)}) copy-start(f32[256,128]{1,0:T(8,128)} %param.8) | copy-start | bytes 393220
  20.0 1.7 %collective-permute-start.3 = (bf16[2,2,256,128]{3,2,0,1:T(8,128)(2,1)S(1)}, bf16[2,2,256,128]{3,2,0,1:T(8,128)(2,1)S(1)}, u32[]{:S(2)}, u32[]{:S(2)}) collective-permute-start(bf16[2,2,256,128]{3,2,0,1:T(8,128)(2,1)S(1)} %fusion.10), channel_id=1, source_target_pairs={{0,1},{1,0},{2,3},{3,2},{4,5},{5,4},{6,7},{7,6},{8,9},{9,8},{10,11... | collective-permute-start | bytes 786440 | tf_op jit(solution)/shard_map/ppermute | solution.py:21
  21.8 19.5 %copy-start.4 = (s32[25]{0:T(128)S(1)}, s32[25]{0:T(128)}, u32[]{:S(2)}) copy-start(s32[25]{0:T(128)} %scalars_ref.3) | copy-start | bytes 304
  21.8 5.8 %collective-permute-start.4 = (bf16[2,256,128]{2,1,0:T(8,128)(2,1)S(1)}, bf16[2,256,128]{2,1,0:T(8,128)(2,1)S(1)}, u32[]{:S(2)}, u32[]{:S(2)}) collective-permute-start(bf16[2,256,128]{2,1,0:T(8,128)(2,1)S(1)} %fusion.12), channel_id=1, source_target_pairs={{0,2},{1,3},{2,0},{3,1},{4,6},{5,7},{6,4},{7,5},{8,10},{9,11},{10,... | collective-permute-start | bytes 393224 | tf_op jit(solution)/shard_map/ppermute | solution.py:21
  27.7 6.1 %collective-permute-start.5 = (bf16[256,128]{1,0:T(8,128)(2,1)S(1)}, bf16[256,128]{1,0:T(8,128)(2,1)S(1)}, u32[]{:S(2)}, u32[]{:S(2)}) collective-permute-start(bf16[256,128]{1,0:T(8,128)(2,1)S(1)} %fusion.19), channel_id=1, source_target_pairs={{0,4},{1,5},{2,6},{3,7},{4,0},{5,1},{6,2},{7,3},{8,12},{9,13},{10,... | collective-permute-start | bytes 196616 | tf_op jit(solution)/shard_map/ppermute | solution.py:21
  30.1 11.9 %collective-permute-start.11 = (f32[128,256]{1,0:T(8,128)}, f32[128,256]{1,0:T(8,128)}, u32[]{:S(2)}, u32[]{:S(2)}) collective-permute-start(f32[128,256]{1,0:T(8,128)} %times_ref.1), channel_id=1, source_target_pairs={{0,1},{1,2},{2,3},{3,4},{4,5},{5,6},{6,7},{8,9},{9,10},{10,11},{11... | collective-permute-start | bytes 393224 | tf_op jit(solution)/shard_map/ppermute | solution.py:16
  34.5 5.9 %collective-permute-start.6 = (bf16[256,128]{1,0:T(8,128)(2,1)S(1)}, bf16[256,128]{1,0:T(8,128)(2,1)S(1)}, u32[]{:S(2)}, u32[]{:S(2)}) collective-permute-start(bf16[256,128]{1,0:T(8,128)(2,1)S(1)} %get-tuple-element.5), channel_id=1, source_target_pairs={{0,4},{1,5},{2,6},{3,7},{4,0},{5,1},{6,2},{7,3},{8,12},{9,13},{10,... | collective-permute-start | bytes 196616 | tf_op jit(solution)/shard_map/ppermute | solution.py:21
  36.3 9.1 %collective-permute-start.9 = (f32[128,256]{1,0:T(8,128)S(1)}, f32[128,256]{1,0:T(8,128)S(1)}, u32[]{:S(2)}, u32[]{:S(2)}) collective-permute-start(f32[128,256]{1,0:T(8,128)S(1)} %fusion.37), channel_id=1, source_target_pairs={{0,8},{8,0},{16,24},{24,16},{1,9},{9,1},{17,25},{25,17},{2,10},{10... | collective-permute-start | bytes 393224 | tf_op jit(solution)/shard_map/ppermute | solution.py:21
  41.0 6.5 %collective-permute-start.7 = (bf16[2,256,128]{2,1,0:T(8,128)(2,1)}, bf16[2,256,128]{2,1,0:T(8,128)(2,1)}, u32[]{:S(2)}, u32[]{:S(2)}) collective-permute-start(bf16[2,256,128]{2,1,0:T(8,128)(2,1)} %pad_maximum_fusion.7), channel_id=1, source_target_pairs={{0,2},{1,3},{2,0},{3,1},{4,6},{5,7},{6,4},{7,5},{8,10},{9,11},{10,... | collective-permute-start | bytes 393224 | tf_op jit(solution)/shard_map/ppermute | solution.py:21
  44.2 5.9 %collective-permute-start.12 = (f32[128,256]{1,0:T(8,128)}, f32[128,256]{1,0:T(8,128)}, u32[]{:S(2)}, u32[]{:S(2)}) collective-permute-start(f32[128,256]{1,0:T(8,128)} %shard_map.85.errors_ref), channel_id=1, source_target_pairs={{1,0},{2,1},{3,2},{4,3},{5,4},{6,5},{7,6},{9,8},{10,9},{11,10},{12... | collective-permute-start | bytes 393224 | tf_op jit(solution)/shard_map/ppermute | solution.py:16
  46.1 6.5 %collective-permute-start.10 = (f32[128,256]{1,0:T(8,128)}, f32[128,256]{1,0:T(8,128)}, u32[]{:S(2)}, u32[]{:S(2)}) collective-permute-start(f32[128,256]{1,0:T(8,128)} %add.50), channel_id=1, source_target_pairs={{0,16},{8,24},{16,0},{24,8},{1,17},{9,25},{17,1},{25,9},{2,18},{10... | collective-permute-start | bytes 393224 | tf_op jit(solution)/shard_map/ppermute | solution.py:21
  49.2 5.3 %collective-permute-start.8 = (bf16[2,2,256,128]{3,2,0,1:T(8,128)(2,1)}, bf16[2,2,256,128]{3,2,0,1:T(8,128)(2,1)}, u32[]{:S(2)}, u32[]{:S(2)}) collective-permute-start(bf16[2,2,256,128]{3,2,0,1:T(8,128)(2,1)} %pad_maximum_fusion.4), channel_id=1, source_target_pairs={{0,1},{1,0},{2,3},{3,2},{4,5},{5,4},{6,7},{7,6},{8,9},{9,8},{10,11... | collective-permute-start | bytes 786440 | tf_op jit(solution)/shard_map/ppermute | solution.py:21
  58.3 13.6 %copy-start.3 = (f32[256,128]{1,0:T(8,128)S(1)}, f32[256,128]{1,0:T(8,128)}, u32[]{:S(2)}) copy-start(f32[256,128]{1,0:T(8,128)} %get-tuple-element.6) | copy-start | bytes 393220
  58.4 2.0 %collective-permute-start.13 = (bf16[2,2,256,128]{3,2,0,1:T(8,128)(2,1)S(1)}, bf16[2,2,256,128]{3,2,0,1:T(8,128)(2,1)S(1)}, u32[]{:S(2)}, u32[]{:S(2)}) collective-permute-start(bf16[2,2,256,128]{3,2,0,1:T(8,128)(2,1)S(1)} %fusion.11), channel_id=1, source_target_pairs={{0,1},{1,0},{2,3},{3,2},{4,5},{5,4},{6,7},{7,6},{8,9},{9,8},{10,11... | collective-permute-start | bytes 786440 | tf_op jit(solution)/shard_map/ppermute | solution.py:21
  60.4 5.8 %collective-permute-start.14 = (bf16[2,256,128]{2,1,0:T(8,128)(2,1)S(1)}, bf16[2,256,128]{2,1,0:T(8,128)(2,1)S(1)}, u32[]{:S(2)}, u32[]{:S(2)}) collective-permute-start(bf16[2,256,128]{2,1,0:T(8,128)(2,1)S(1)} %fusion.13), channel_id=1, source_target_pairs={{0,2},{1,3},{2,0},{3,1},{4,6},{5,7},{6,4},{7,5},{8,10},{9,11},{10,... | collective-permute-start | bytes 393224 | tf_op jit(solution)/shard_map/ppermute | solution.py:21
  66.3 5.6 %collective-permute-start.15 = (bf16[256,128]{1,0:T(8,128)(2,1)S(1)}, bf16[256,128]{1,0:T(8,128)(2,1)S(1)}, u32[]{:S(2)}, u32[]{:S(2)}) collective-permute-start(bf16[256,128]{1,0:T(8,128)(2,1)S(1)} %fusion.20), channel_id=1, source_target_pairs={{0,4},{1,5},{2,6},{3,7},{4,0},{5,1},{6,2},{7,3},{8,12},{9,13},{10,... | collective-permute-start | bytes 196616 | tf_op jit(solution)/shard_map/ppermute | solution.py:21
  68.9 10.8 %collective-permute-start.18 = (f32[128,256]{1,0:T(8,128)}, f32[128,256]{1,0:T(8,128)}, u32[]{:S(2)}, u32[]{:S(2)}) collective-permute-start(f32[128,256]{1,0:T(8,128)} %multiply_subtract_fusion.1.times_ref), channel_id=1, source_target_pairs={{0,1},{1,2},{2,3},{3,4},{4,5},{5,6},{6,7},{8,9},{9,10},{10,11},{11... | collective-permute-start | bytes 393224 | tf_op jit(solution)/shard_map/ppermute | solution.py:16
  72.6 5.2 %collective-permute-start.20 = (bf16[256,128]{1,0:T(8,128)(2,1)S(1)}, bf16[256,128]{1,0:T(8,128)(2,1)S(1)}, u32[]{:S(2)}, u32[]{:S(2)}) collective-permute-start(bf16[256,128]{1,0:T(8,128)(2,1)S(1)} %get-tuple-element.3), channel_id=1, source_target_pairs={{0,4},{1,5},{2,6},{3,7},{4,0},{5,1},{6,2},{7,3},{8,12},{9,13},{10,... | collective-permute-start | bytes 196616 | tf_op jit(solution)/shard_map/ppermute | solution.py:21
  75.2 8.1 %collective-permute-start.16 = (f32[128,256]{1,0:T(8,128)S(1)}, f32[128,256]{1,0:T(8,128)S(1)}, u32[]{:S(2)}, u32[]{:S(2)}) collective-permute-start(f32[128,256]{1,0:T(8,128)S(1)} %fusion.38), channel_id=1, source_target_pairs={{0,8},{8,0},{16,24},{24,16},{1,9},{9,1},{17,25},{25,17},{2,10},{10... | collective-permute-start | bytes 393224 | tf_op jit(solution)/shard_map/ppermute | solution.py:21
  78.5 6.9 %collective-permute-start.21 = (bf16[2,256,128]{2,1,0:T(8,128)(2,1)}, bf16[2,256,128]{2,1,0:T(8,128)(2,1)}, u32[]{:S(2)}, u32[]{:S(2)}) collective-permute-start(bf16[2,256,128]{2,1,0:T(8,128)(2,1)} %pad_maximum_fusion.8), channel_id=1, source_target_pairs={{0,2},{1,3},{2,0},{3,1},{4,6},{5,7},{6,4},{7,5},{8,10},{9,11},{10,... | collective-permute-start | bytes 393224 | tf_op jit(solution)/shard_map/ppermute | solution.py:21
  82.0 5.9 %collective-permute-start.19 = (f32[128,256]{1,0:T(8,128)}, f32[128,256]{1,0:T(8,128)}, u32[]{:S(2)}, u32[]{:S(2)}) collective-permute-start(f32[128,256]{1,0:T(8,128)} %shard_map.87.errors_ref), channel_id=1, source_target_pairs={{1,0},{2,1},{3,2},{4,3},{5,4},{6,5},{7,6},{9,8},{10,9},{11,10},{12... | collective-permute-start | bytes 393224 | tf_op jit(solution)/shard_map/ppermute | solution.py:16
  84.0 6.5 %collective-permute-start.17 = (f32[128,256]{1,0:T(8,128)}, f32[128,256]{1,0:T(8,128)}, u32[]{:S(2)}, u32[]{:S(2)}) collective-permute-start(f32[128,256]{1,0:T(8,128)} %add.55), channel_id=1, source_target_pairs={{0,16},{8,24},{16,0},{24,8},{1,17},{9,25},{17,1},{25,9},{2,18},{10... | collective-permute-start | bytes 393224 | tf_op jit(solution)/shard_map/ppermute | solution.py:21
  87.0 4.6 %collective-permute-start.22 = (bf16[2,2,256,128]{3,2,0,1:T(8,128)(2,1)}, bf16[2,2,256,128]{3,2,0,1:T(8,128)(2,1)}, u32[]{:S(2)}, u32[]{:S(2)}) collective-permute-start(bf16[2,2,256,128]{3,2,0,1:T(8,128)(2,1)} %pad_maximum_fusion.5), channel_id=1, source_target_pairs={{0,1},{1,0},{2,3},{3,2},{4,5},{5,4},{6,7},{7,6},{8,9},{9,8},{10,11... | collective-permute-start | bytes 786440 | tf_op jit(solution)/shard_map/ppermute | solution.py:21
  91.6 2.6 %copy-start.2 = (f32[128,256]{1,0:T(8,128)}, f32[128,256]{1,0:T(8,128)S(1)}, u32[]{:S(2)}) copy-start(f32[128,256]{1,0:T(8,128)S(1)} %multiply_subtract_fusion) | copy-start | bytes 393220

commit v5 on v4

--- a/solution.py
+++ b/solution.py
@@ -48,11 +48,13 @@
     return block
 
 
-def doubling_gather(block, axis):
+def doubling_gather(block, axis, after=None):
     devices = lax.axis_size(axis)
     position = lax.axis_index(axis)
     levels = devices.bit_length() - 1
     for step in range(levels):
+        if step == 1 and after is not None:
+            block = block + (0.0 * after[:1, :1]).astype(block.dtype)
         bit = 1 << (levels - 1 - step)
         upper = (position & bit) != 0
         other = exchange(block, axis, bit)
@@ -119,8 +121,8 @@
     )(scalars, weights, first, second)
 
 
-def fetch_rows(factors):
-    return doubling_gather(factors.astype(jnp.bfloat16), "tm")
+def fetch_rows(factors, after=None):
+    return doubling_gather(factors.astype(jnp.bfloat16), "tm", after)
 
 
 def local(panel, observed, series_factors, time_factors, ar_weights, lags):
@@ -162,7 +164,7 @@
         times_new = times - 24.0 / total_series * grad_times - 0.25 * ar_grad
         factors = factors - 2.0 / total_hours * grad_rows
         times = times_new
-    final_rows = fetch_rows(factors)
+    final_rows = fetch_rows(factors, errors)
     misfit_final = compute_misfit(final_rows, times.astype(jnp.bfloat16))
     return (factors, times, misfit_final)
 

time: 94.7 us -> 92.8 us (0.980)
  local copies, waits for them, and re-layouts: 0.24 us -> 2.33 us
  starting transfers between devices: 32.6 us -> 30.8 us
  waiting for transfers between devices: 27 us -> 25.4 us
    ppermute x19, starting transfers between devices: 26.2 us -> 23.7 us  [exchange(): return lax.ppermute(block, axis, [(i, i ^ bit) for i in range(devices)])]
    ppermute x19, waiting for transfers between devices: 26.9 us -> 25.4 us  [exchange(): return lax.ppermute(block, axis, [(i, i ^ bit) for i in range(devices)])]
    another operation x18 -> x17, other arithmetic: 7.88 us -> 6.35 us  [doubling_gather(): block = jnp.stack([low, high], axis=step)]
    dot_general x2, matrix products: 0.68 us -> 2.07 us  [local(): lax.dot_general(rows_low, misfit, (((0,), (0,)), ((), ())), preferred_ele...]
    slice x0 -> x1, local copies, waits for them, and re-layouts: none -> 1.25 us  [doubling_gather(): block = block + (0.0 * after[:1, :1]).astype(block.dtype)]
  transfers between devices with their start and end apart: 23 -> 23, of which waited for: 12 -> 13; matrix products, arithmetic and copies ran while one was open for 14% -> 15% of each run, Pallas kernels for 9% -> 10%
where the time goes in v5:
time: 92.8 us; the launch traced here: 92.3 us
  starting transfers between devices  30.8 us (33%)
  waiting for transfers between devices  25.4 us (27%)
  other arithmetic  14.6 us (16%)
  Pallas kernels  8.9 us (10%)
  matrix products  8.64 us (9%)
  local copies, waits for them, and re-layouts  2.33 us (3%)
  between operations  1.58 us (2%)
    ppermute x19, waiting for transfers between devices, exchange(): return lax.ppermute(block, axis, [(i, i ^ bit) for i in range(devices)])  25.4 us
    ppermute x19, starting transfers between devices, exchange(): return lax.ppermute(block, axis, [(i, i ^ bit) for i in range(devices)])  23.7 us
    pallas_call x4, Pallas kernels, lag_call(): pl.pallas_call(kernel, out_shape=jax.ShapeDtypeStruct((rank, width), jnp....  8.9 us
    ppermute x4, starting transfers between devices, shifted(): return lax.ppermute(block, axis, route)  7.12 us
    another operation x17, other arithmetic, doubling_gather(): block = jnp.stack([low, high], axis=step)  6.35 us
    dot_general x3, matrix products, compute_misfit(): predicted = jnp.dot(rows_low, times_low, preferred_element_type=jnp.float32)  3.18 us
    convert_element_type x3, other arithmetic, fetch_rows(): return doubling_gather(factors.astype(jnp.bfloat16), 'tm', after)  3.14 us
    sub x2, other arithmetic, local(): times_new = times - 24.0 / total_series * grad_times - 0.25 * ar_grad  2.19 us
  transfers between devices with their start and end apart: 23, of which 13 were waited for; matrix products, arithmetic and copies ran while one was open for 15% of the time, Pallas kernels for 10%

profile of v5, /device:TPU:0, one launch (start us, length us, event | category | flops | bytes accessed | tf_op | source)
XLA Modules:
  0.0 92.3 jit_solution(1674584089782506949)
XLA Ops:
  1.5 4.0 %collective-permute-start = (bf16[256,128]{1,0:T(8,128)(2,1)S(1)}, bf16[256,128]{1,0:T(8,128)(2,1)S(1)}, u32[]{:S(2)}, u32[]{:S(2)}) collective-permute-start(bf16[256,128]{1,0:T(8,128)(2,1)S(1)} %convert_element_type.107), channel_id=1, source_target_pairs={{0,4},{1,5},{2,6},{3,7},{4,0},{5,1},{6,2},{7,3},{8,12},{9,13},{10,... | collective-permute-start | bytes 196616 | tf_op jit(solution)/shard_map/ppermute | solution.py:21
  5.6 3.6 %collective-permute-done = bf16[256,128]{1,0:T(8,128)(2,1)S(1)} collective-permute-done((bf16[256,128]{1,0:T(8,128)(2,1)S(1)}, bf16[256,128]{1,0:T(8,128)(2,1)S(1)}, u32[]{:S(2)}, u32[]{:S(2)}) %collective-permute-start) | collective-permute-done | bytes 65568 | tf_op jit(solution)/shard_map/ppermute | solution.py:21
  10.8 4.4 %collective-permute-done.1 = bf16[2,256,128]{2,1,0:T(8,128)(2,1)S(1)} collective-permute-done((bf16[2,256,128]{2,1,0:T(8,128)(2,1)S(1)}, bf16[2,256,128]{2,1,0:T(8,128)(2,1)S(1)}, u32[]{:S(2)}, u32[]{:S(2)}) %collective-permute-start.1) | collective-permute-done | bytes 131104 | tf_op jit(solution)/shard_map/ppermute | solution.py:21
  15.4 1.6 %fusion.3 = f32[2048,256]{1,0:T(8,128)S(1)} fusion(s32[256]{0:T(256)S(1)} %get-tuple-element.29, s32[2048,32]{0,1:T(8,128)} %param.7, s32[256]{0:T(256)S(1)} %get-tuple-element.30), kind=kOutput, calls=%fused_computation.7 | convolution fusion | flops 35725312 | bytes 2361344 | tf_op jit(solution)/shard_map/dot_general | solution.py:71
  17.1 1.3 %fusion.7 = bf16[2048,256]{1,0:T(8,128)(2,1)S(1)} fusion(f32[2048,256]{1,0:T(8,128)S(1)} %fusion.3, bf16[2048,256]{1,0:T(8,128)(2,1)S(1)} %copy-done, bf16[2048,128]{1,0:T(8,128)(2,1)S(1)} %bitcast.94, f32[128,256]{1,0:T(8,128)} %times_ref.1), kind=kOutput, calls=%fused_computation.11 | convolution fusion | flops 136347648 | bytes 4849664 | tf_op jit(solution)/shard_map/dot_general | solution.py:140
  18.5 1.3 %fusion.25 = f32[2048,128]{1,0:T(8,128)S(1)} fusion(bf16[2048,256]{1,0:T(8,128)(2,1)S(1)} %fusion.7, f32[128,256]{1,0:T(8,128)} %times_ref.1), kind=kOutput, calls=%fused_computation.70 | convolution fusion | flops 134250496 | bytes 2228224 | tf_op jit(solution)/shard_map/dot_general | solution.py:151
  22.4 5.2 %collective-permute-done.4 = bf16[2,256,128]{2,1,0:T(8,128)(2,1)S(1)} collective-permute-done((bf16[2,256,128]{2,1,0:T(8,128)(2,1)S(1)}, bf16[2,256,128]{2,1,0:T(8,128)(2,1)S(1)}, u32[]{:S(2)}, u32[]{:S(2)}) %collective-permute-start.4) | collective-permute-done | bytes 131104 | tf_op jit(solution)/shard_map/ppermute | solution.py:21
  27.7 2.4 %collective-permute-start.5 = (bf16[256,128]{1,0:T(8,128)(2,1)S(1)}, bf16[256,128]{1,0:T(8,128)(2,1)S(1)}, u32[]{:S(2)}, u32[]{:S(2)}) collective-permute-start(bf16[256,128]{1,0:T(8,128)(2,1)S(1)} %fusion.19), channel_id=1, source_target_pairs={{0,4},{1,5},{2,6},{3,7},{4,0},{5,1},{6,2},{7,3},{8,12},{9,13},{10,... | collective-permute-start | bytes 196616 | tf_op jit(solution)/shard_map/ppermute | solution.py:21
  30.1 1.9 %collective-permute-start.11 = (f32[128,256]{1,0:T(8,128)}, f32[128,256]{1,0:T(8,128)}, u32[]{:S(2)}, u32[]{:S(2)}) collective-permute-start(f32[128,256]{1,0:T(8,128)} %times_ref.1), channel_id=1, source_target_pairs={{0,1},{1,2},{2,3},{3,4},{4,5},{5,6},{6,7},{8,9},{9,10},{10,11},{11... | collective-permute-start | bytes 393224 | tf_op jit(solution)/shard_map/ppermute | solution.py:16
  32.0 1.7 %collective-permute-done.5 = bf16[256,128]{1,0:T(8,128)(2,1)S(1)} collective-permute-done((bf16[256,128]{1,0:T(8,128)(2,1)S(1)}, bf16[256,128]{1,0:T(8,128)(2,1)S(1)}, u32[]{:S(2)}, u32[]{:S(2)}) %collective-permute-start.5) | collective-permute-done | bytes 65568 | tf_op jit(solution)/shard_map/ppermute | solution.py:21
  34.5 1.5 %collective-permute-start.6 = (bf16[256,128]{1,0:T(8,128)(2,1)S(1)}, bf16[256,128]{1,0:T(8,128)(2,1)S(1)}, u32[]{:S(2)}, u32[]{:S(2)}) collective-permute-start(bf16[256,128]{1,0:T(8,128)(2,1)S(1)} %get-tuple-element.5), channel_id=1, source_target_pairs={{0,4},{1,5},{2,6},{3,7},{4,0},{5,1},{6,2},{7,3},{8,12},{9,13},{10,... | collective-permute-start | bytes 196616 | tf_op jit(solution)/shard_map/ppermute | solution.py:21
  36.3 1.6 %collective-permute-start.9 = (f32[128,256]{1,0:T(8,128)S(1)}, f32[128,256]{1,0:T(8,128)S(1)}, u32[]{:S(2)}, u32[]{:S(2)}) collective-permute-start(f32[128,256]{1,0:T(8,128)S(1)} %fusion.37), channel_id=1, source_target_pairs={{0,8},{8,0},{16,24},{24,16},{1,9},{9,1},{17,25},{25,17},{2,10},{10... | collective-permute-start | bytes 393224 | tf_op jit(solution)/shard_map/ppermute | solution.py:21
  37.9 2.4 %collective-permute-done.6 = bf16[256,128]{1,0:T(8,128)(2,1)S(1)} collective-permute-done((bf16[256,128]{1,0:T(8,128)(2,1)S(1)}, bf16[256,128]{1,0:T(8,128)(2,1)S(1)}, u32[]{:S(2)}, u32[]{:S(2)}) %collective-permute-start.6) | collective-permute-done | bytes 65568 | tf_op jit(solution)/shard_map/ppermute | solution.py:21
  41.9 2.2 %shard_map.85.errors_ref = f32[128,256]{1,0:T(8,128)} custom-call(s32[26]{0:T(128)} %pad_add_fusion.scalars_ref, f32[25,128]{1,0:T(8,128)} %weights_ref.7, f32[128,256]{1,0:T(8,128)} %collective-permute-done.11.before_ref, f32[128,256]{1,0:T(8,128)} %times_ref.1), custom_call_target="tpu_custom_call" | custom-call | flops 1638400 | bytes 406016 | tf_op jit(solution)/shard_map/pallas_call | solution.py:105
  44.1 1.3 %collective-permute-start.12 = (f32[128,256]{1,0:T(8,128)}, f32[128,256]{1,0:T(8,128)}, u32[]{:S(2)}, u32[]{:S(2)}) collective-permute-start(f32[128,256]{1,0:T(8,128)} %shard_map.85.errors_ref), channel_id=1, source_target_pairs={{1,0},{2,1},{3,2},{4,3},{5,4},{6,5},{7,6},{9,8},{10,9},{11,10},{12... | collective-permute-start | bytes 393224 | tf_op jit(solution)/shard_map/ppermute | solution.py:16
  46.1 1.4 %collective-permute-start.10 = (f32[128,256]{1,0:T(8,128)}, f32[128,256]{1,0:T(8,128)}, u32[]{:S(2)}, u32[]{:S(2)}) collective-permute-start(f32[128,256]{1,0:T(8,128)} %add.60), channel_id=1, source_target_pairs={{0,16},{8,24},{16,0},{24,8},{1,17},{9,25},{17,1},{25,9},{2,18},{10... | collective-permute-start | bytes 393224 | tf_op jit(solution)/shard_map/ppermute | solution.py:21
  50.0 2.2 %shard_map.86 = f32[128,256]{1,0:T(8,128)} custom-call(s32[25]{0:T(128)} %scalars_ref.3, f32[25,128]{1,0:T(8,128)} %weights_ref.7, f32[128,256]{1,0:T(8,128)} %shard_map.85.errors_ref, f32[128,256]{1,0:T(8,128)} %collective-permute-done.12.after_ref), custom_call_target="tpu_custom_call" | custom-call | flops 1638400 | bytes 406016 | tf_op jit(solution)/shard_map/pallas_call | solution.py:105
  58.8 1.8 %collective-permute-start.14 = (bf16[2,256,128]{2,1,0:T(8,128)(2,1)S(1)}, bf16[2,256,128]{2,1,0:T(8,128)(2,1)S(1)}, u32[]{:S(2)}, u32[]{:S(2)}) collective-permute-start(bf16[2,256,128]{2,1,0:T(8,128)(2,1)S(1)} %fusion.13), channel_id=1, source_target_pairs={{0,2},{1,3},{2,0},{3,1},{4,6},{5,7},{6,4},{7,5},{8,10},{9,11},{10,... | collective-permute-start | bytes 393224 | tf_op jit(solution)/shard_map/ppermute | solution.py:21
  60.6 2.6 %collective-permute-start.18 = (f32[128,256]{1,0:T(8,128)S(1)}, f32[128,256]{1,0:T(8,128)}, u32[]{:S(2)}, u32[]{:S(2)}) collective-permute-start(f32[128,256]{1,0:T(8,128)S(1)} %multiply_subtract_fusion.1.times_ref), channel_id=1, source_target_pairs={{0,1},{1,2},{2,3},{3,4},{4,5},{5,6},{6,7},{8,9},{9,10},{10,11},{11... | collective-permute-start | bytes 393224 | tf_op jit(solution)/shard_map/ppermute | solution.py:16
  63.2 1.5 %collective-permute-done.14 = bf16[2,256,128]{2,1,0:T(8,128)(2,1)S(1)} collective-permute-done((bf16[2,256,128]{2,1,0:T(8,128)(2,1)S(1)}, bf16[2,256,128]{2,1,0:T(8,128)(2,1)S(1)}, u32[]{:S(2)}, u32[]{:S(2)}) %collective-permute-start.14) | collective-permute-done | bytes 131104 | tf_op jit(solution)/shard_map/ppermute | solution.py:21
  65.3 2.5 %collective-permute-start.15 = (bf16[256,128]{1,0:T(8,128)(2,1)}, bf16[256,128]{1,0:T(8,128)(2,1)}, u32[]{:S(2)}, u32[]{:S(2)}) collective-permute-start(bf16[256,128]{1,0:T(8,128)(2,1)} %fusion.20), channel_id=1, source_target_pairs={{0,4},{1,5},{2,6},{3,7},{4,0},{5,1},{6,2},{7,3},{8,12},{9,13},{10,... | collective-permute-start | bytes 196616 | tf_op jit(solution)/shard_map/ppermute | solution.py:21
  67.9 2.2 %shard_map.87.errors_ref = f32[128,256]{1,0:T(8,128)} custom-call(s32[26]{0:T(128)} %pad_add_fusion.scalars_ref, f32[25,128]{1,0:T(8,128)} %weights_ref.7, f32[128,256]{1,0:T(8,128)} %collective-permute-done.18.before_ref, f32[128,256]{1,0:T(8,128)} %copy-done.3), custom_call_target="tpu_custom_call" | custom-call | flops 1638400 | bytes 406016 | tf_op jit(solution)/shard_map/pallas_call | solution.py:105
  70.1 1.2 %slice.64 = f32[1,1]{1,0:T(1,128)} slice(f32[128,256]{1,0:T(8,128)} %shard_map.87.errors_ref), slice={[0:1], [0:1]} | slice | bytes 8 | tf_op jit(solution)/shard_map/slice | solution.py:57
  71.9 1.5 %fusion.31 = (bf16[256,128]{1,0:T(8,128)(2,1)S(1)}, f32[256,128]{1,0:T(8,128)}) fusion(f32[256,128]{1,0:T(8,128)S(1)} %copy-done.8, bf16[256,128]{1,0:T(8,128)(2,1)} %collective-permute-done.15, f32[2,256,128]{2,1,0:T(8,128)S(1)} %bitcast_add_fusion.2, pred[]{:T(512)S(6)} %ne.63), kind=kLoop, calls=%fused_computation.84 | loop fusion | flops 196608 | bytes 655361 | tf_op jit(solution)/shard_map/convert_element_type | solution.py:125
  73.5 1.4 %collective-permute-start.20 = (bf16[256,128]{1,0:T(8,128)(2,1)S(1)}, bf16[256,128]{1,0:T(8,128)(2,1)S(1)}, u32[]{:S(2)}, u32[]{:S(2)}) collective-permute-start(bf16[256,128]{1,0:T(8,128)(2,1)S(1)} %get-tuple-element.3), channel_id=1, source_target_pairs={{0,4},{1,5},{2,6},{3,7},{4,0},{5,1},{6,2},{7,3},{8,12},{9,13},{10,... | collective-permute-start | bytes 196616 | tf_op jit(solution)/shard_map/ppermute | solution.py:21
  74.9 1.7 %fusion.38 = f32[128,256]{1,0:T(8,128)S(1)} fusion(bf16[2048,128]{1,0:T(8,128)(2,1)} %bitcast.93, bf16[2048,256]{1,0:T(8,128)(2,1)} %copy-done.1), kind=kOutput, calls=%fused_computation.89 | convolution fusion | flops 134217728 | bytes 1703936 | tf_op jit(solution)/shard_map/dot_general | solution.py:156
  76.6 1.4 %collective-permute-start.16 = (f32[128,256]{1,0:T(8,128)S(1)}, f32[128,256]{1,0:T(8,128)S(1)}, u32[]{:S(2)}, u32[]{:S(2)}) collective-permute-start(f32[128,256]{1,0:T(8,128)S(1)} %fusion.38), channel_id=1, source_target_pairs={{0,8},{8,0},{16,24},{24,16},{1,9},{9,1},{17,25},{25,17},{2,10},{10... | collective-permute-start | bytes 393224 | tf_op jit(solution)/shard_map/ppermute | solution.py:21
  78.0 1.3 %collective-permute-done.20 = bf16[256,128]{1,0:T(8,128)(2,1)S(1)} collective-permute-done((bf16[256,128]{1,0:T(8,128)(2,1)S(1)}, bf16[256,128]{1,0:T(8,128)(2,1)S(1)}, u32[]{:S(2)}, u32[]{:S(2)}) %collective-permute-start.20) | collective-permute-done | bytes 65568 | tf_op jit(solution)/shard_map/ppermute | solution.py:21
  79.8 1.3 %collective-permute-start.19 = (f32[128,256]{1,0:T(8,128)S(1)}, f32[128,256]{1,0:T(8,128)}, u32[]{:S(2)}, u32[]{:S(2)}) collective-permute-start(f32[128,256]{1,0:T(8,128)S(1)} %copy-done.7), channel_id=1, source_target_pairs={{1,0},{2,1},{3,2},{4,3},{5,4},{6,5},{7,6},{9,8},{10,9},{11,10},{12... | collective-permute-start | bytes 393224 | tf_op jit(solution)/shard_map/ppermute | solution.py:16
  82.3 1.4 %collective-permute-start.17 = (f32[128,256]{1,0:T(8,128)}, f32[128,256]{1,0:T(8,128)}, u32[]{:S(2)}, u32[]{:S(2)}) collective-permute-start(f32[128,256]{1,0:T(8,128)} %add.65), channel_id=1, source_target_pairs={{0,16},{8,24},{16,0},{24,8},{1,17},{9,25},{17,1},{25,9},{2,18},{10... | collective-permute-start | bytes 393224 | tf_op jit(solution)/shard_map/ppermute | solution.py:21
  85.2 2.2 %shard_map.88 = f32[128,256]{1,0:T(8,128)} custom-call(s32[25]{0:T(128)} %scalars_ref.3, f32[25,128]{1,0:T(8,128)} %weights_ref.7, f32[128,256]{1,0:T(8,128)} %shard_map.87.errors_ref, f32[128,256]{1,0:T(8,128)} %collective-permute-done.19.after_ref), custom_call_target="tpu_custom_call" | custom-call | flops 1638400 | bytes 406016 | tf_op jit(solution)/shard_map/pallas_call | solution.py:105
  90.9 1.4 %fusion.9 = bf16[2048,256]{1,0:T(8,128)(2,1)} fusion(f32[2048,256]{1,0:T(8,128)S(1)} %fusion.3, bf16[2048,256]{1,0:T(8,128)(2,1)S(1)} %copy-done, bf16[2048,128]{1,0:T(8,128)(2,1)S(1)} %bitcast.98, f32[128,256]{1,0:T(8,128)S(1)} %multiply_subtract_fusion), kind=kOutput, calls=%fused_computation.13 | convolution fusion | flops 136347648 | bytes 4849664 | tf_op jit(solution)/shard_map/dot_general | solution.py:140
  (89 shorter events, 24.8 us)
Async XLA Ops:
  1.5 7.7 %collective-permute-start = (bf16[256,128]{1,0:T(8,128)(2,1)S(1)}, bf16[256,128]{1,0:T(8,128)(2,1)S(1)}, u32[]{:S(2)}, u32[]{:S(2)}) collective-permute-start(bf16[256,128]{1,0:T(8,128)(2,1)S(1)} %convert_element_type.107), channel_id=1, source_target_pairs={{0,4},{1,5},{2,6},{3,7},{4,0},{5,1},{6,2},{7,3},{8,12},{9,13},{10,... | collective-permute-start | bytes 196616 | tf_op jit(solution)/shard_map/ppermute | solution.py:21
  10.2 5.0 %collective-permute-start.1 = (bf16[2,256,128]{2,1,0:T(8,128)(2,1)S(1)}, bf16[2,256,128]{2,1,0:T(8,128)(2,1)S(1)}, u32[]{:S(2)}, u32[]{:S(2)}) collective-permute-start(bf16[2,256,128]{2,1,0:T(8,128)(2,1)S(1)} %pad_maximum_fusion.6), channel_id=1, source_target_pairs={{0,2},{1,3},{2,0},{3,1},{4,6},{5,7},{6,4},{7,5},{8,10},{9,11},{10,... | collective-permute-start | bytes 393224 | tf_op jit(solution)/shard_map/ppermute | solution.py:21
  15.3 1.7 %collective-permute-start.2 = (bf16[2,2,256,128]{3,2,1,0:T(8,128)(2,1)S(1)}, bf16[2,2,256,128]{3,2,1,0:T(8,128)(2,1)S(1)}, u32[]{:S(2)}, u32[]{:S(2)}) collective-permute-start(bf16[2,2,256,128]{3,2,1,0:T(8,128)(2,1)S(1)} %pad_maximum_fusion.3), channel_id=1, source_target_pairs={{0,1},{1,0},{2,3},{3,2},{4,5},{5,4},{6,7},{7,6},{8,9},{9,8},{10,11... | collective-permute-start | bytes 786440 | tf_op jit(solution)/shard_map/ppermute | solution.py:21
  15.3 1.8 %copy-start = (bf16[2048,256]{1,0:T(8,128)(2,1)S(1)}, bf16[2048,256]{1,0:T(8,128)(2,1)}, u32[]{:S(2)}) copy-start(bf16[2048,256]{1,0:T(8,128)(2,1)} %param.6) | copy-start | bytes 3145732
  19.9 13.9 %copy-start.5 = (f32[256,128]{1,0:T(8,128)S(1)}, f32[256,128]{1,0:T(8,128)}, u32[]{:S(2)}) copy-start(f32[256,128]{1,0:T(8,128)} %param.8) | copy-start | bytes 393220
  20.0 1.7 %collective-permute-start.3 = (bf16[2,2,256,128]{3,2,0,1:T(8,128)(2,1)S(1)}, bf16[2,2,256,128]{3,2,0,1:T(8,128)(2,1)S(1)}, u32[]{:S(2)}, u32[]{:S(2)}) collective-permute-start(bf16[2,2,256,128]{3,2,0,1:T(8,128)(2,1)S(1)} %fusion.10), channel_id=1, source_target_pairs={{0,1},{1,0},{2,3},{3,2},{4,5},{5,4},{6,7},{7,6},{8,9},{9,8},{10,11... | collective-permute-start | bytes 786440 | tf_op jit(solution)/shard_map/ppermute | solution.py:21
  21.8 19.5 %copy-start.9 = (s32[25]{0:T(128)S(1)}, s32[25]{0:T(128)}, u32[]{:S(2)}) copy-start(s32[25]{0:T(128)} %scalars_ref.3) | copy-start | bytes 304
  21.8 5.8 %collective-permute-start.4 = (bf16[2,256,128]{2,1,0:T(8,128)(2,1)S(1)}, bf16[2,256,128]{2,1,0:T(8,128)(2,1)S(1)}, u32[]{:S(2)}, u32[]{:S(2)}) collective-permute-start(bf16[2,256,128]{2,1,0:T(8,128)(2,1)S(1)} %fusion.12), channel_id=1, source_target_pairs={{0,2},{1,3},{2,0},{3,1},{4,6},{5,7},{6,4},{7,5},{8,10},{9,11},{10,... | collective-permute-start | bytes 393224 | tf_op jit(solution)/shard_map/ppermute | solution.py:21
  27.7 6.1 %collective-permute-start.5 = (bf16[256,128]{1,0:T(8,128)(2,1)S(1)}, bf16[256,128]{1,0:T(8,128)(2,1)S(1)}, u32[]{:S(2)}, u32[]{:S(2)}) collective-permute-start(bf16[256,128]{1,0:T(8,128)(2,1)S(1)} %fusion.19), channel_id=1, source_target_pairs={{0,4},{1,5},{2,6},{3,7},{4,0},{5,1},{6,2},{7,3},{8,12},{9,13},{10,... | collective-permute-start | bytes 196616 | tf_op jit(solution)/shard_map/ppermute | solution.py:21
  30.1 11.8 %collective-permute-start.11 = (f32[128,256]{1,0:T(8,128)}, f32[128,256]{1,0:T(8,128)}, u32[]{:S(2)}, u32[]{:S(2)}) collective-permute-start(f32[128,256]{1,0:T(8,128)} %times_ref.1), channel_id=1, source_target_pairs={{0,1},{1,2},{2,3},{3,4},{4,5},{5,6},{6,7},{8,9},{9,10},{10,11},{11... | collective-permute-start | bytes 393224 | tf_op jit(solution)/shard_map/ppermute | solution.py:16
  34.5 5.9 %collective-permute-start.6 = (bf16[256,128]{1,0:T(8,128)(2,1)S(1)}, bf16[256,128]{1,0:T(8,128)(2,1)S(1)}, u32[]{:S(2)}, u32[]{:S(2)}) collective-permute-start(bf16[256,128]{1,0:T(8,128)(2,1)S(1)} %get-tuple-element.5), channel_id=1, source_target_pairs={{0,4},{1,5},{2,6},{3,7},{4,0},{5,1},{6,2},{7,3},{8,12},{9,13},{10,... | collective-permute-start | bytes 196616 | tf_op jit(solution)/shard_map/ppermute | solution.py:21
  36.3 9.1 %collective-permute-start.9 = (f32[128,256]{1,0:T(8,128)S(1)}, f32[128,256]{1,0:T(8,128)S(1)}, u32[]{:S(2)}, u32[]{:S(2)}) collective-permute-start(f32[128,256]{1,0:T(8,128)S(1)} %fusion.37), channel_id=1, source_target_pairs={{0,8},{8,0},{16,24},{24,16},{1,9},{9,1},{17,25},{25,17},{2,10},{10... | collective-permute-start | bytes 393224 | tf_op jit(solution)/shard_map/ppermute | solution.py:21
  41.0 6.4 %collective-permute-start.7 = (bf16[2,256,128]{2,1,0:T(8,128)(2,1)}, bf16[2,256,128]{2,1,0:T(8,128)(2,1)}, u32[]{:S(2)}, u32[]{:S(2)}) collective-permute-start(bf16[2,256,128]{2,1,0:T(8,128)(2,1)} %pad_maximum_fusion.7), channel_id=1, source_target_pairs={{0,2},{1,3},{2,0},{3,1},{4,6},{5,7},{6,4},{7,5},{8,10},{9,11},{10,... | collective-permute-start | bytes 393224 | tf_op jit(solution)/shard_map/ppermute | solution.py:21
  44.1 5.9 %collective-permute-start.12 = (f32[128,256]{1,0:T(8,128)}, f32[128,256]{1,0:T(8,128)}, u32[]{:S(2)}, u32[]{:S(2)}) collective-permute-start(f32[128,256]{1,0:T(8,128)} %shard_map.85.errors_ref), channel_id=1, source_target_pairs={{1,0},{2,1},{3,2},{4,3},{5,4},{6,5},{7,6},{9,8},{10,9},{11,10},{12... | collective-permute-start | bytes 393224 | tf_op jit(solution)/shard_map/ppermute | solution.py:16
  46.1 6.5 %collective-permute-start.10 = (f32[128,256]{1,0:T(8,128)}, f32[128,256]{1,0:T(8,128)}, u32[]{:S(2)}, u32[]{:S(2)}) collective-permute-start(f32[128,256]{1,0:T(8,128)} %add.60), channel_id=1, source_target_pairs={{0,16},{8,24},{16,0},{24,8},{1,17},{9,25},{17,1},{25,9},{2,18},{10... | collective-permute-start | bytes 393224 | tf_op jit(solution)/shard_map/ppermute | solution.py:21
  49.1 4.6 %collective-permute-start.8 = (bf16[2,2,256,128]{3,2,0,1:T(8,128)(2,1)}, bf16[2,2,256,128]{3,2,0,1:T(8,128)(2,1)}, u32[]{:S(2)}, u32[]{:S(2)}) collective-permute-start(bf16[2,2,256,128]{3,2,0,1:T(8,128)(2,1)} %pad_maximum_fusion.4), channel_id=1, source_target_pairs={{0,1},{1,0},{2,3},{3,2},{4,5},{5,4},{6,7},{7,6},{8,9},{9,8},{10,11... | collective-permute-start | bytes 786440 | tf_op jit(solution)/shard_map/ppermute | solution.py:21
  53.7 6.8 %copy-start.3 = (f32[128,256]{1,0:T(8,128)}, f32[128,256]{1,0:T(8,128)S(1)}, u32[]{:S(2)}) copy-start(f32[128,256]{1,0:T(8,128)S(1)} %multiply_subtract_fusion.1.times_ref) | copy-start | bytes 393220
  55.7 1.0 %copy-start.1 = (bf16[2048,256]{1,0:T(8,128)(2,1)}, bf16[2048,256]{1,0:T(8,128)(2,1)S(1)}, u32[]{:S(2)}) copy-start(bf16[2048,256]{1,0:T(8,128)(2,1)S(1)} %fusion.8) | copy-start | bytes 3145732
  56.7 15.2 %copy-start.8 = (f32[256,128]{1,0:T(8,128)S(1)}, f32[256,128]{1,0:T(8,128)}, u32[]{:S(2)}) copy-start(f32[256,128]{1,0:T(8,128)} %get-tuple-element.6) | copy-start | bytes 393220
  56.7 2.0 %collective-permute-start.13 = (bf16[2,2,256,128]{3,2,0,1:T(8,128)(2,1)S(1)}, bf16[2,2,256,128]{3,2,0,1:T(8,128)(2,1)S(1)}, u32[]{:S(2)}, u32[]{:S(2)}) collective-permute-start(bf16[2,2,256,128]{3,2,0,1:T(8,128)(2,1)S(1)} %fusion.11), channel_id=1, source_target_pairs={{0,1},{1,0},{2,3},{3,2},{4,5},{5,4},{6,7},{7,6},{8,9},{9,8},{10,11... | collective-permute-start | bytes 786440 | tf_op jit(solution)/shard_map/ppermute | solution.py:21
  58.8 5.8 %collective-permute-start.14 = (bf16[2,256,128]{2,1,0:T(8,128)(2,1)S(1)}, bf16[2,256,128]{2,1,0:T(8,128)(2,1)S(1)}, u32[]{:S(2)}, u32[]{:S(2)}) collective-permute-start(bf16[2,256,128]{2,1,0:T(8,128)(2,1)S(1)} %fusion.13), channel_id=1, source_target_pairs={{0,2},{1,3},{2,0},{3,1},{4,6},{5,7},{6,4},{7,5},{8,10},{9,11},{10,... | collective-permute-start | bytes 393224 | tf_op jit(solution)/shard_map/ppermute | solution.py:21
  60.6 7.3 %collective-permute-start.18 = (f32[128,256]{1,0:T(8,128)S(1)}, f32[128,256]{1,0:T(8,128)}, u32[]{:S(2)}, u32[]{:S(2)}) collective-permute-start(f32[128,256]{1,0:T(8,128)S(1)} %multiply_subtract_fusion.1.times_ref), channel_id=1, source_target_pairs={{0,1},{1,2},{2,3},{3,4},{4,5},{5,6},{6,7},{8,9},{9,10},{10,11},{11... | collective-permute-start | bytes 393224 | tf_op jit(solution)/shard_map/ppermute | solution.py:16
  65.3 6.6 %collective-permute-start.15 = (bf16[256,128]{1,0:T(8,128)(2,1)}, bf16[256,128]{1,0:T(8,128)(2,1)}, u32[]{:S(2)}, u32[]{:S(2)}) collective-permute-start(bf16[256,128]{1,0:T(8,128)(2,1)} %fusion.20), channel_id=1, source_target_pairs={{0,4},{1,5},{2,6},{3,7},{4,0},{5,1},{6,2},{7,3},{8,12},{9,13},{10,... | collective-permute-start | bytes 196616 | tf_op jit(solution)/shard_map/ppermute | solution.py:21
  70.1 9.7 %copy-start.7 = (f32[128,256]{1,0:T(8,128)S(1)}, f32[128,256]{1,0:T(8,128)}, u32[]{:S(2)}) copy-start(f32[128,256]{1,0:T(8,128)} %shard_map.87.errors_ref) | copy-start | bytes 393220
  73.5 15.2 %copy-start.4 = (f32[128,256]{1,0:T(8,128)S(1)}, f32[128,256]{1,0:T(8,128)}, u32[]{:S(2)}) copy-start(f32[128,256]{1,0:T(8,128)} %copy-done.3) | copy-start | bytes 393220
  73.5 5.9 %collective-permute-start.20 = (bf16[256,128]{1,0:T(8,128)(2,1)S(1)}, bf16[256,128]{1,0:T(8,128)(2,1)S(1)}, u32[]{:S(2)}, u32[]{:S(2)}) collective-permute-start(bf16[256,128]{1,0:T(8,128)(2,1)S(1)} %get-tuple-element.3), channel_id=1, source_target_pairs={{0,4},{1,5},{2,6},{3,7},{4,0},{5,1},{6,2},{7,3},{8,12},{9,13},{10,... | collective-permute-start | bytes 196616 | tf_op jit(solution)/shard_map/ppermute | solution.py:21
  76.6 5.0 %collective-permute-start.16 = (f32[128,256]{1,0:T(8,128)S(1)}, f32[128,256]{1,0:T(8,128)S(1)}, u32[]{:S(2)}, u32[]{:S(2)}) collective-permute-start(f32[128,256]{1,0:T(8,128)S(1)} %fusion.38), channel_id=1, source_target_pairs={{0,8},{8,0},{16,24},{24,16},{1,9},{9,1},{17,25},{25,17},{2,10},{10... | collective-permute-start | bytes 393224 | tf_op jit(solution)/shard_map/ppermute | solution.py:21
  79.4 5.0 %collective-permute-start.21 = (bf16[2,256,128]{2,1,0:T(8,128)(2,1)S(1)}, bf16[2,256,128]{2,1,0:T(8,128)(2,1)S(1)}, u32[]{:S(2)}, u32[]{:S(2)}) collective-permute-start(bf16[2,256,128]{2,1,0:T(8,128)(2,1)S(1)} %maximum_add_fusion), channel_id=1, source_target_pairs={{0,2},{1,3},{2,0},{3,1},{4,6},{5,7},{6,4},{7,5},{8,10},{9,11},{10,... | collective-permute-start | bytes 393224 | tf_op jit(solution)/shard_map/ppermute | solution.py:21
  79.8 5.4 %collective-permute-start.19 = (f32[128,256]{1,0:T(8,128)S(1)}, f32[128,256]{1,0:T(8,128)}, u32[]{:S(2)}, u32[]{:S(2)}) collective-permute-start(f32[128,256]{1,0:T(8,128)S(1)} %copy-done.7), channel_id=1, source_target_pairs={{1,0},{2,1},{3,2},{4,3},{5,4},{6,5},{7,6},{9,8},{10,9},{11,10},{12... | collective-permute-start | bytes 393224 | tf_op jit(solution)/shard_map/ppermute | solution.py:16
  82.3 6.3 %collective-permute-start.17 = (f32[128,256]{1,0:T(8,128)}, f32[128,256]{1,0:T(8,128)}, u32[]{:S(2)}, u32[]{:S(2)}) collective-permute-start(f32[128,256]{1,0:T(8,128)} %add.65), channel_id=1, source_target_pairs={{0,16},{8,24},{16,0},{24,8},{1,17},{9,25},{17,1},{25,9},{2,18},{10... | collective-permute-start | bytes 393224 | tf_op jit(solution)/shard_map/ppermute | solution.py:21
  85.2 4.5 %collective-permute-start.22 = (bf16[2,2,256,128]{3,2,0,1:T(8,128)(2,1)}, bf16[2,2,256,128]{3,2,0,1:T(8,128)(2,1)}, u32[]{:S(2)}, u32[]{:S(2)}) collective-permute-start(bf16[2,2,256,128]{3,2,0,1:T(8,128)(2,1)} %pad_maximum_fusion.5), channel_id=1, source_target_pairs={{0,1},{1,0},{2,3},{3,2},{4,5},{5,4},{6,7},{7,6},{8,9},{9,8},{10,11... | collective-permute-start | bytes 786440 | tf_op jit(solution)/shard_map/ppermute | solution.py:21
  89.7 2.6 %copy-start.6 = (f32[128,256]{1,0:T(8,128)}, f32[128,256]{1,0:T(8,128)S(1)}, u32[]{:S(2)}) copy-start(f32[128,256]{1,0:T(8,128)S(1)} %multiply_subtract_fusion) | copy-start | bytes 393220
  (1 other events, 0.8 us)

commit v6 on v5

--- a/solution.py
+++ b/solution.py
@@ -144,7 +144,9 @@
     times = time_factors
     factors = series_factors
     for iteration in range(ITERS):
-        rows_low = fetch_rows(factors)
+        before_block = shifted(times, "tm", 1)
+        errors = lag_call(error_kernel, before_scalars, ar_weights, before_block, times)
+        rows_low = fetch_rows(factors, errors if iteration == 0 else None)
         times_low = times.astype(jnp.bfloat16)
         misfit = compute_misfit(rows_low, times_low)
         grad_rows = halving_sum(
@@ -157,8 +159,6 @@
             rows_low, misfit, (((0,), (0,)), ((), ())), preferred_element_type=jnp.float32
         )
         grad_times = butterfly_sum(partial_value, "series")
-        before_block = shifted(times, "tm", 1)
-        errors = lag_call(error_kernel, before_scalars, ar_weights, before_block, times)
         after_block = shifted(errors, "tm", -1)
         ar_grad = lag_call(ar_kernel, after_scalars, ar_weights, errors, after_block)
         times_new = times - 24.0 / total_series * grad_times - 0.25 * ar_grad

time: 92.8 us -> 92.2 us (level)
  matrix products: 8.64 us -> 5.77 us
  local copies, waits for them, and re-layouts: 2.33 us -> 4.24 us
    another operation x17 -> x16, other arithmetic: 6.35 us -> 4.77 us  [doubling_gather(): block = jnp.stack([low, high], axis=step)]
    slice x1 -> x2, local copies, waits for them, and re-layouts: 1.25 us -> 2.48 us  [doubling_gather(): block = block + (0.0 * after[:1, :1]).astype(block.dtype)]
    dot_general x1, matrix products: 1.63 us -> 0.59 us  [unpack(): jnp.dot(packed_words.astype(jnp.bfloat16), spread, preferred_element_type...]
  transfers between devices with their start and end apart: 23 -> 23, of which waited for: 13 -> 15; matrix products, arithmetic and copies ran while one was open for 15% -> 13% of each run, Pallas kernels for 10% -> 7%
where the time goes in v6:
time: 92.2 us; the launch traced here: 91.7 us
  starting transfers between devices  30.9 us (34%)
  waiting for transfers between devices  25.7 us (28%)
  other arithmetic  13.8 us (15%)
  Pallas kernels  8.9 us (10%)
  matrix products  5.77 us (6%)
  local copies, waits for them, and re-layouts  4.24 us (5%)
  between operations  2.37 us (3%)
    ppermute x19, waiting for transfers between devices, exchange(): return lax.ppermute(block, axis, [(i, i ^ bit) for i in range(devices)])  25.7 us
    ppermute x19, starting transfers between devices, exchange(): return lax.ppermute(block, axis, [(i, i ^ bit) for i in range(devices)])  24.3 us
    pallas_call x4, Pallas kernels, lag_call(): pl.pallas_call(kernel, out_shape=jax.ShapeDtypeStruct((rank, width), jnp....  8.9 us
    ppermute x4, starting transfers between devices, shifted(): return lax.ppermute(block, axis, route)  6.51 us
    another operation x16, other arithmetic, doubling_gather(): block = jnp.stack([low, high], axis=step)  4.77 us
    convert_element_type x3, other arithmetic, fetch_rows(): return doubling_gather(factors.astype(jnp.bfloat16), 'tm', after)  3.17 us
    slice x2, local copies, waits for them, and re-layouts, doubling_gather(): block = block + (0.0 * after[:1, :1]).astype(block.dtype)  2.48 us
    dot_general x3, matrix products, compute_misfit(): predicted = jnp.dot(rows_low, times_low, preferred_element_type=jnp.float32)  2.27 us
  transfers between devices with their start and end apart: 23, of which 15 were waited for; matrix products, arithmetic and copies ran while one was open for 13% of the time, Pallas kernels for 7%

profile of v6, /device:TPU:0, one launch (start us, length us, event | category | flops | bytes accessed | tf_op | source)
XLA Modules:
  0.0 91.7 jit_solution(6541477026530842417)
XLA Ops:
  1.6 4.0 %collective-permute-start = (bf16[256,128]{1,0:T(8,128)(2,1)S(1)}, bf16[256,128]{1,0:T(8,128)(2,1)S(1)}, u32[]{:S(2)}, u32[]{:S(2)}) collective-permute-start(bf16[256,128]{1,0:T(8,128)(2,1)S(1)} %convert_element_type.110), channel_id=1, source_target_pairs={{0,4},{1,5},{2,6},{3,7},{4,0},{5,1},{6,2},{7,3},{8,12},{9,13},{10,... | collective-permute-start | bytes 196616 | tf_op jit(solution)/shard_map/ppermute | solution.py:21
  5.6 1.5 %collective-permute-start.1 = (f32[128,256]{1,0:T(8,128)}, f32[128,256]{1,0:T(8,128)S(1)}, u32[]{:S(2)}, u32[]{:S(2)}) collective-permute-start(f32[128,256]{1,0:T(8,128)} %times_ref.1), channel_id=1, source_target_pairs={{0,1},{1,2},{2,3},{3,4},{4,5},{5,6},{6,7},{8,9},{9,10},{10,11},{11... | collective-permute-start | bytes 393224 | tf_op jit(solution)/shard_map/ppermute | solution.py:16
  10.9 2.2 %shard_map.85.errors_ref = f32[128,256]{1,0:T(8,128)} custom-call(s32[26]{0:T(128)} %pad_add_fusion.scalars_ref, f32[25,128]{1,0:T(8,128)} %weights_ref.7, f32[128,256]{1,0:T(8,128)} %copy-done.12, f32[128,256]{1,0:T(8,128)} %times_ref.1), custom_call_target="tpu_custom_call" | custom-call | flops 1638400 | bytes 406016 | tf_op jit(solution)/shard_map/pallas_call | solution.py:105
  13.1 1.2 %slice.56 = f32[1,1]{1,0:T(1,128)} slice(f32[128,256]{1,0:T(8,128)} %shard_map.85.errors_ref), slice={[0:1], [0:1]} | slice | bytes 8 | tf_op jit(solution)/shard_map/slice | solution.py:57
  15.0 3.5 %collective-permute-start.2 = (bf16[2,256,128]{2,1,0:T(8,128)(2,1)S(1)}, bf16[2,256,128]{2,1,0:T(8,128)(2,1)S(1)}, u32[]{:S(2)}, u32[]{:S(2)}) collective-permute-start(bf16[2,256,128]{2,1,0:T(8,128)(2,1)S(1)} %maximum_add_fusion), channel_id=1, source_target_pairs={{0,2},{1,3},{2,0},{3,1},{4,6},{5,7},{6,4},{7,5},{8,10},{9,11},{10,... | collective-permute-start | bytes 393224 | tf_op jit(solution)/shard_map/ppermute | solution.py:21
  18.5 3.2 %collective-permute-done.2 = bf16[2,256,128]{2,1,0:T(8,128)(2,1)S(1)} collective-permute-done((bf16[2,256,128]{2,1,0:T(8,128)(2,1)S(1)}, bf16[2,256,128]{2,1,0:T(8,128)(2,1)S(1)}, u32[]{:S(2)}, u32[]{:S(2)}) %collective-permute-start.2) | collective-permute-done | bytes 131104 | tf_op jit(solution)/shard_map/ppermute | solution.py:21
  24.7 1.4 %collective-permute-done.4 = bf16[2,2,256,128]{3,2,0,1:T(8,128)(2,1)S(1)} collective-permute-done((bf16[2,2,256,128]{3,2,0,1:T(8,128)(2,1)S(1)}, bf16[2,2,256,128]{3,2,0,1:T(8,128)(2,1)S(1)}, u32[]{:S(2)}, u32[]{:S(2)}) %collective-permute-start.4) | collective-permute-done | bytes 262176 | tf_op jit(solution)/shard_map/ppermute | solution.py:21
  26.3 1.8 %collective-permute-start.5 = (bf16[2,256,128]{2,1,0:T(8,128)(2,1)S(1)}, bf16[2,256,128]{2,1,0:T(8,128)(2,1)S(1)}, u32[]{:S(2)}, u32[]{:S(2)}) collective-permute-start(bf16[2,256,128]{2,1,0:T(8,128)(2,1)S(1)} %fusion.12), channel_id=1, source_target_pairs={{0,2},{1,3},{2,0},{3,1},{4,6},{5,7},{6,4},{7,5},{8,10},{9,11},{10,... | collective-permute-start | bytes 393224 | tf_op jit(solution)/shard_map/ppermute | solution.py:21
  28.1 3.8 %collective-permute-done.5 = bf16[2,256,128]{2,1,0:T(8,128)(2,1)S(1)} collective-permute-done((bf16[2,256,128]{2,1,0:T(8,128)(2,1)S(1)}, bf16[2,256,128]{2,1,0:T(8,128)(2,1)S(1)}, u32[]{:S(2)}, u32[]{:S(2)}) %collective-permute-start.5) | collective-permute-done | bytes 131104 | tf_op jit(solution)/shard_map/ppermute | solution.py:21
  31.9 1.3 %collective-permute-start.6 = (bf16[256,128]{1,0:T(8,128)(2,1)S(1)}, bf16[256,128]{1,0:T(8,128)(2,1)S(1)}, u32[]{:S(2)}, u32[]{:S(2)}) collective-permute-start(bf16[256,128]{1,0:T(8,128)(2,1)S(1)} %fusion.19), channel_id=1, source_target_pairs={{0,4},{1,5},{2,6},{3,7},{4,0},{5,1},{6,2},{7,3},{8,12},{9,13},{10,... | collective-permute-start | bytes 196616 | tf_op jit(solution)/shard_map/ppermute | solution.py:21
  33.2 4.2 %collective-permute-done.6 = bf16[256,128]{1,0:T(8,128)(2,1)S(1)} collective-permute-done((bf16[256,128]{1,0:T(8,128)(2,1)S(1)}, bf16[256,128]{1,0:T(8,128)(2,1)S(1)}, u32[]{:S(2)}, u32[]{:S(2)}) %collective-permute-start.6) | collective-permute-done | bytes 65568 | tf_op jit(solution)/shard_map/ppermute | solution.py:21
  39.5 1.6 %collective-permute-start.10 = (f32[128,256]{1,0:T(8,128)S(1)}, f32[128,256]{1,0:T(8,128)S(1)}, u32[]{:S(2)}, u32[]{:S(2)}) collective-permute-start(f32[128,256]{1,0:T(8,128)S(1)} %fusion.37), channel_id=1, source_target_pairs={{0,8},{8,0},{16,24},{24,16},{1,9},{9,1},{17,25},{25,17},{2,10},{10... | collective-permute-start | bytes 393224 | tf_op jit(solution)/shard_map/ppermute | solution.py:21
  41.1 2.2 %collective-permute-done.7 = bf16[256,128]{1,0:T(8,128)(2,1)S(1)} collective-permute-done((bf16[256,128]{1,0:T(8,128)(2,1)S(1)}, bf16[256,128]{1,0:T(8,128)(2,1)S(1)}, u32[]{:S(2)}, u32[]{:S(2)}) %collective-permute-start.7) | collective-permute-done | bytes 65568 | tf_op jit(solution)/shard_map/ppermute | solution.py:21
  43.3 1.9 %collective-permute-start.8 = (bf16[2,256,128]{2,1,0:T(8,128)(2,1)S(1)}, bf16[2,256,128]{2,1,0:T(8,128)(2,1)S(1)}, u32[]{:S(2)}, u32[]{:S(2)}) collective-permute-start(bf16[2,256,128]{2,1,0:T(8,128)(2,1)S(1)} %pad_maximum_fusion.6), channel_id=1, source_target_pairs={{0,2},{1,3},{2,0},{3,1},{4,6},{5,7},{6,4},{7,5},{8,10},{9,11},{10,... | collective-permute-start | bytes 393224 | tf_op jit(solution)/shard_map/ppermute | solution.py:21
  45.3 1.3 %collective-permute-start.12 = (f32[128,256]{1,0:T(8,128)S(1)}, f32[128,256]{1,0:T(8,128)}, u32[]{:S(2)}, u32[]{:S(2)}) collective-permute-start(f32[128,256]{1,0:T(8,128)S(1)} %copy-done.8), channel_id=1, source_target_pairs={{1,0},{2,1},{3,2},{4,3},{5,4},{6,5},{7,6},{9,8},{10,9},{11,10},{12... | collective-permute-start | bytes 393224 | tf_op jit(solution)/shard_map/ppermute | solution.py:16
  47.3 1.5 %collective-permute-start.11 = (f32[128,256]{1,0:T(8,128)}, f32[128,256]{1,0:T(8,128)}, u32[]{:S(2)}, u32[]{:S(2)}) collective-permute-start(f32[128,256]{1,0:T(8,128)} %add.73), channel_id=1, source_target_pairs={{0,16},{8,24},{16,0},{24,8},{1,17},{9,25},{17,1},{25,9},{2,18},{10... | collective-permute-start | bytes 393224 | tf_op jit(solution)/shard_map/ppermute | solution.py:21
  50.4 2.2 %shard_map.86 = f32[128,256]{1,0:T(8,128)} custom-call(s32[25]{0:T(128)} %scalars_ref.3, f32[25,128]{1,0:T(8,128)} %weights_ref.7, f32[128,256]{1,0:T(8,128)} %shard_map.85.errors_ref, f32[128,256]{1,0:T(8,128)} %collective-permute-done.12.after_ref), custom_call_target="tpu_custom_call" | custom-call | flops 1638400 | bytes 406016 | tf_op jit(solution)/shard_map/pallas_call | solution.py:105
  52.6 1.2 %collective-permute-done.11 = f32[128,256]{1,0:T(8,128)} collective-permute-done((f32[128,256]{1,0:T(8,128)}, f32[128,256]{1,0:T(8,128)}, u32[]{:S(2)}, u32[]{:S(2)}) %collective-permute-start.11) | collective-permute-done | bytes 131104 | tf_op jit(solution)/shard_map/ppermute | solution.py:21
  58.0 1.4 %collective-permute-done.13 = bf16[2,2,256,128]{3,2,0,1:T(8,128)(2,1)S(1)} collective-permute-done((bf16[2,2,256,128]{3,2,0,1:T(8,128)(2,1)S(1)}, bf16[2,2,256,128]{3,2,0,1:T(8,128)(2,1)S(1)}, u32[]{:S(2)}, u32[]{:S(2)}) %collective-permute-start.13) | collective-permute-done | bytes 262176 | tf_op jit(solution)/shard_map/ppermute | solution.py:21
  60.1 2.5 %collective-permute-start.18 = (f32[128,256]{1,0:T(8,128)S(1)}, f32[128,256]{1,0:T(8,128)}, u32[]{:S(2)}, u32[]{:S(2)}) collective-permute-start(f32[128,256]{1,0:T(8,128)S(1)} %multiply_subtract_fusion.1.times_ref), channel_id=1, source_target_pairs={{0,1},{1,2},{2,3},{3,4},{4,5},{5,6},{6,7},{8,9},{9,10},{10,11},{11... | collective-permute-start | bytes 393224 | tf_op jit(solution)/shard_map/ppermute | solution.py:16
  62.6 2.6 %collective-permute-done.14 = bf16[2,256,128]{2,1,0:T(8,128)(2,1)S(1)} collective-permute-done((bf16[2,256,128]{2,1,0:T(8,128)(2,1)S(1)}, bf16[2,256,128]{2,1,0:T(8,128)(2,1)S(1)}, u32[]{:S(2)}, u32[]{:S(2)}) %collective-permute-start.14) | collective-permute-done | bytes 131104 | tf_op jit(solution)/shard_map/ppermute | solution.py:21
  65.9 1.6 %collective-permute-start.15 = (bf16[256,128]{1,0:T(8,128)(2,1)}, bf16[256,128]{1,0:T(8,128)(2,1)}, u32[]{:S(2)}, u32[]{:S(2)}) collective-permute-start(bf16[256,128]{1,0:T(8,128)(2,1)} %fusion.20), channel_id=1, source_target_pairs={{0,4},{1,5},{2,6},{3,7},{4,0},{5,1},{6,2},{7,3},{8,12},{9,13},{10,... | collective-permute-start | bytes 196616 | tf_op jit(solution)/shard_map/ppermute | solution.py:21
  67.5 2.2 %shard_map.87.errors_ref = f32[128,256]{1,0:T(8,128)} custom-call(s32[26]{0:T(128)} %pad_add_fusion.scalars_ref, f32[25,128]{1,0:T(8,128)} %weights_ref.7, f32[128,256]{1,0:T(8,128)} %collective-permute-done.18.before_ref, f32[128,256]{1,0:T(8,128)} %copy-done.3), custom_call_target="tpu_custom_call" | custom-call | flops 1638400 | bytes 406016 | tf_op jit(solution)/shard_map/pallas_call | solution.py:105
  69.7 1.3 %slice.69 = f32[1,1]{1,0:T(1,128)} slice(f32[128,256]{1,0:T(8,128)} %shard_map.87.errors_ref), slice={[0:1], [0:1]} | slice | bytes 8 | tf_op jit(solution)/shard_map/slice | solution.py:57
  72.0 1.5 %fusion.31 = (bf16[256,128]{1,0:T(8,128)(2,1)S(1)}, f32[256,128]{1,0:T(8,128)}) fusion(f32[256,128]{1,0:T(8,128)S(1)} %copy-done.10, bf16[256,128]{1,0:T(8,128)(2,1)} %collective-permute-done.15, f32[2,256,128]{2,1,0:T(8,128)S(1)} %bitcast_add_fusion.2, pred[]{:T(512)S(6)} %ne.63), kind=kLoop, calls=%fused_computation.84 | loop fusion | flops 196608 | bytes 655361 | tf_op jit(solution)/shard_map/convert_element_type | solution.py:125
  74.5 1.7 %fusion.38 = f32[128,256]{1,0:T(8,128)S(1)} fusion(bf16[2048,128]{1,0:T(8,128)(2,1)} %bitcast.94, bf16[2048,256]{1,0:T(8,128)(2,1)} %copy-done.1), kind=kOutput, calls=%fused_computation.89 | convolution fusion | flops 134217728 | bytes 1703936 | tf_op jit(solution)/shard_map/dot_general | solution.py:158
  76.3 1.6 %collective-permute-start.16 = (f32[128,256]{1,0:T(8,128)S(1)}, f32[128,256]{1,0:T(8,128)S(1)}, u32[]{:S(2)}, u32[]{:S(2)}) collective-permute-start(f32[128,256]{1,0:T(8,128)S(1)} %fusion.38), channel_id=1, source_target_pairs={{0,8},{8,0},{16,24},{24,16},{1,9},{9,1},{17,25},{25,17},{2,10},{10... | collective-permute-start | bytes 393224 | tf_op jit(solution)/shard_map/ppermute | solution.py:21
  77.8 1.2 %collective-permute-done.20 = bf16[256,128]{1,0:T(8,128)(2,1)S(1)} collective-permute-done((bf16[256,128]{1,0:T(8,128)(2,1)S(1)}, bf16[256,128]{1,0:T(8,128)(2,1)S(1)}, u32[]{:S(2)}, u32[]{:S(2)}) %collective-permute-start.20) | collective-permute-done | bytes 65568 | tf_op jit(solution)/shard_map/ppermute | solution.py:21
  79.2 1.3 %collective-permute-start.19 = (f32[128,256]{1,0:T(8,128)S(1)}, f32[128,256]{1,0:T(8,128)}, u32[]{:S(2)}, u32[]{:S(2)}) collective-permute-start(f32[128,256]{1,0:T(8,128)S(1)} %copy-done.9), channel_id=1, source_target_pairs={{1,0},{2,1},{3,2},{4,3},{5,4},{6,5},{7,6},{9,8},{10,9},{11,10},{12... | collective-permute-start | bytes 393224 | tf_op jit(solution)/shard_map/ppermute | solution.py:16
  82.0 1.5 %collective-permute-start.17 = (f32[128,256]{1,0:T(8,128)}, f32[128,256]{1,0:T(8,128)}, u32[]{:S(2)}, u32[]{:S(2)}) collective-permute-start(f32[128,256]{1,0:T(8,128)} %add.78), channel_id=1, source_target_pairs={{0,16},{8,24},{16,0},{24,8},{1,17},{9,25},{17,1},{25,9},{2,18},{10... | collective-permute-start | bytes 393224 | tf_op jit(solution)/shard_map/ppermute | solution.py:21
  84.9 2.2 %shard_map.88 = f32[128,256]{1,0:T(8,128)} custom-call(s32[25]{0:T(128)} %scalars_ref.3, f32[25,128]{1,0:T(8,128)} %weights_ref.7, f32[128,256]{1,0:T(8,128)} %shard_map.87.errors_ref, f32[128,256]{1,0:T(8,128)} %collective-permute-done.19.after_ref), custom_call_target="tpu_custom_call" | custom-call | flops 1638400 | bytes 406016 | tf_op jit(solution)/shard_map/pallas_call | solution.py:105
  90.2 1.4 %fusion.9 = bf16[2048,256]{1,0:T(8,128)(2,1)} fusion(f32[2048,256]{1,0:T(8,128)S(1)} %fusion.3, bf16[2048,256]{1,0:T(8,128)(2,1)S(1)} %copy-done, bf16[2048,128]{1,0:T(8,128)(2,1)S(1)} %bitcast.99, f32[128,256]{1,0:T(8,128)S(1)} %multiply_subtract_fusion), kind=kOutput, calls=%fused_computation.13 | convolution fusion | flops 136347648 | bytes 4849664 | tf_op jit(solution)/shard_map/dot_general | solution.py:140
  (96 shorter events, 25.0 us)
Async XLA Ops:
  0.6 21.2 %copy-start.11 = (s32[2048,32]{0,1:T(8,128)S(1)}, s32[2048,32]{0,1:T(8,128)}, u32[]{:S(2)}) copy-start(s32[2048,32]{0,1:T(8,128)} %param.7) | copy-start | bytes 786436
  1.6 7.7 %collective-permute-start = (bf16[256,128]{1,0:T(8,128)(2,1)S(1)}, bf16[256,128]{1,0:T(8,128)(2,1)S(1)}, u32[]{:S(2)}, u32[]{:S(2)}) collective-permute-start(bf16[256,128]{1,0:T(8,128)(2,1)S(1)} %convert_element_type.110), channel_id=1, source_target_pairs={{0,4},{1,5},{2,6},{3,7},{4,0},{5,1},{6,2},{7,3},{8,12},{9,13},{10,... | collective-permute-start | bytes 196616 | tf_op jit(solution)/shard_map/ppermute | solution.py:21
  5.6 4.6 %collective-permute-start.1 = (f32[128,256]{1,0:T(8,128)}, f32[128,256]{1,0:T(8,128)S(1)}, u32[]{:S(2)}, u32[]{:S(2)}) collective-permute-start(f32[128,256]{1,0:T(8,128)} %times_ref.1), channel_id=1, source_target_pairs={{0,1},{1,2},{2,3},{3,4},{4,5},{5,6},{6,7},{8,9},{9,10},{10,11},{11... | collective-permute-start | bytes 393224 | tf_op jit(solution)/shard_map/ppermute | solution.py:16
  15.0 6.8 %collective-permute-start.2 = (bf16[2,256,128]{2,1,0:T(8,128)(2,1)S(1)}, bf16[2,256,128]{2,1,0:T(8,128)(2,1)S(1)}, u32[]{:S(2)}, u32[]{:S(2)}) collective-permute-start(bf16[2,256,128]{2,1,0:T(8,128)(2,1)S(1)} %maximum_add_fusion), channel_id=1, source_target_pairs={{0,2},{1,3},{2,0},{3,1},{4,6},{5,7},{6,4},{7,5},{8,10},{9,11},{10,... | collective-permute-start | bytes 393224 | tf_op jit(solution)/shard_map/ppermute | solution.py:21
  21.8 1.6 %collective-permute-start.3 = (bf16[2,2,256,128]{3,2,1,0:T(8,128)(2,1)S(1)}, bf16[2,2,256,128]{3,2,1,0:T(8,128)(2,1)S(1)}, u32[]{:S(2)}, u32[]{:S(2)}) collective-permute-start(bf16[2,2,256,128]{3,2,1,0:T(8,128)(2,1)S(1)} %pad_maximum_fusion.3), channel_id=1, source_target_pairs={{0,1},{1,0},{2,3},{3,2},{4,5},{5,4},{6,7},{7,6},{8,9},{9,8},{10,11... | collective-permute-start | bytes 786440 | tf_op jit(solution)/shard_map/ppermute | solution.py:21
  21.9 1.6 %copy-start = (bf16[2048,256]{1,0:T(8,128)(2,1)S(1)}, bf16[2048,256]{1,0:T(8,128)(2,1)}, u32[]{:S(2)}) copy-start(bf16[2048,256]{1,0:T(8,128)(2,1)} %param.6) | copy-start | bytes 3145732
  24.5 12.9 %copy-start.6 = (f32[256,128]{1,0:T(8,128)S(1)}, f32[256,128]{1,0:T(8,128)}, u32[]{:S(2)}) copy-start(f32[256,128]{1,0:T(8,128)} %param.8) | copy-start | bytes 393220
  24.5 1.6 %collective-permute-start.4 = (bf16[2,2,256,128]{3,2,0,1:T(8,128)(2,1)S(1)}, bf16[2,2,256,128]{3,2,0,1:T(8,128)(2,1)S(1)}, u32[]{:S(2)}, u32[]{:S(2)}) collective-permute-start(bf16[2,2,256,128]{3,2,0,1:T(8,128)(2,1)S(1)} %fusion.10), channel_id=1, source_target_pairs={{0,1},{1,0},{2,3},{3,2},{4,5},{5,4},{6,7},{7,6},{8,9},{9,8},{10,11... | collective-permute-start | bytes 786440 | tf_op jit(solution)/shard_map/ppermute | solution.py:21
  26.2 19.0 %copy-start.8 = (f32[128,256]{1,0:T(8,128)S(1)}, f32[128,256]{1,0:T(8,128)}, u32[]{:S(2)}) copy-start(f32[128,256]{1,0:T(8,128)} %shard_map.85.errors_ref) | copy-start | bytes 393220
  26.3 5.6 %collective-permute-start.5 = (bf16[2,256,128]{2,1,0:T(8,128)(2,1)S(1)}, bf16[2,256,128]{2,1,0:T(8,128)(2,1)S(1)}, u32[]{:S(2)}, u32[]{:S(2)}) collective-permute-start(bf16[2,256,128]{2,1,0:T(8,128)(2,1)S(1)} %fusion.12), channel_id=1, source_target_pairs={{0,2},{1,3},{2,0},{3,1},{4,6},{5,7},{6,4},{7,5},{8,10},{9,11},{10,... | collective-permute-start | bytes 393224 | tf_op jit(solution)/shard_map/ppermute | solution.py:21
  31.9 5.5 %collective-permute-start.6 = (bf16[256,128]{1,0:T(8,128)(2,1)S(1)}, bf16[256,128]{1,0:T(8,128)(2,1)S(1)}, u32[]{:S(2)}, u32[]{:S(2)}) collective-permute-start(bf16[256,128]{1,0:T(8,128)(2,1)S(1)} %fusion.19), channel_id=1, source_target_pairs={{0,4},{1,5},{2,6},{3,7},{4,0},{5,1},{6,2},{7,3},{8,12},{9,13},{10,... | collective-permute-start | bytes 196616 | tf_op jit(solution)/shard_map/ppermute | solution.py:21
  38.1 5.2 %collective-permute-start.7 = (bf16[256,128]{1,0:T(8,128)(2,1)S(1)}, bf16[256,128]{1,0:T(8,128)(2,1)S(1)}, u32[]{:S(2)}, u32[]{:S(2)}) collective-permute-start(bf16[256,128]{1,0:T(8,128)(2,1)S(1)} %get-tuple-element.5), channel_id=1, source_target_pairs={{0,4},{1,5},{2,6},{3,7},{4,0},{5,1},{6,2},{7,3},{8,12},{9,13},{10,... | collective-permute-start | bytes 196616 | tf_op jit(solution)/shard_map/ppermute | solution.py:21
  39.5 7.1 %collective-permute-start.10 = (f32[128,256]{1,0:T(8,128)S(1)}, f32[128,256]{1,0:T(8,128)S(1)}, u32[]{:S(2)}, u32[]{:S(2)}) collective-permute-start(f32[128,256]{1,0:T(8,128)S(1)} %fusion.37), channel_id=1, source_target_pairs={{0,8},{8,0},{16,24},{24,16},{1,9},{9,1},{17,25},{25,17},{2,10},{10... | collective-permute-start | bytes 393224 | tf_op jit(solution)/shard_map/ppermute | solution.py:21
  43.3 5.4 %collective-permute-start.8 = (bf16[2,256,128]{2,1,0:T(8,128)(2,1)S(1)}, bf16[2,256,128]{2,1,0:T(8,128)(2,1)S(1)}, u32[]{:S(2)}, u32[]{:S(2)}) collective-permute-start(bf16[2,256,128]{2,1,0:T(8,128)(2,1)S(1)} %pad_maximum_fusion.6), channel_id=1, source_target_pairs={{0,2},{1,3},{2,0},{3,1},{4,6},{5,7},{6,4},{7,5},{8,10},{9,11},{10,... | collective-permute-start | bytes 393224 | tf_op jit(solution)/shard_map/ppermute | solution.py:21
  45.3 5.1 %collective-permute-start.12 = (f32[128,256]{1,0:T(8,128)S(1)}, f32[128,256]{1,0:T(8,128)}, u32[]{:S(2)}, u32[]{:S(2)}) collective-permute-start(f32[128,256]{1,0:T(8,128)S(1)} %copy-done.8), channel_id=1, source_target_pairs={{1,0},{2,1},{3,2},{4,3},{5,4},{6,5},{7,6},{9,8},{10,9},{11,10},{12... | collective-permute-start | bytes 393224 | tf_op jit(solution)/shard_map/ppermute | solution.py:16
  47.3 6.5 %collective-permute-start.11 = (f32[128,256]{1,0:T(8,128)}, f32[128,256]{1,0:T(8,128)}, u32[]{:S(2)}, u32[]{:S(2)}) collective-permute-start(f32[128,256]{1,0:T(8,128)} %add.73), channel_id=1, source_target_pairs={{0,16},{8,24},{16,0},{24,8},{1,17},{9,25},{17,1},{25,9},{2,18},{10... | collective-permute-start | bytes 393224 | tf_op jit(solution)/shard_map/ppermute | solution.py:21
  49.5 5.4 %collective-permute-start.9 = (bf16[2,2,256,128]{3,2,0,1:T(8,128)(2,1)}, bf16[2,2,256,128]{3,2,0,1:T(8,128)(2,1)}, u32[]{:S(2)}, u32[]{:S(2)}) collective-permute-start(bf16[2,2,256,128]{3,2,0,1:T(8,128)(2,1)} %pad_maximum_fusion.4), channel_id=1, source_target_pairs={{0,1},{1,0},{2,3},{3,2},{4,5},{5,4},{6,7},{7,6},{8,9},{9,8},{10,11... | collective-permute-start | bytes 786440 | tf_op jit(solution)/shard_map/ppermute | solution.py:21
  54.9 5.2 %copy-start.3 = (f32[128,256]{1,0:T(8,128)}, f32[128,256]{1,0:T(8,128)S(1)}, u32[]{:S(2)}) copy-start(f32[128,256]{1,0:T(8,128)S(1)} %multiply_subtract_fusion.1.times_ref) | copy-start | bytes 393220
  57.9 14.2 %copy-start.10 = (f32[256,128]{1,0:T(8,128)S(1)}, f32[256,128]{1,0:T(8,128)}, u32[]{:S(2)}) copy-start(f32[256,128]{1,0:T(8,128)} %get-tuple-element.6) | copy-start | bytes 393220
  57.9 1.6 %collective-permute-start.13 = (bf16[2,2,256,128]{3,2,0,1:T(8,128)(2,1)S(1)}, bf16[2,2,256,128]{3,2,0,1:T(8,128)(2,1)S(1)}, u32[]{:S(2)}, u32[]{:S(2)}) collective-permute-start(bf16[2,2,256,128]{3,2,0,1:T(8,128)(2,1)S(1)} %fusion.11), channel_id=1, source_target_pairs={{0,1},{1,0},{2,3},{3,2},{4,5},{5,4},{6,7},{7,6},{8,9},{9,8},{10,11... | collective-permute-start | bytes 786440 | tf_op jit(solution)/shard_map/ppermute | solution.py:21
  59.6 5.6 %collective-permute-start.14 = (bf16[2,256,128]{2,1,0:T(8,128)(2,1)S(1)}, bf16[2,256,128]{2,1,0:T(8,128)(2,1)S(1)}, u32[]{:S(2)}, u32[]{:S(2)}) collective-permute-start(bf16[2,256,128]{2,1,0:T(8,128)(2,1)S(1)} %fusion.13), channel_id=1, source_target_pairs={{0,2},{1,3},{2,0},{3,1},{4,6},{5,7},{6,4},{7,5},{8,10},{9,11},{10,... | collective-permute-start | bytes 393224 | tf_op jit(solution)/shard_map/ppermute | solution.py:21
  60.1 7.4 %collective-permute-start.18 = (f32[128,256]{1,0:T(8,128)S(1)}, f32[128,256]{1,0:T(8,128)}, u32[]{:S(2)}, u32[]{:S(2)}) collective-permute-start(f32[128,256]{1,0:T(8,128)S(1)} %multiply_subtract_fusion.1.times_ref), channel_id=1, source_target_pairs={{0,1},{1,2},{2,3},{3,4},{4,5},{5,6},{6,7},{8,9},{9,10},{10,11},{11... | collective-permute-start | bytes 393224 | tf_op jit(solution)/shard_map/ppermute | solution.py:16
  65.9 6.2 %collective-permute-start.15 = (bf16[256,128]{1,0:T(8,128)(2,1)}, bf16[256,128]{1,0:T(8,128)(2,1)}, u32[]{:S(2)}, u32[]{:S(2)}) collective-permute-start(bf16[256,128]{1,0:T(8,128)(2,1)} %fusion.20), channel_id=1, source_target_pairs={{0,4},{1,5},{2,6},{3,7},{4,0},{5,1},{6,2},{7,3},{8,12},{9,13},{10,... | collective-permute-start | bytes 196616 | tf_op jit(solution)/shard_map/ppermute | solution.py:21
  69.7 9.4 %copy-start.9 = (f32[128,256]{1,0:T(8,128)S(1)}, f32[128,256]{1,0:T(8,128)}, u32[]{:S(2)}) copy-start(f32[128,256]{1,0:T(8,128)} %shard_map.87.errors_ref) | copy-start | bytes 393220
  73.5 14.5 %copy-start.4 = (f32[128,256]{1,0:T(8,128)S(1)}, f32[128,256]{1,0:T(8,128)}, u32[]{:S(2)}) copy-start(f32[128,256]{1,0:T(8,128)} %copy-done.3) | copy-start | bytes 393220
  73.5 5.5 %collective-permute-start.20 = (bf16[256,128]{1,0:T(8,128)(2,1)S(1)}, bf16[256,128]{1,0:T(8,128)(2,1)S(1)}, u32[]{:S(2)}, u32[]{:S(2)}) collective-permute-start(bf16[256,128]{1,0:T(8,128)(2,1)S(1)} %get-tuple-element.3), channel_id=1, source_target_pairs={{0,4},{1,5},{2,6},{3,7},{4,0},{5,1},{6,2},{7,3},{8,12},{9,13},{10,... | collective-permute-start | bytes 196616 | tf_op jit(solution)/shard_map/ppermute | solution.py:21
  76.3 5.0 %collective-permute-start.16 = (f32[128,256]{1,0:T(8,128)S(1)}, f32[128,256]{1,0:T(8,128)S(1)}, u32[]{:S(2)}, u32[]{:S(2)}) collective-permute-start(f32[128,256]{1,0:T(8,128)S(1)} %fusion.38), channel_id=1, source_target_pairs={{0,8},{8,0},{16,24},{24,16},{1,9},{9,1},{17,25},{25,17},{2,10},{10... | collective-permute-start | bytes 393224 | tf_op jit(solution)/shard_map/ppermute | solution.py:21
  79.1 5.0 %collective-permute-start.21 = (bf16[2,256,128]{2,1,0:T(8,128)(2,1)S(1)}, bf16[2,256,128]{2,1,0:T(8,128)(2,1)S(1)}, u32[]{:S(2)}, u32[]{:S(2)}) collective-permute-start(bf16[2,256,128]{2,1,0:T(8,128)(2,1)S(1)} %maximum_add_fusion.1), channel_id=1, source_target_pairs={{0,2},{1,3},{2,0},{3,1},{4,6},{5,7},{6,4},{7,5},{8,10},{9,11},{10,... | collective-permute-start | bytes 393224 | tf_op jit(solution)/shard_map/ppermute | solution.py:21
  79.2 5.7 %collective-permute-start.19 = (f32[128,256]{1,0:T(8,128)S(1)}, f32[128,256]{1,0:T(8,128)}, u32[]{:S(2)}, u32[]{:S(2)}) collective-permute-start(f32[128,256]{1,0:T(8,128)S(1)} %copy-done.9), channel_id=1, source_target_pairs={{1,0},{2,1},{3,2},{4,3},{5,4},{6,5},{7,6},{9,8},{10,9},{11,10},{12... | collective-permute-start | bytes 393224 | tf_op jit(solution)/shard_map/ppermute | solution.py:16
  82.0 6.1 %collective-permute-start.17 = (f32[128,256]{1,0:T(8,128)}, f32[128,256]{1,0:T(8,128)}, u32[]{:S(2)}, u32[]{:S(2)}) collective-permute-start(f32[128,256]{1,0:T(8,128)} %add.78), channel_id=1, source_target_pairs={{0,16},{8,24},{16,0},{24,8},{1,17},{9,25},{17,1},{25,9},{2,18},{10... | collective-permute-start | bytes 393224 | tf_op jit(solution)/shard_map/ppermute | solution.py:21
  84.9 4.2 %collective-permute-start.22 = (bf16[2,2,256,128]{3,2,0,1:T(8,128)(2,1)}, bf16[2,2,256,128]{3,2,0,1:T(8,128)(2,1)}, u32[]{:S(2)}, u32[]{:S(2)}) collective-permute-start(bf16[2,2,256,128]{3,2,0,1:T(8,128)(2,1)} %pad_maximum_fusion.5), channel_id=1, source_target_pairs={{0,1},{1,0},{2,3},{3,2},{4,5},{5,4},{6,7},{7,6},{8,9},{9,8},{10,11... | collective-permute-start | bytes 786440 | tf_op jit(solution)/shard_map/ppermute | solution.py:21
  89.1 2.6 %copy-start.7 = (f32[128,256]{1,0:T(8,128)}, f32[128,256]{1,0:T(8,128)S(1)}, u32[]{:S(2)}) copy-start(f32[128,256]{1,0:T(8,128)S(1)} %multiply_subtract_fusion) | copy-start | bytes 393220
  (4 other events, 4.0 us)
